TPU v7x, 512 devices: a whole 4x4x16 slice. The times are simulated.
512 devices in a mesh: dp: 64 (over z, x_lo, core), slab: 8 (over y, x_hi).
Axes of the slice: x: 4 (x_hi: 2, x_lo: 2; x = x_hi * 2 + x_lo), y: 4, z: 16, core: 2. Of those that a mesh axis runs over, the one named last changes fastest.
Arguments:
- voxels: bfloat16 [64, 8, 12, 32, 128], P('dp', None, None, 'slab'), may hold values from -16 to 16
- occupancy: int32 [64, 8, 12, 32], P('dp', None, None, 'slab'), may hold values 0 or 1
- out_grad: bfloat16 [64, 8, 12, 32, 128], P('dp', None, None, 'slab'), may hold values from -192 to 192
- weights: bfloat16 [2, 3456, 128], replicated, may hold values from -5 to 5
- master: float32 [2, 3456, 128], P(None, 'dp', 'slab'), may hold values from -5 to 5
- moment: float32 [2, 3456, 128], P(None, 'dp', 'slab'), may hold values from -18 to 18
- second: float32 [2, 3456, 128], P(None, 'dp', 'slab'), may hold values from 1 to 10
- teacher: float32 [2, 3456, 128], P(None, 'dp', 'slab'), may hold values from -5 to 5
Outputs:
- new_master: float32 [2, 3456, 128], P(None, 'dp', 'slab')
- new_moment: float32 [2, 3456, 128], P(None, 'dp', 'slab')
- new_second: float32 [2, 3456, 128], P(None, 'dp', 'slab')
- new_teacher: float32 [2, 3456, 128], P(None, 'dp', 'slab')
- new_weights: bfloat16 [2, 3456, 128], P(None, None, 'slab')
All inputs are finite; a program needn't handle non-finite values. No bound on the sum of `occupancy` on one device may be relied on, other than what follows from the above.
Results may differ from a plain program's by a relative error of at most 0.0013.
Values may be sent and summed in bfloat16 or wider, within the bound.
No kernel may reach another device: no remote copies, remote signals or barrier semaphores. Data moves between devices by JAX's collectives and lax.ppermute only.
A program may use at most 64 MiB of HBM per device.

v0:
```python
import jax
import jax.numpy as jnp
from jax import lax
from jax.sharding import PartitionSpec as P

C = 128
TAPS = 27
STEP_COUNT = 10


beta_first = 0.9
beta_second = 0.999
learning_rate = 0.01
weight_decay = 0.05
teacher_keep = 0.99
adam_epsilon = 1e-08


def with_halo(cells, sides, width):
    for axis, dim in sides:
        count = lax.axis_size(axis)
        ends = count - 1
        head = lax.slice_in_dim(cells, 0, width, axis=dim)
        tail = lax.slice_in_dim(cells, cells.shape[dim] - width, cells.shape[dim], axis=dim)
        cells = jnp.concatenate(
            [
                lax.ppermute(tail, axis, [(i, (i + 1) % count) for i in range(ends)]),
                cells,
                lax.ppermute(head, axis, [((i + 1) % count, i) for i in range(ends)]),
            ],
            axis=dim,
        )
    return cells


def tap_corners():
    return [
        (along_x, along_y, along_z)
        for along_x in range(3)
        for along_y in range(3)
        for along_z in range(3)
    ]


def unit_scale():
    return (TAPS * C) ** (-0.5)


def silu_slope(values):
    logistic = jax.nn.sigmoid(values)
    return logistic * (1.0 + values * (1.0 - logistic))


def take_window(padded, start, extent):
    window = padded[
        start[0] : start[0] + extent[0],
        start[1] : start[1] + extent[1],
        start[2] : start[2] + extent[2],
    ]
    return window.reshape(-1, window.shape[-1])


def forward_conv(padded, weight_rows, extent):
    channels = weight_rows.shape[1]
    summed = jnp.zeros((extent[0] * extent[1] * extent[2], channels), jnp.float32)
    for tap_index, corner in enumerate(tap_corners()):
        window = take_window(padded, corner, extent)
        block = weight_rows[tap_index * channels : (tap_index + 1) * channels]
        summed = summed + jnp.dot(window, block, preferred_element_type=jnp.float32)
    return (summed * unit_scale()).reshape(extent + (channels,))


def transposed_conv(padded_grad, weight_rows, extent):
    channels = weight_rows.shape[1]
    summed = jnp.zeros((extent[0] * extent[1] * extent[2], channels), jnp.float32)
    for tap_index, corner in enumerate(tap_corners()):
        start = (2 - corner[0], 2 - corner[1], 2 - corner[2])
        window = take_window(padded_grad, start, extent)
        block = weight_rows[tap_index * channels : (tap_index + 1) * channels]
        summed = summed + lax.dot_general(
            window, block, (((1,), (1,)), ((), ())), preferred_element_type=jnp.float32
        )
    return (summed * unit_scale()).reshape(extent + (channels,))


def weight_grad(padded, grad_field, extent):
    grad_rows = grad_field.reshape(-1, grad_field.shape[-1])
    blocks = []
    for corner in tap_corners():
        window = take_window(padded, corner, extent)
        blocks.append(
            lax.dot_general(
                window, grad_rows, (((0,), (0,)), ((), ())), preferred_element_type=jnp.float32
            )
        )
    return jnp.concatenate(blocks, axis=0)


def adam_update(master, moment, second, teacher, gradient):
    new_moment = beta_first * moment + (1.0 - beta_first) * gradient
    new_second = beta_second * second + (1.0 - beta_second) * gradient * gradient
    first_fix = 1.0 - beta_first**STEP_COUNT
    second_fix = 1.0 - beta_second**STEP_COUNT
    ratio = new_moment / first_fix / (jnp.sqrt(new_second / second_fix) + adam_epsilon)
    new_master = master - learning_rate * (ratio + weight_decay * master)
    new_teacher = teacher_keep * teacher + (1.0 - teacher_keep) * new_master
    return (new_master, new_moment, new_second, new_teacher)


def local(voxels, occupancy, out_grad, weights, master, moment, second, teacher):
    own_cells = voxels[0]
    extent = tuple(own_cells.shape[:3])
    occupied = occupancy[0].astype(jnp.float32)[..., None]
    plane_pad = ((1, 1), (1, 1), (0, 0), (0, 0))
    rim_input = with_halo(own_cells, ((COLUMN_AXES, 2),), 1)
    padded_in = jnp.pad(rim_input, plane_pad)
    pre_one = forward_conv(padded_in, weights[0], extent)
    act_one = (occupied * jax.nn.silu(pre_one)).astype(jnp.bfloat16)
    rim_hidden = with_halo(act_one, ((COLUMN_AXES, 2),), 1)
    padded_act = jnp.pad(rim_hidden, plane_pad)
    pre_two = forward_conv(padded_act, weights[1], extent)
    grad_two = (out_grad[0].astype(jnp.float32) * occupied * silu_slope(pre_two)).astype(
        jnp.bfloat16
    )
    rim_grad = with_halo(grad_two, ((COLUMN_AXES, 2),), 1)
    padded_grad = jnp.pad(rim_grad, plane_pad)
    wgrad_two = weight_grad(padded_act, grad_two, extent)
    back_one = transposed_conv(padded_grad, weights[1], extent)
    grad_one = (back_one * occupied * silu_slope(pre_one)).astype(jnp.bfloat16)
    wgrad_one = weight_grad(padded_in, grad_one, extent)
    weight_grads = jnp.stack([wgrad_one, wgrad_two])
    gradient = scatter_rows_and_columns(weight_grads, master.shape)
    new_master, new_moment, new_second, new_teacher = adam_update(
        master, moment, second, teacher, gradient
    )
    fresh_weights = new_master.astype(jnp.bfloat16)
    new_weights = gather_rows(fresh_weights)
    return (new_master, new_moment, new_second, new_teacher, new_weights)


ROW_AXES = ("z", "x_lo", "core")
COLUMN_AXES = ("y", "x_hi")


def exchange_and_sum(blocks, axes):
    moved = lax.all_to_all(blocks, axes, 0, 0, tiled=True)
    return moved.sum(axis=0)


def scatter_rows_and_columns(weight_grads, own_shape):
    layers, rows, cols = own_shape
    lanes = weight_grads.shape[-1]
    z, x_lo, core = (lax.axis_size(name) for name in ROW_AXES)
    y, x_hi = (lax.axis_size(name) for name in COLUMN_AXES)
    blocks = weight_grads.reshape(layers, z, x_lo, core, rows, y, x_hi, cols)
    blocks = blocks.transpose(3, 5, 6, 2, 1, 0, 4, 7)
    blocks = exchange_and_sum(blocks.reshape(core, -1, lanes), "core")
    blocks = exchange_and_sum(blocks.reshape(y, -1, lanes), "y")
    blocks = exchange_and_sum(blocks.reshape(x_hi * x_lo, -1, lanes), ("x_hi", "x_lo"))
    blocks = exchange_and_sum(blocks.reshape(z, -1), "z")
    return blocks.reshape(own_shape) * unit_scale()


def gather_rows(fresh_weights):
    layers, rows, cols = fresh_weights.shape
    gathered = lax.all_gather(fresh_weights, "z", axis=0)
    gathered = lax.all_gather(gathered, ("x_lo", "core"), axis=0)
    gathered = gathered.reshape((-1,) + gathered.shape[1:])
    x_lo, core = lax.axis_size("x_lo"), lax.axis_size("core")
    gathered = gathered.reshape((x_lo, core) + gathered.shape[1:])
    gathered = gathered.transpose(3, 2, 0, 1, 4, 5)
    return gathered.reshape(layers, -1, cols)


def solution(mesh):
    rows_over, columns_over = mesh.shape["dp"], mesh.shape["slab"]
    fine = jax.sharding.Mesh(
        mesh.devices.reshape(rows_over // 4, 2, 2, columns_over // 2, 2), ROW_AXES + COLUMN_AXES
    )
    dp, slab = ROW_AXES, COLUMN_AXES
    in_specs = (
        P(dp, None, None, slab, None),
        P(dp, None, None, slab),
        P(dp, None, None, slab, None),
        P(),
        P(None, dp, slab),
        P(None, dp, slab),
        P(None, dp, slab),
        P(None, dp, slab),
    )
    out_specs = (
        P(None, dp, slab),
        P(None, dp, slab),
        P(None, dp, slab),
        P(None, dp, slab),
        P(None, None, slab),
    )
    return jax.shard_map(local, mesh=fine, in_specs=in_specs, out_specs=out_specs, check_vma=False)
```

profile of v0, /device:TPU:1, one launch (start us, length us, event | category | flops | bytes accessed | tf_op | source)
XLA Modules:
  0.0 295.4 jit_solution(17363981600307724744)
XLA Ops:
  0.6 0.9 copy.878
  1.6 5.5 %collective-permute-start = (bf16[8,12,1,128]{3,1,2,0:T(8,128)(2,1)S(1)}, bf16[8,12,1,128]{3,1,2,0:T(8,128)(2,1)S(1)}, u32[]{:S(2)}, u32[]{:S(2)}) collective-permute-start(bf16[8,12,1,128]{3,1,2,0:T(8,128)(2,1)S(1)} %get-tuple-element.105), channel_id=1, source_target_pairs={{0,1},{1,2},{2,3},{3,4},{4,5},{5,6},{6,7},{8,9},{9,10},{10,11},{11... | collective-permute-start | bytes 73736 | tf_op jit(solution)/shard_map/ppermute | solution.py:27
  7.1 1.3 collective-permute-start.1
  8.4 0.9 copy_convert_fusion
  10.4 2.9 collective-permute-done.1
  20.7 4.0 %collective-permute-start.2 = (bf16[8,12,1,128]{3,0,2,1:T(8,128)(2,1)S(1)}, bf16[8,12,1,128]{3,0,2,1:T(8,128)(2,1)S(1)}, u32[]{:S(2)}, u32[]{:S(2)}) collective-permute-start(bf16[8,12,1,128]{3,0,2,1:T(8,128)(2,1)S(1)} %get-tuple-element.113), channel_id=1, source_target_pairs={{0,1},{1,2},{2,3},{3,4},{4,5},{5,6},{6,7},{8,9},{9,10},{10,11},{11... | collective-permute-start | bytes 73736 | tf_op jit(solution)/shard_map/ppermute | solution.py:27
  24.7 1.3 collective-permute-start.3
  26.1 4.7 %collective-permute-done.3 = bf16[8,12,1,128]{3,0,2,1:T(8,128)(2,1)S(1)} collective-permute-done((bf16[8,12,1,128]{3,0,2,1:T(8,128)(2,1)S(1)}, bf16[8,12,1,128]{3,0,2,1:T(8,128)(2,1)S(1)}, u32[]{:S(2)}, u32[]{:S(2)}) %collective-permute-start.3) | collective-permute-done | bytes 24608 | tf_op jit(solution)/shard_map/ppermute | solution.py:29
  38.2 4.6 %collective-permute-start.4 = (bf16[8,12,1,128]{3,0,2,1:T(8,128)(2,1)S(1)}, bf16[8,12,1,128]{3,0,2,1:T(8,128)(2,1)S(1)}, u32[]{:S(2)}, u32[]{:S(2)}) collective-permute-start(bf16[8,12,1,128]{3,0,2,1:T(8,128)(2,1)S(1)} %get-tuple-element.109), channel_id=1, source_target_pairs={{0,1},{1,2},{2,3},{3,4},{4,5},{5,6},{6,7},{8,9},{9,10},{10,11},{11... | collective-permute-start | bytes 73736 | tf_op jit(solution)/shard_map/ppermute | solution.py:27
  42.8 1.3 collective-permute-start.5
  44.1 0.9 fusion.29
  45.0 0.9 fusion.28
  45.9 0.9 fusion.27
  46.7 0.9 fusion.26
  48.4 0.9 fusion.24
  49.3 0.9 fusion.23
  50.1 0.9 fusion.22
  51.0 0.9 fusion.21
  51.9 0.9 fusion.20
  52.7 0.9 fusion.19
  54.4 0.9 fusion.18
  55.4 0.9 fusion.2
  58.8 0.9 fusion.14
  59.6 0.9 fusion.13
  63.9 0.9 fusion.8
  64.7 0.9 fusion.7
  66.4 2.0 copy.742
  68.4 9.3 %stack.10 = f32[1,16,2,2,54,4,2,16]{4,3,2,1,7,6,5,0:T(2,128)} reshape(f32[3456,128]{0,1:T(8,128)S(1)} %copy.742) | data formatting | bytes 3538944 | tf_op jit(solution)/shard_map/stack | solution.py:131
  85.6 0.9 fusion.55
  86.5 0.9 fusion.54
  87.3 0.9 fusion.53
  88.2 0.9 fusion.52
  89.0 0.9 fusion.51
  90.8 0.9 fusion.49
  91.6 0.9 fusion.48
  93.3 0.9 fusion.46
  94.2 0.9 fusion.45
  95.0 0.9 fusion.44
  95.9 0.9 fusion.5
  97.6 0.9 fusion.4
  98.5 0.9 fusion.42
  99.3 0.9 fusion.41
  101.9 0.9 fusion.38
  102.8 0.9 fusion.37
  103.6 0.9 fusion.36
  104.5 0.9 fusion.35
  105.3 0.9 fusion.34
  106.2 0.9 fusion.33
  107.1 0.9 fusion.32
  107.9 0.9 fusion.31
  108.8 2.0 copy.737
  110.8 9.6 %stack.9 = f32[1,16,2,2,54,4,2,16]{4,3,2,1,7,6,5,0:T(2,128)} reshape(f32[3456,128]{0,1:T(8,128)S(1)} %copy.737) | data formatting | bytes 3538944 | tf_op jit(solution)/shard_map/stack | solution.py:131
  120.3 9.1 %maximum_bitcast_fusion = f32[2,4,2,2,16,2,54,16]{6,0,3,4,7,2,1,5:T(2,128)} fusion(f32[1,16,2,2,54,4,2,16]{4,3,2,1,7,6,5,0:T(2,128)} %stack.10, f32[1,16,2,2,54,4,2,16]{4,3,2,1,7,6,5,0:T(2,128)} %stack.9), kind=kLoop, calls=%fused_computation | loop fusion | flops 884736 | bytes 7077888 | tf_op jit(solution)/shard_map/transpose | solution.py:156
  129.4 23.6 %copy.743 = f32[2,4,2,2,16,2,54,16]{7,6,5,4,3,2,1,0:T(8,128)} copy(f32[2,4,2,2,16,2,54,16]{6,0,3,4,7,2,1,5:T(2,128)} %maximum_bitcast_fusion) | data formatting | bytes 7077888 | tf_op jit(solution)/shard_map/transpose | solution.py:156
  153.1 16.3 %reshape.531 = f32[2,3456,128]{2,1,0:T(8,128)} reshape(f32[2,4,2,2,16,2,54,16]{7,6,5,4,3,2,1,0:T(8,128)} %copy.743) | data formatting | bytes 7077888 | tf_op jit(solution)/shard_map/reshape | solution.py:157
  169.4 14.4 %all_to_all.25 = f32[2,3456,128]{2,1,0:T(8,128)} all-to-all(f32[2,3456,128]{2,1,0:T(8,128)} %reshape.531), channel_id=1, replica_groups=mesh['z'=16,'x_lo'=2,'core'=2,'y'=4,'x_hi'=2] {'core'}, dimensions={0} | all-to-all | bytes 7077888 | tf_op jit(solution)/shard_map/all_to_all | solution.py:146
  183.8 2.4 reduce_sum.36
  186.2 28.1 %all_to_all.26 = f32[4,864,128]{2,1,0:T(8,128)} all-to-all(f32[4,864,128]{2,1,0:T(8,128)S(1)} %bitcast.767), channel_id=1, replica_groups=mesh['z'=16,'x_lo'=2,'core'=2,'y'=4,'x_hi'=2] {'y'}, dimensions={0} | all-to-all | bytes 3538944 | tf_op jit(solution)/shard_map/all_to_all | solution.py:146
  214.3 1.6 reduce_sum.37
  215.9 9.4 %all_to_all.27 = f32[4,216,128]{2,1,0:T(8,128)S(1)} all-to-all(f32[4,216,128]{2,1,0:T(8,128)S(1)} %bitcast.769), channel_id=1, replica_groups=mesh['z'=16,'x_lo'=2,'core'=2,'y'=4,'x_hi'=2] {'x_hi','x_lo'}, dimensions={0} | all-to-all | bytes 884736 | tf_op jit(solution)/shard_map/all_to_all | solution.py:146
  225.6 26.6 %all_to_all.28 = f32[16,1,1728]{2,1,0:T(1,128)S(1)} all-to-all(f32[16,1,1728]{2,1,0:T(1,128)S(1)} %all_to_all.20), channel_id=1, replica_groups=mesh['z'=16,'x_lo'=2,'core'=2,'y'=4,'x_hi'=2] {'z'}, dimensions={0} | all-to-all | bytes 221184 | tf_op jit(solution)/shard_map/all_to_all | solution.py:146
  253.3 21.7 %all-gather = bf16[32,54,16]{1,2,0:T(8,128)(2,1)S(1)} all-gather(bf16[2,54,16]{1,2,0:T(8,128)(2,1)S(1)} %get-tuple-element.25), channel_id=2, replica_groups=mesh['z'=16,'x_lo'=2,'core'=2,'y'=4,'x_hi'=2] {'z'}, dimensions={0}, use_global_device_ids=true | all-gather | bytes 58752 | tf_op jit(solution)/shard_map/all_gather | solution.py:166
  275.0 17.9 %all-gather.1 = bf16[64,2,54,16]{2,3,1,0:T(8,128)(2,1)S(1)} all-gather(bf16[16,2,54,16]{2,3,1,0:T(8,128)(2,1)S(1)} %bitcast.779), channel_id=3, replica_groups=mesh['z'=16,'x_lo'=2,'core'=2,'y'=4,'x_hi'=2] {'x_lo','core'}, dimensions={0}, use_global_device_ids=true | all-gather | bytes 276480 | tf_op jit(solution)/shard_map/all_gather | solution.py:167
  293.5 1.4 reshape.535
  (232 shorter events, 38.0 us)
Async XLA Ops:
  1.6 8.8 %collective-permute-start = (bf16[8,12,1,128]{3,1,2,0:T(8,128)(2,1)S(1)}, bf16[8,12,1,128]{3,1,2,0:T(8,128)(2,1)S(1)}, u32[]{:S(2)}, u32[]{:S(2)}) collective-permute-start(bf16[8,12,1,128]{3,1,2,0:T(8,128)(2,1)S(1)} %get-tuple-element.105), channel_id=1, source_target_pairs={{0,1},{1,2},{2,3},{3,4},{4,5},{5,6},{6,7},{8,9},{9,10},{10,11},{11... | collective-permute-start | bytes 73736 | tf_op jit(solution)/shard_map/ppermute | solution.py:27
  7.1 6.2 %collective-permute-start.1 = (bf16[8,12,1,128]{3,1,2,0:T(8,128)(2,1)S(1)}, bf16[8,12,1,128]{3,1,2,0:T(8,128)(2,1)S(1)}, u32[]{:S(2)}, u32[]{:S(2)}) collective-permute-start(bf16[8,12,1,128]{3,1,2,0:T(8,128)(2,1)S(1)} %get-tuple-element.106), channel_id=1, source_target_pairs={{1,0},{2,1},{3,2},{4,3},{5,4},{6,5},{7,6},{9,8},{10,9},{11,10},{12... | collective-permute-start | bytes 73736 | tf_op jit(solution)/shard_map/ppermute | solution.py:29
  14.5 1.5 copy-start
  17.0 1.2 copy-start.2
  20.7 5.4 %collective-permute-start.2 = (bf16[8,12,1,128]{3,0,2,1:T(8,128)(2,1)S(1)}, bf16[8,12,1,128]{3,0,2,1:T(8,128)(2,1)S(1)}, u32[]{:S(2)}, u32[]{:S(2)}) collective-permute-start(bf16[8,12,1,128]{3,0,2,1:T(8,128)(2,1)S(1)} %get-tuple-element.113), channel_id=1, source_target_pairs={{0,1},{1,2},{2,3},{3,4},{4,5},{5,6},{6,7},{8,9},{9,10},{10,11},{11... | collective-permute-start | bytes 73736 | tf_op jit(solution)/shard_map/ppermute | solution.py:27
  24.7 6.1 %collective-permute-start.3 = (bf16[8,12,1,128]{3,0,2,1:T(8,128)(2,1)S(1)}, bf16[8,12,1,128]{3,0,2,1:T(8,128)(2,1)S(1)}, u32[]{:S(2)}, u32[]{:S(2)}) collective-permute-start(bf16[8,12,1,128]{3,0,2,1:T(8,128)(2,1)S(1)} %get-tuple-element.114), channel_id=1, source_target_pairs={{1,0},{2,1},{3,2},{4,3},{5,4},{6,5},{7,6},{9,8},{10,9},{11,10},{12... | collective-permute-start | bytes 73736 | tf_op jit(solution)/shard_map/ppermute | solution.py:29
  36.0 1.2 copy-start.3
  38.2 39.5 %collective-permute-start.4 = (bf16[8,12,1,128]{3,0,2,1:T(8,128)(2,1)S(1)}, bf16[8,12,1,128]{3,0,2,1:T(8,128)(2,1)S(1)}, u32[]{:S(2)}, u32[]{:S(2)}) collective-permute-start(bf16[8,12,1,128]{3,0,2,1:T(8,128)(2,1)S(1)} %get-tuple-element.109), channel_id=1, source_target_pairs={{0,1},{1,2},{2,3},{3,4},{4,5},{5,6},{6,7},{8,9},{9,10},{10,11},{11... | collective-permute-start | bytes 73736 | tf_op jit(solution)/shard_map/ppermute | solution.py:27
  42.8 34.9 %collective-permute-start.5 = (bf16[8,12,1,128]{3,0,2,1:T(8,128)(2,1)S(1)}, bf16[8,12,1,128]{3,0,2,1:T(8,128)(2,1)S(1)}, u32[]{:S(2)}, u32[]{:S(2)}) collective-permute-start(bf16[8,12,1,128]{3,0,2,1:T(8,128)(2,1)S(1)} %get-tuple-element.110), channel_id=1, source_target_pairs={{1,0},{2,1},{3,2},{4,3},{5,4},{6,5},{7,6},{9,8},{10,9},{11,10},{12... | collective-permute-start | bytes 73736 | tf_op jit(solution)/shard_map/ppermute | solution.py:29
  78.0 1.5 copy-start.1
  214.3 38.3 %copy-start.5 = (f32[2,54,16]{1,2,0:T(8,128)S(1)}, f32[2,54,16]{1,2,0:T(8,128)}, u32[]{:S(2)}) copy-start(f32[2,54,16]{1,2,0:T(8,128)} %param.12) | copy-start | bytes 20740
  214.3 38.3 %copy-start.6 = (f32[2,54,16]{1,2,0:T(8,128)S(1)}, f32[2,54,16]{1,2,0:T(8,128)}, u32[]{:S(2)}) copy-start(f32[2,54,16]{1,2,0:T(8,128)} %param.13) | copy-start | bytes 20740
  214.3 38.3 %copy-start.7 = (f32[2,54,16]{1,2,0:T(8,128)S(1)}, f32[2,54,16]{1,2,0:T(8,128)}, u32[]{:S(2)}) copy-start(f32[2,54,16]{1,2,0:T(8,128)} %param.14) | copy-start | bytes 20740
  225.4 69.4 %copy-start.8 = (f32[2,54,16]{1,2,0:T(8,128)S(1)}, f32[2,54,16]{1,2,0:T(8,128)}, u32[]{:S(2)}) copy-start(f32[2,54,16]{1,2,0:T(8,128)} %param.15) | copy-start | bytes 20740
  253.3 42.2 %copy-start.4 = (f32[2,54,16]{1,2,0:T(8,128)}, f32[2,54,16]{1,2,0:T(8,128)S(1)}, u32[]{:S(2)}) copy-start(f32[2,54,16]{1,2,0:T(8,128)S(1)} %get-tuple-element.26) | copy-start | bytes 20740
where the time goes:
time: 297 us; the launch traced here: 295 us
  blocking collectives  118 us (40%)
  local copies, waits for them, and re-layouts  72.4 us (24%)
  matrix products  60.2 us (20%)
  starting transfers between devices  18 us (6%)
  other arithmetic  17.1 us (6%)
  waiting for transfers between devices  7.56 us (3%)
    all_to_all x4, blocking collectives, exchange_and_sum(): moved = lax.all_to_all(blocks, axes, 0, 0, tiled=True)  78.6 us
    dot_general x54, matrix products, weight_grad(): lax.dot_general(window, grad_rows, (((0,), (0,)), ((), ())), preferred_el...  46.3 us
    transpose x1, local copies, waits for them, and re-layouts, scatter_rows_and_columns(): blocks = blocks.transpose(3, 5, 6, 2, 1, 0, 4, 7)  23.6 us
    all_gather x1, blocking collectives, gather_rows(): gathered = lax.all_gather(fresh_weights, 'z', axis=0)  21.7 us
    another operation x2, local copies, waits for them, and re-layouts, local(): weight_grads = jnp.stack([wgrad_one, wgrad_two])  18.8 us
    all_gather x1, blocking collectives, gather_rows(): gathered = lax.all_gather(gathered, ('x_lo', 'core'), axis=0)  17.9 us
    reshape x1, local copies, waits for them, and re-layouts, scatter_rows_and_columns(): blocks = exchange_and_sum(blocks.reshape(core, -1, lanes), 'core')  16.3 us
    ppermute x3, starting transfers between devices, with_halo(): lax.ppermute(tail, axis, [(i, (i + 1) % count) for i in range(ends)])  14.2 us
  transfers between devices with their start and end apart: 6, of which 2 were waited for; matrix products, arithmetic and copies ran while one was open for 12% of the time, Pallas kernels for 0%

commit v1 on v0

--- a/solution.py
+++ b/solution.py
@@ -152,13 +152,14 @@
     lanes = weight_grads.shape[-1]
     z, x_lo, core = (lax.axis_size(name) for name in ROW_AXES)
     y, x_hi = (lax.axis_size(name) for name in COLUMN_AXES)
-    blocks = weight_grads.reshape(layers, z, x_lo, core, rows, y, x_hi, cols)
-    blocks = blocks.transpose(3, 5, 6, 2, 1, 0, 4, 7)
-    blocks = exchange_and_sum(blocks.reshape(core, -1, lanes), "core")
-    blocks = exchange_and_sum(blocks.reshape(y, -1, lanes), "y")
-    blocks = exchange_and_sum(blocks.reshape(x_hi * x_lo, -1, lanes), ("x_hi", "x_lo"))
-    blocks = exchange_and_sum(blocks.reshape(z, -1), "z")
-    return blocks.reshape(own_shape) * unit_scale()
+    blocks = weight_grads.reshape(layers, z, x_lo, core, rows, lanes)
+    blocks = blocks.transpose(3, 2, 1, 0, 4, 5)
+    blocks = exchange_and_sum(blocks, "core")
+    blocks = exchange_and_sum(blocks, "x_lo")
+    blocks = exchange_and_sum(blocks, "z")
+    blocks = blocks.reshape(layers, rows, y * x_hi, cols).transpose(2, 0, 1, 3)
+    blocks = exchange_and_sum(blocks, COLUMN_AXES)
+    return blocks * unit_scale()
 
 
 def gather_rows(fresh_weights):

time: 297 us -> 261 us (0.88)
  local copies, waits for them, and re-layouts: 72.4 us -> 17.3 us
  blocking collectives: 118 us -> 146 us
  other arithmetic: 17.1 us -> 8.51 us
    all_to_all x4, blocking collectives: 78.6 us -> 102 us  [exchange_and_sum(): moved = lax.all_to_all(blocks, axes, 0, 0, tiled=True)]
    transpose x1 -> x2, local copies, waits for them, and re-layouts: 23.6 us -> 2.06 us  [the longest x1 2.05 us: scatter_rows_and_columns(): blocks = blocks.transpose(3, 2, 1, 0, 4, 5)]
    reshape x1 -> x0, local copies, waits for them, and re-layouts: 16.3 us -> none  [scatter_rows_and_columns(): blocks = exchange_and_sum(blocks.reshape(core, -1, lanes), 'core')]
    another operation x2, local copies, waits for them, and re-layouts: 18.8 us -> 4.09 us  [local(): weight_grads = jnp.stack([wgrad_one, wgrad_two])]
    transpose x1, other arithmetic: 9.08 us -> 1.74 us  [scatter_rows_and_columns(): blocks = blocks.transpose(3, 2, 1, 0, 4, 5)]
    all_gather x1, blocking collectives: 21.7 us -> 26.1 us  [gather_rows(): gathered = lax.all_gather(fresh_weights, 'z', axis=0)]
    concatenate x2 -> x0, local copies, waits for them, and re-layouts: 3.94 us -> none  [weight_grad(): return jnp.concatenate(blocks, axis=0)]
  transfers between devices with their start and end apart: 6 -> 6, of which waited for: 2 -> 2; matrix products, arithmetic and copies ran while one was open for 12% -> 10% of each run, Pallas kernels for 0% -> 0%
where the time goes in v1:
time: 261 us; the launch traced here: 260 us
  blocking collectives  146 us (56%)
  matrix products  60.2 us (23%)
  starting transfers between devices  18.1 us (7%)
  local copies, waits for them, and re-layouts  17.3 us (7%)
  other arithmetic  8.51 us (3%)
  waiting for transfers between devices  7.57 us (3%)
    all_to_all x4, blocking collectives, exchange_and_sum(): moved = lax.all_to_all(blocks, axes, 0, 0, tiled=True)  102 us
    dot_general x54, matrix products, weight_grad(): lax.dot_general(window, grad_rows, (((0,), (0,)), ((), ())), preferred_el...  46.2 us
    all_gather x1, blocking collectives, gather_rows(): gathered = lax.all_gather(fresh_weights, 'z', axis=0)  26.1 us
    all_gather x1, blocking collectives, gather_rows(): gathered = lax.all_gather(gathered, ('x_lo', 'core'), axis=0)  17.8 us
    ppermute x3, starting transfers between devices, with_halo(): lax.ppermute(tail, axis, [(i, (i + 1) % count) for i in range(ends)])  14.2 us
    dot_general x54, matrix products, forward_conv(): summed = summed + jnp.dot(window, block, preferred_element_type=jnp.float32)  9.01 us
    ppermute x3, waiting for transfers between devices, with_halo(): lax.ppermute(head, axis, [((i + 1) % count, i) for i in range(ends)])  7.56 us
  transfers between devices with their start and end apart: 6, of which 2 were waited for; matrix products, arithmetic and copies ran while one was open for 10% of the time, Pallas kernels for 0%

profile of v1, /device:TPU:1, one launch (start us, length us, event | category | flops | bytes accessed | tf_op | source)
XLA Modules:
  0.0 259.9 jit_solution(9949858792519145307)
XLA Ops:
  0.6 0.9 copy.837
  1.6 5.5 %collective-permute-start = (bf16[8,12,1,128]{3,1,2,0:T(8,128)(2,1)S(1)}, bf16[8,12,1,128]{3,1,2,0:T(8,128)(2,1)S(1)}, u32[]{:S(2)}, u32[]{:S(2)}) collective-permute-start(bf16[8,12,1,128]{3,1,2,0:T(8,128)(2,1)S(1)} %get-tuple-element.85), channel_id=1, source_target_pairs={{0,1},{1,2},{2,3},{3,4},{4,5},{5,6},{6,7},{8,9},{9,10},{10,11},{11... | collective-permute-start | bytes 73736 | tf_op jit(solution)/shard_map/ppermute | solution.py:27
  7.1 1.3 collective-permute-start.1
  8.4 0.9 copy_convert_fusion
  10.4 2.9 %collective-permute-done.1 = bf16[8,12,1,128]{3,1,2,0:T(8,128)(2,1)S(1)} collective-permute-done((bf16[8,12,1,128]{3,1,2,0:T(8,128)(2,1)S(1)}, bf16[8,12,1,128]{3,1,2,0:T(8,128)(2,1)S(1)}, u32[]{:S(2)}, u32[]{:S(2)}) %collective-permute-start.1) | collective-permute-done | bytes 24608 | tf_op jit(solution)/shard_map/ppermute | solution.py:29
  20.6 4.0 %collective-permute-start.2 = (bf16[8,12,1,128]{3,0,2,1:T(8,128)(2,1)S(1)}, bf16[8,12,1,128]{3,0,2,1:T(8,128)(2,1)S(1)}, u32[]{:S(2)}, u32[]{:S(2)}) collective-permute-start(bf16[8,12,1,128]{3,0,2,1:T(8,128)(2,1)S(1)} %get-tuple-element.93), channel_id=1, source_target_pairs={{0,1},{1,2},{2,3},{3,4},{4,5},{5,6},{6,7},{8,9},{9,10},{10,11},{11... | collective-permute-start | bytes 73736 | tf_op jit(solution)/shard_map/ppermute | solution.py:27
  24.7 1.3 collective-permute-start.3
  26.1 4.7 %collective-permute-done.3 = bf16[8,12,1,128]{3,0,2,1:T(8,128)(2,1)S(1)} collective-permute-done((bf16[8,12,1,128]{3,0,2,1:T(8,128)(2,1)S(1)}, bf16[8,12,1,128]{3,0,2,1:T(8,128)(2,1)S(1)}, u32[]{:S(2)}, u32[]{:S(2)}) %collective-permute-start.3) | collective-permute-done | bytes 24608 | tf_op jit(solution)/shard_map/ppermute | solution.py:29
  37.3 0.9 fusion.30
  38.2 4.6 %collective-permute-start.4 = (bf16[8,12,1,128]{3,0,2,1:T(8,128)(2,1)S(1)}, bf16[8,12,1,128]{3,0,2,1:T(8,128)(2,1)S(1)}, u32[]{:S(2)}, u32[]{:S(2)}) collective-permute-start(bf16[8,12,1,128]{3,0,2,1:T(8,128)(2,1)S(1)} %get-tuple-element.89), channel_id=1, source_target_pairs={{0,1},{1,2},{2,3},{3,4},{4,5},{5,6},{6,7},{8,9},{9,10},{10,11},{11... | collective-permute-start | bytes 73736 | tf_op jit(solution)/shard_map/ppermute | solution.py:27
  42.8 1.3 collective-permute-start.5
  45.0 0.9 fusion.28
  45.8 0.9 fusion.27
  46.7 0.9 fusion.26
  47.5 0.9 fusion.25
  49.2 0.9 fusion.23
  50.1 0.9 fusion.22
  51.0 0.9 fusion.21
  51.8 0.9 fusion.20
  52.7 0.9 fusion.19
  53.5 0.9 fusion.3
  54.4 0.9 fusion.18
  56.2 0.9 fusion.17
  58.7 0.9 fusion.14
  59.6 0.9 fusion.13
  60.4 0.9 fusion.12
  62.1 0.9 fusion.10
  63.0 0.9 fusion.9
  64.7 0.9 fusion.7
  65.6 0.9 fusion.6
  66.4 1.5 stack.10
  68.5 1.1 copy-done.1
  76.1 0.9 fusion.55
  77.0 0.9 fusion.54
  77.9 0.9 fusion.53
  78.7 0.9 fusion.52
  80.4 0.9 fusion.50
  81.3 0.9 fusion.49
  82.1 0.9 fusion.48
  83.0 0.9 fusion.47
  83.8 0.9 fusion.46
  84.7 0.9 fusion.45
  85.6 0.9 fusion.44
  88.1 0.9 fusion.4
  89.0 0.9 fusion.42
  89.8 0.9 fusion.41
  90.7 0.9 fusion.40
  91.6 0.9 fusion.39
  92.4 0.9 fusion.38
  93.3 0.9 fusion.37
  94.1 0.9 fusion.36
  95.0 0.9 fusion.35
  96.7 0.9 fusion.33
  99.3 2.6 %stack.9 = f32[1,16,2,2,54,128]{5,4,3,2,1,0:T(8,128)} reshape(f32[3456,128]{1,0:T(8,128)} %fusion.31) | data formatting | bytes 3538944 | tf_op jit(solution)/shard_map/stack | solution.py:131
  101.9 1.7 maximum_bitcast_fusion
  103.6 2.1 copy.698
  105.7 10.0 %all_to_all.20 = f32[2,2,16,2,54,128]{5,2,4,3,1,0:T(8,128)S(1)} all-to-all(f32[2,2,16,2,54,128]{5,2,4,3,1,0:T(8,128)S(1)} %copy.698), channel_id=1, replica_groups=mesh['z'=16,'x_lo'=2,'core'=2,'y'=4,'x_hi'=2] {'core'}, dimensions={0} | all-to-all | bytes 7077888 | tf_op jit(solution)/shard_map/all_to_all | solution.py:146
  115.7 1.7 reduce_sum.36
  117.3 24.8 %all_to_all.21 = f32[2,16,2,54,128]{4,1,3,2,0:T(8,128)S(1)} all-to-all(f32[2,16,2,54,128]{4,1,3,2,0:T(8,128)} %reduce_sum.36), channel_id=1, replica_groups=mesh['z'=16,'x_lo'=2,'core'=2,'y'=4,'x_hi'=2] {'x_lo'}, dimensions={0} | all-to-all | bytes 3538944 | tf_op jit(solution)/shard_map/all_to_all | solution.py:146
  143.0 53.7 %all_to_all.22 = f32[16,2,54,128]{3,1,2,0:T(2,128)S(1)} all-to-all(f32[16,2,54,128]{3,1,2,0:T(2,128)S(1)} %copy.701), channel_id=1, replica_groups=mesh['z'=16,'x_lo'=2,'core'=2,'y'=4,'x_hi'=2] {'z'}, dimensions={0} | all-to-all | bytes 1769472 | tf_op jit(solution)/shard_map/all_to_all | solution.py:146
  197.3 14.0 %all_to_all.23 = f32[8,1,1728]{2,1,0:T(1,128)S(1)} all-to-all(f32[8,1,1728]{2,1,0:T(1,128)S(1)} %reshape.575), channel_id=1, replica_groups=mesh['z'=16,'x_lo'=2,'core'=2,'y'=4,'x_hi'=2] {'y','x_hi'}, dimensions={0} | all-to-all | bytes 110592 | tf_op jit(solution)/shard_map/all_to_all | solution.py:146
  213.4 26.1 %all-gather = bf16[32,54,16]{1,2,0:T(8,128)(2,1)S(1)} all-gather(bf16[2,54,16]{1,2,0:T(8,128)(2,1)S(1)} %get-tuple-element.5), channel_id=2, replica_groups=mesh['z'=16,'x_lo'=2,'core'=2,'y'=4,'x_hi'=2] {'z'}, dimensions={0}, use_global_device_ids=true | all-gather | bytes 58752 | tf_op jit(solution)/shard_map/all_gather | solution.py:167
  239.6 17.8 %all-gather.1 = bf16[64,2,54,16]{2,3,1,0:T(8,128)(2,1)S(1)} all-gather(bf16[16,2,54,16]{2,3,1,0:T(8,128)(2,1)S(1)} %bitcast.779), channel_id=3, replica_groups=mesh['z'=16,'x_lo'=2,'core'=2,'y'=4,'x_hi'=2] {'x_lo','core'}, dimensions={0}, use_global_device_ids=true | all-gather | bytes 276480 | tf_op jit(solution)/shard_map/all_gather | solution.py:168
  257.9 1.4 reshape.515
  (230 shorter events, 37.0 us)
Async XLA Ops:
  1.6 8.8 %collective-permute-start = (bf16[8,12,1,128]{3,1,2,0:T(8,128)(2,1)S(1)}, bf16[8,12,1,128]{3,1,2,0:T(8,128)(2,1)S(1)}, u32[]{:S(2)}, u32[]{:S(2)}) collective-permute-start(bf16[8,12,1,128]{3,1,2,0:T(8,128)(2,1)S(1)} %get-tuple-element.85), channel_id=1, source_target_pairs={{0,1},{1,2},{2,3},{3,4},{4,5},{5,6},{6,7},{8,9},{9,10},{10,11},{11... | collective-permute-start | bytes 73736 | tf_op jit(solution)/shard_map/ppermute | solution.py:27
  7.1 6.2 %collective-permute-start.1 = (bf16[8,12,1,128]{3,1,2,0:T(8,128)(2,1)S(1)}, bf16[8,12,1,128]{3,1,2,0:T(8,128)(2,1)S(1)}, u32[]{:S(2)}, u32[]{:S(2)}) collective-permute-start(bf16[8,12,1,128]{3,1,2,0:T(8,128)(2,1)S(1)} %get-tuple-element.86), channel_id=1, source_target_pairs={{1,0},{2,1},{3,2},{4,3},{5,4},{6,5},{7,6},{9,8},{10,9},{11,10},{12... | collective-permute-start | bytes 73736 | tf_op jit(solution)/shard_map/ppermute | solution.py:29
  14.4 1.5 copy-start
  16.9 1.2 copy-start.2
  20.6 5.4 %collective-permute-start.2 = (bf16[8,12,1,128]{3,0,2,1:T(8,128)(2,1)S(1)}, bf16[8,12,1,128]{3,0,2,1:T(8,128)(2,1)S(1)}, u32[]{:S(2)}, u32[]{:S(2)}) collective-permute-start(bf16[8,12,1,128]{3,0,2,1:T(8,128)(2,1)S(1)} %get-tuple-element.93), channel_id=1, source_target_pairs={{0,1},{1,2},{2,3},{3,4},{4,5},{5,6},{6,7},{8,9},{9,10},{10,11},{11... | collective-permute-start | bytes 73736 | tf_op jit(solution)/shard_map/ppermute | solution.py:27
  24.7 6.1 %collective-permute-start.3 = (bf16[8,12,1,128]{3,0,2,1:T(8,128)(2,1)S(1)}, bf16[8,12,1,128]{3,0,2,1:T(8,128)(2,1)S(1)}, u32[]{:S(2)}, u32[]{:S(2)}) collective-permute-start(bf16[8,12,1,128]{3,0,2,1:T(8,128)(2,1)S(1)} %get-tuple-element.94), channel_id=1, source_target_pairs={{1,0},{2,1},{3,2},{4,3},{5,4},{6,5},{7,6},{9,8},{10,9},{11,10},{12... | collective-permute-start | bytes 73736 | tf_op jit(solution)/shard_map/ppermute | solution.py:29
  35.9 1.2 copy-start.3
  38.2 29.8 %collective-permute-start.4 = (bf16[8,12,1,128]{3,0,2,1:T(8,128)(2,1)S(1)}, bf16[8,12,1,128]{3,0,2,1:T(8,128)(2,1)S(1)}, u32[]{:S(2)}, u32[]{:S(2)}) collective-permute-start(bf16[8,12,1,128]{3,0,2,1:T(8,128)(2,1)S(1)} %get-tuple-element.89), channel_id=1, source_target_pairs={{0,1},{1,2},{2,3},{3,4},{4,5},{5,6},{6,7},{8,9},{9,10},{10,11},{11... | collective-permute-start | bytes 73736 | tf_op jit(solution)/shard_map/ppermute | solution.py:27
  42.8 25.1 %collective-permute-start.5 = (bf16[8,12,1,128]{3,0,2,1:T(8,128)(2,1)S(1)}, bf16[8,12,1,128]{3,0,2,1:T(8,128)(2,1)S(1)}, u32[]{:S(2)}, u32[]{:S(2)}) collective-permute-start(bf16[8,12,1,128]{3,0,2,1:T(8,128)(2,1)S(1)} %get-tuple-element.90), channel_id=1, source_target_pairs={{1,0},{2,1},{3,2},{4,3},{5,4},{6,5},{7,6},{9,8},{10,9},{11,10},{12... | collective-permute-start | bytes 73736 | tf_op jit(solution)/shard_map/ppermute | solution.py:29
  68.2 1.5 copy-start.1
  143.0 69.8 %copy-start.5 = (f32[2,54,16]{1,2,0:T(8,128)S(1)}, f32[2,54,16]{1,2,0:T(8,128)}, u32[]{:S(2)}) copy-start(f32[2,54,16]{1,2,0:T(8,128)} %param.12) | copy-start | bytes 20740
  143.0 69.8 %copy-start.6 = (f32[2,54,16]{1,2,0:T(8,128)S(1)}, f32[2,54,16]{1,2,0:T(8,128)}, u32[]{:S(2)}) copy-start(f32[2,54,16]{1,2,0:T(8,128)} %param.13) | copy-start | bytes 20740
  143.0 69.8 %copy-start.7 = (f32[2,54,16]{1,2,0:T(8,128)S(1)}, f32[2,54,16]{1,2,0:T(8,128)}, u32[]{:S(2)}) copy-start(f32[2,54,16]{1,2,0:T(8,128)} %param.14) | copy-start | bytes 20740
  197.1 62.1 %copy-start.8 = (f32[2,54,16]{1,2,0:T(8,128)S(1)}, f32[2,54,16]{1,2,0:T(8,128)}, u32[]{:S(2)}) copy-start(f32[2,54,16]{1,2,0:T(8,128)} %param.15) | copy-start | bytes 20740
  213.4 46.4 %copy-start.4 = (f32[2,54,16]{1,2,0:T(8,128)}, f32[2,54,16]{1,2,0:T(8,128)S(1)}, u32[]{:S(2)}) copy-start(f32[2,54,16]{1,2,0:T(8,128)S(1)} %get-tuple-element.6) | copy-start | bytes 20740

commit v2 on v1

--- a/solution.py
+++ b/solution.py
@@ -138,7 +138,7 @@
     return (new_master, new_moment, new_second, new_teacher, new_weights)
 
 
-ROW_AXES = ("z", "x_lo", "core")
+ROW_AXES = ("z_hi", "z_lo", "x_lo", "core")
 COLUMN_AXES = ("y", "x_hi")
 
 
@@ -150,13 +150,14 @@
 def scatter_rows_and_columns(weight_grads, own_shape):
     layers, rows, cols = own_shape
     lanes = weight_grads.shape[-1]
-    z, x_lo, core = (lax.axis_size(name) for name in ROW_AXES)
+    z_hi, z_lo, x_lo, core = (lax.axis_size(name) for name in ROW_AXES)
     y, x_hi = (lax.axis_size(name) for name in COLUMN_AXES)
-    blocks = weight_grads.reshape(layers, z, x_lo, core, rows, lanes)
-    blocks = blocks.transpose(3, 2, 1, 0, 4, 5)
+    blocks = weight_grads.reshape(layers, z_hi, z_lo, x_lo, core, rows, lanes)
+    blocks = blocks.transpose(4, 3, 2, 1, 0, 5, 6)
     blocks = exchange_and_sum(blocks, "core")
     blocks = exchange_and_sum(blocks, "x_lo")
-    blocks = exchange_and_sum(blocks, "z")
+    blocks = exchange_and_sum(blocks, "z_lo")
+    blocks = exchange_and_sum(blocks, "z_hi")
     blocks = blocks.reshape(layers, rows, y * x_hi, cols).transpose(2, 0, 1, 3)
     blocks = exchange_and_sum(blocks, COLUMN_AXES)
     return blocks * unit_scale()
@@ -164,19 +165,17 @@
 
 def gather_rows(fresh_weights):
     layers, rows, cols = fresh_weights.shape
-    gathered = lax.all_gather(fresh_weights, "z", axis=0)
-    gathered = lax.all_gather(gathered, ("x_lo", "core"), axis=0)
-    gathered = gathered.reshape((-1,) + gathered.shape[1:])
-    x_lo, core = lax.axis_size("x_lo"), lax.axis_size("core")
-    gathered = gathered.reshape((x_lo, core) + gathered.shape[1:])
-    gathered = gathered.transpose(3, 2, 0, 1, 4, 5)
+    gathered = fresh_weights
+    for name in ROW_AXES:
+        gathered = lax.all_gather(gathered, name, axis=0)
+    gathered = gathered.transpose(4, 3, 2, 1, 0, 5, 6)
     return gathered.reshape(layers, -1, cols)
 
 
 def solution(mesh):
     rows_over, columns_over = mesh.shape["dp"], mesh.shape["slab"]
     fine = jax.sharding.Mesh(
-        mesh.devices.reshape(rows_over // 4, 2, 2, columns_over // 2, 2), ROW_AXES + COLUMN_AXES
+        mesh.devices.reshape(rows_over // 16, 4, 2, 2, columns_over // 2, 2), ROW_AXES + COLUMN_AXES
     )
     dp, slab = ROW_AXES, COLUMN_AXES
     in_specs = (

time: 261 us -> 262 us (level)
    all_gather x2 -> x4, blocking collectives: 43.9 us -> 45.1 us  [gather_rows(): gathered = lax.all_gather(gathered, name, axis=0)]
    all_to_all x4 -> x5, blocking collectives: 102 us -> 102 us  [exchange_and_sum(): moved = lax.all_to_all(blocks, axes, 0, 0, tiled=True)]
where the time goes in v2:
time: 262 us
  blocking collectives  147 us (56%)
  matrix products  60 us (23%)
  starting transfers between devices  18.1 us (7%)
  local copies, waits for them, and re-layouts  17 us (6%)
  other arithmetic  10.4 us (4%)
  waiting for transfers between devices  7.57 us (3%)
    all_to_all x5, blocking collectives, exchange_and_sum(): moved = lax.all_to_all(blocks, axes, 0, 0, tiled=True)  102 us
    dot_general x54, matrix products, weight_grad(): lax.dot_general(window, grad_rows, (((0,), (0,)), ((), ())), preferred_el...  45.9 us
    all_gather x4, blocking collectives, gather_rows(): gathered = lax.all_gather(gathered, name, axis=0)  45.1 us
    ppermute x3, starting transfers between devices, with_halo(): lax.ppermute(tail, axis, [(i, (i + 1) % count) for i in range(ends)])  14.2 us
    dot_general x54, matrix products, forward_conv(): summed = summed + jnp.dot(window, block, preferred_element_type=jnp.float32)  9.01 us
    ppermute x3, waiting for transfers between devices, with_halo(): lax.ppermute(head, axis, [((i + 1) % count, i) for i in range(ends)])  7.56 us
  transfers between devices with their start and end apart: 6, of which 2 were waited for; matrix products, arithmetic and copies ran while one was open for 10% of the time, Pallas kernels for 0%

profile of v2, /device:TPU:1, one launch (start us, length us, event | category | flops | bytes accessed | tf_op | source)
XLA Modules:
  0.0 261.5 jit_solution(3447097496495958220)
XLA Ops:
  0.6 0.9 copy.837
  1.6 5.5 %collective-permute-start = (bf16[8,12,1,128]{3,1,2,0:T(8,128)(2,1)S(1)}, bf16[8,12,1,128]{3,1,2,0:T(8,128)(2,1)S(1)}, u32[]{:S(2)}, u32[]{:S(2)}) collective-permute-start(bf16[8,12,1,128]{3,1,2,0:T(8,128)(2,1)S(1)} %get-tuple-element.85), channel_id=1, source_target_pairs={{0,1},{1,2},{2,3},{3,4},{4,5},{5,6},{6,7},{8,9},{9,10},{10,11},{11... | collective-permute-start | bytes 73736 | tf_op jit(solution)/shard_map/ppermute | solution.py:27
  7.1 1.3 collective-permute-start.1
  8.4 0.9 copy_convert_fusion
  10.4 2.9 %collective-permute-done.1 = bf16[8,12,1,128]{3,1,2,0:T(8,128)(2,1)S(1)} collective-permute-done((bf16[8,12,1,128]{3,1,2,0:T(8,128)(2,1)S(1)}, bf16[8,12,1,128]{3,1,2,0:T(8,128)(2,1)S(1)}, u32[]{:S(2)}, u32[]{:S(2)}) %collective-permute-start.1) | collective-permute-done | bytes 24608 | tf_op jit(solution)/shard_map/ppermute | solution.py:29
  20.6 4.0 %collective-permute-start.2 = (bf16[8,12,1,128]{3,0,2,1:T(8,128)(2,1)S(1)}, bf16[8,12,1,128]{3,0,2,1:T(8,128)(2,1)S(1)}, u32[]{:S(2)}, u32[]{:S(2)}) collective-permute-start(bf16[8,12,1,128]{3,0,2,1:T(8,128)(2,1)S(1)} %get-tuple-element.93), channel_id=1, source_target_pairs={{0,1},{1,2},{2,3},{3,4},{4,5},{5,6},{6,7},{8,9},{9,10},{10,11},{11... | collective-permute-start | bytes 73736 | tf_op jit(solution)/shard_map/ppermute | solution.py:27
  24.7 1.3 collective-permute-start.3
  26.1 4.7 %collective-permute-done.3 = bf16[8,12,1,128]{3,0,2,1:T(8,128)(2,1)S(1)} collective-permute-done((bf16[8,12,1,128]{3,0,2,1:T(8,128)(2,1)S(1)}, bf16[8,12,1,128]{3,0,2,1:T(8,128)(2,1)S(1)}, u32[]{:S(2)}, u32[]{:S(2)}) %collective-permute-start.3) | collective-permute-done | bytes 24608 | tf_op jit(solution)/shard_map/ppermute | solution.py:29
  37.3 0.9 fusion.30
  38.2 4.6 %collective-permute-start.4 = (bf16[8,12,1,128]{3,0,2,1:T(8,128)(2,1)S(1)}, bf16[8,12,1,128]{3,0,2,1:T(8,128)(2,1)S(1)}, u32[]{:S(2)}, u32[]{:S(2)}) collective-permute-start(bf16[8,12,1,128]{3,0,2,1:T(8,128)(2,1)S(1)} %get-tuple-element.89), channel_id=1, source_target_pairs={{0,1},{1,2},{2,3},{3,4},{4,5},{5,6},{6,7},{8,9},{9,10},{10,11},{11... | collective-permute-start | bytes 73736 | tf_op jit(solution)/shard_map/ppermute | solution.py:27
  42.8 1.3 collective-permute-start.5
  44.1 0.9 fusion.29
  45.0 0.9 fusion.28
  45.8 0.8 fusion.27
  47.5 0.8 fusion.25
  49.2 0.9 fusion.23
  50.9 0.8 fusion.21
  51.8 0.9 fusion.20
  52.6 0.9 fusion.19
  54.3 0.9 fusion.18
  55.3 0.8 fusion.2
  56.1 0.8 fusion.17
  57.0 0.9 fusion.16
  58.7 0.8 fusion.14
  59.5 0.8 fusion.13
  60.4 0.8 fusion.12
  62.0 0.8 fusion.10
  62.9 0.9 fusion.9
  63.8 0.9 fusion.8
  66.3 1.5 stack.10
  68.4 1.1 copy-done.1
  76.9 0.9 fusion.54
  78.6 0.9 fusion.52
  79.4 0.9 fusion.51
  80.3 0.9 fusion.50
  81.1 0.8 fusion.49
  82.0 0.9 fusion.48
  82.8 0.9 fusion.47
  84.5 0.8 fusion.45
  85.4 0.9 fusion.44
  86.2 0.8 fusion.5
  87.9 0.8 fusion.4
  88.8 0.8 fusion.42
  89.6 0.8 fusion.41
  90.5 0.8 fusion.40
  93.0 0.8 fusion.37
  93.9 0.9 fusion.36
  95.6 0.8 fusion.34
  97.3 0.9 fusion.32
  98.1 0.8 fusion.31
  99.0 2.6 stack.9
  101.6 1.7 maximum_bitcast_fusion
  103.3 2.3 copy.698
  105.6 10.0 %all_to_all.25 = f32[2,2,4,4,2,54,128]{6,3,5,4,2,1,0:T(4,128)S(1)} all-to-all(f32[2,2,4,4,2,54,128]{6,3,5,4,2,1,0:T(4,128)S(1)} %copy.698), channel_id=1, replica_groups=mesh['z_hi'=4,'z_lo'=4,'x_lo'=2,'core'=2,'y'=4,'x_hi'=2] {'core'}, dimensions={0} | all-to-all | bytes 7077888 | tf_op jit(solution)/shard_map/all_to_all | solution.py:146
  115.6 2.9 %reduce_sum.45 = f32[2,4,4,2,54,128]{5,2,4,3,1,0:T(4,128)} reduce(f32[2,2,4,4,2,54,128]{6,3,5,4,2,1,0:T(4,128)S(1)} %all_to_all.25, f32[]{:T(128)} %constant.8.clone.1), dimensions={0}, to_apply=%region_0.1 | reduce | flops 442368 | bytes 5308420 | tf_op jit(solution)/shard_map/reduce_sum | solution.py:147
  118.5 25.0 %all_to_all.26 = f32[2,4,4,2,54,128]{5,2,4,3,1,0:T(4,128)S(1)} all-to-all(f32[2,4,4,2,54,128]{5,2,4,3,1,0:T(4,128)} %reduce_sum.45), channel_id=1, replica_groups=mesh['z_hi'=4,'z_lo'=4,'x_lo'=2,'core'=2,'y'=4,'x_hi'=2] {'x_lo'}, dimensions={0} | all-to-all | bytes 3538944 | tf_op jit(solution)/shard_map/all_to_all | solution.py:146
  144.3 26.9 %all_to_all.27 = f32[4,4,2,54,128]{4,1,3,2,0:T(4,128)S(1)} all-to-all(f32[4,4,2,54,128]{4,1,3,2,0:T(4,128)S(1)} %reduce_sum.46), channel_id=1, replica_groups=mesh['z_hi'=4,'z_lo'=4,'x_lo'=2,'core'=2,'y'=4,'x_hi'=2] {'z_lo'}, dimensions={0} | all-to-all | bytes 1769472 | tf_op jit(solution)/shard_map/all_to_all | solution.py:146
  171.5 25.9 %all_to_all.28 = f32[4,2,54,128]{3,1,2,0:T(2,128)S(1)} all-to-all(f32[4,2,54,128]{3,1,2,0:T(2,128)S(1)} %copy.701), channel_id=1, replica_groups=mesh['z_hi'=4,'z_lo'=4,'x_lo'=2,'core'=2,'y'=4,'x_hi'=2] {'z_hi'}, dimensions={0} | all-to-all | bytes 442368 | tf_op jit(solution)/shard_map/all_to_all | solution.py:146
  197.8 14.0 %all_to_all.29 = f32[8,1,1728]{2,1,0:T(1,128)S(1)} all-to-all(f32[8,1,1728]{2,1,0:T(1,128)S(1)} %reshape.572), channel_id=1, replica_groups=mesh['z_hi'=4,'z_lo'=4,'x_lo'=2,'core'=2,'y'=4,'x_hi'=2] {'y','x_hi'}, dimensions={0} | all-to-all | bytes 110592 | tf_op jit(solution)/shard_map/all_to_all | solution.py:146
  213.9 14.4 %all-gather = bf16[8,54,16]{1,2,0:T(8,128)(2,1)S(1)} all-gather(bf16[2,54,16]{1,2,0:T(8,128)(2,1)S(1)} %get-tuple-element.5), channel_id=2, replica_groups=mesh['z_hi'=4,'z_lo'=4,'x_lo'=2,'core'=2,'y'=4,'x_hi'=2] {'z_hi'}, dimensions={0}, use_global_device_ids=true | all-gather | bytes 17280 | tf_op jit(solution)/shard_map/all_gather | solution.py:170
  228.3 11.6 %all-gather.1 = bf16[16,2,54,16]{2,3,1,0:T(8,128)(2,1)S(1)} all-gather(bf16[4,2,54,16]{2,3,1,0:T(8,128)(2,1)S(1)} %bitcast.864), channel_id=3, replica_groups=mesh['z_hi'=4,'z_lo'=4,'x_lo'=2,'core'=2,'y'=4,'x_hi'=2] {'z_lo'}, dimensions={0}, use_global_device_ids=true | all-gather | bytes 69120 | tf_op jit(solution)/shard_map/all_gather | solution.py:170
  239.9 4.5 %all-gather.2 = bf16[8,4,2,54,16]{3,4,2,1,0:T(8,128)(2,1)S(1)} all-gather(bf16[4,4,2,54,16]{3,4,2,1,0:T(8,128)(2,1)S(1)} %bitcast.782), channel_id=4, replica_groups=mesh['z_hi'=4,'z_lo'=4,'x_lo'=2,'core'=2,'y'=4,'x_hi'=2] {'x_lo'}, dimensions={0}, use_global_device_ids=true | all-gather | bytes 165888 | tf_op jit(solution)/shard_map/all_gather | solution.py:170
  244.4 14.6 %all-gather.3 = bf16[4,4,4,2,54,16]{4,5,3,2,1,0:T(8,128)(2,1)S(1)} all-gather(bf16[2,4,4,2,54,16]{4,5,3,2,1,0:T(8,128)(2,1)S(1)} %bitcast.777), channel_id=5, replica_groups=mesh['z_hi'=4,'z_lo'=4,'x_lo'=2,'core'=2,'y'=4,'x_hi'=2] {'core'}, dimensions={0}, use_global_device_ids=true | all-gather | bytes 331776 | tf_op jit(solution)/shard_map/all_gather | solution.py:170
  259.6 1.4 reshape.511
  (234 shorter events, 39.6 us)
Async XLA Ops:
  1.6 8.8 %collective-permute-start = (bf16[8,12,1,128]{3,1,2,0:T(8,128)(2,1)S(1)}, bf16[8,12,1,128]{3,1,2,0:T(8,128)(2,1)S(1)}, u32[]{:S(2)}, u32[]{:S(2)}) collective-permute-start(bf16[8,12,1,128]{3,1,2,0:T(8,128)(2,1)S(1)} %get-tuple-element.85), channel_id=1, source_target_pairs={{0,1},{1,2},{2,3},{3,4},{4,5},{5,6},{6,7},{8,9},{9,10},{10,11},{11... | collective-permute-start | bytes 73736 | tf_op jit(solution)/shard_map/ppermute | solution.py:27
  7.1 6.2 %collective-permute-start.1 = (bf16[8,12,1,128]{3,1,2,0:T(8,128)(2,1)S(1)}, bf16[8,12,1,128]{3,1,2,0:T(8,128)(2,1)S(1)}, u32[]{:S(2)}, u32[]{:S(2)}) collective-permute-start(bf16[8,12,1,128]{3,1,2,0:T(8,128)(2,1)S(1)} %get-tuple-element.86), channel_id=1, source_target_pairs={{1,0},{2,1},{3,2},{4,3},{5,4},{6,5},{7,6},{9,8},{10,9},{11,10},{12... | collective-permute-start | bytes 73736 | tf_op jit(solution)/shard_map/ppermute | solution.py:29
  14.4 1.5 copy-start
  16.9 1.2 copy-start.2
  20.6 5.4 %collective-permute-start.2 = (bf16[8,12,1,128]{3,0,2,1:T(8,128)(2,1)S(1)}, bf16[8,12,1,128]{3,0,2,1:T(8,128)(2,1)S(1)}, u32[]{:S(2)}, u32[]{:S(2)}) collective-permute-start(bf16[8,12,1,128]{3,0,2,1:T(8,128)(2,1)S(1)} %get-tuple-element.93), channel_id=1, source_target_pairs={{0,1},{1,2},{2,3},{3,4},{4,5},{5,6},{6,7},{8,9},{9,10},{10,11},{11... | collective-permute-start | bytes 73736 | tf_op jit(solution)/shard_map/ppermute | solution.py:27
  24.7 6.1 %collective-permute-start.3 = (bf16[8,12,1,128]{3,0,2,1:T(8,128)(2,1)S(1)}, bf16[8,12,1,128]{3,0,2,1:T(8,128)(2,1)S(1)}, u32[]{:S(2)}, u32[]{:S(2)}) collective-permute-start(bf16[8,12,1,128]{3,0,2,1:T(8,128)(2,1)S(1)} %get-tuple-element.94), channel_id=1, source_target_pairs={{1,0},{2,1},{3,2},{4,3},{5,4},{6,5},{7,6},{9,8},{10,9},{11,10},{12... | collective-permute-start | bytes 73736 | tf_op jit(solution)/shard_map/ppermute | solution.py:29
  35.9 1.2 copy-start.3
  38.2 29.6 %collective-permute-start.4 = (bf16[8,12,1,128]{3,0,2,1:T(8,128)(2,1)S(1)}, bf16[8,12,1,128]{3,0,2,1:T(8,128)(2,1)S(1)}, u32[]{:S(2)}, u32[]{:S(2)}) collective-permute-start(bf16[8,12,1,128]{3,0,2,1:T(8,128)(2,1)S(1)} %get-tuple-element.89), channel_id=1, source_target_pairs={{0,1},{1,2},{2,3},{3,4},{4,5},{5,6},{6,7},{8,9},{9,10},{10,11},{11... | collective-permute-start | bytes 73736 | tf_op jit(solution)/shard_map/ppermute | solution.py:27
  42.8 25.0 %collective-permute-start.5 = (bf16[8,12,1,128]{3,0,2,1:T(8,128)(2,1)S(1)}, bf16[8,12,1,128]{3,0,2,1:T(8,128)(2,1)S(1)}, u32[]{:S(2)}, u32[]{:S(2)}) collective-permute-start(bf16[8,12,1,128]{3,0,2,1:T(8,128)(2,1)S(1)} %get-tuple-element.90), channel_id=1, source_target_pairs={{1,0},{2,1},{3,2},{4,3},{5,4},{6,5},{7,6},{9,8},{10,9},{11,10},{12... | collective-permute-start | bytes 73736 | tf_op jit(solution)/shard_map/ppermute | solution.py:29
  68.1 1.5 copy-start.1
  171.2 42.1 %copy-start.5 = (f32[2,54,16]{1,2,0:T(8,128)S(1)}, f32[2,54,16]{1,2,0:T(8,128)}, u32[]{:S(2)}) copy-start(f32[2,54,16]{1,2,0:T(8,128)} %param.12) | copy-start | bytes 20740
  171.2 42.1 %copy-start.6 = (f32[2,54,16]{1,2,0:T(8,128)S(1)}, f32[2,54,16]{1,2,0:T(8,128)}, u32[]{:S(2)}) copy-start(f32[2,54,16]{1,2,0:T(8,128)} %param.13) | copy-start | bytes 20740
  171.2 42.1 %copy-start.7 = (f32[2,54,16]{1,2,0:T(8,128)S(1)}, f32[2,54,16]{1,2,0:T(8,128)}, u32[]{:S(2)}) copy-start(f32[2,54,16]{1,2,0:T(8,128)} %param.14) | copy-start | bytes 20740
  213.2 47.7 %copy-start.8 = (f32[2,54,16]{1,2,0:T(8,128)S(1)}, f32[2,54,16]{1,2,0:T(8,128)}, u32[]{:S(2)}) copy-start(f32[2,54,16]{1,2,0:T(8,128)} %param.15) | copy-start | bytes 20740
  213.9 47.6 %copy-start.4 = (f32[2,54,16]{1,2,0:T(8,128)}, f32[2,54,16]{1,2,0:T(8,128)S(1)}, u32[]{:S(2)}) copy-start(f32[2,54,16]{1,2,0:T(8,128)S(1)} %get-tuple-element.6) | copy-start | bytes 20740

commit v3 on v1

--- a/solution.py
+++ b/solution.py
@@ -60,40 +60,34 @@
     return window.reshape(-1, window.shape[-1])
 
 
+def stacked_windows(padded, starts, extent):
+    return jnp.concatenate([take_window(padded, start, extent) for start in starts], axis=-1)
+
+
 def forward_conv(padded, weight_rows, extent):
     channels = weight_rows.shape[1]
-    summed = jnp.zeros((extent[0] * extent[1] * extent[2], channels), jnp.float32)
-    for tap_index, corner in enumerate(tap_corners()):
-        window = take_window(padded, corner, extent)
-        block = weight_rows[tap_index * channels : (tap_index + 1) * channels]
-        summed = summed + jnp.dot(window, block, preferred_element_type=jnp.float32)
+    columns = stacked_windows(padded, tap_corners(), extent)
+    summed = jnp.dot(columns, weight_rows, preferred_element_type=jnp.float32)
     return (summed * unit_scale()).reshape(extent + (channels,))
 
 
 def transposed_conv(padded_grad, weight_rows, extent):
     channels = weight_rows.shape[1]
-    summed = jnp.zeros((extent[0] * extent[1] * extent[2], channels), jnp.float32)
-    for tap_index, corner in enumerate(tap_corners()):
-        start = (2 - corner[0], 2 - corner[1], 2 - corner[2])
-        window = take_window(padded_grad, start, extent)
-        block = weight_rows[tap_index * channels : (tap_index + 1) * channels]
-        summed = summed + lax.dot_general(
-            window, block, (((1,), (1,)), ((), ())), preferred_element_type=jnp.float32
-        )
+    starts = [(2 - a, 2 - b, 2 - c) for a, b, c in tap_corners()]
+    columns = stacked_windows(padded_grad, starts, extent)
+    flipped = weight_rows.reshape(TAPS, channels, channels).transpose(0, 2, 1)
+    summed = jnp.dot(
+        columns, flipped.reshape(TAPS * channels, channels), preferred_element_type=jnp.float32
+    )
     return (summed * unit_scale()).reshape(extent + (channels,))
 
 
 def weight_grad(padded, grad_field, extent):
     grad_rows = grad_field.reshape(-1, grad_field.shape[-1])
-    blocks = []
-    for corner in tap_corners():
-        window = take_window(padded, corner, extent)
-        blocks.append(
-            lax.dot_general(
-                window, grad_rows, (((0,), (0,)), ((), ())), preferred_element_type=jnp.float32
-            )
-        )
-    return jnp.concatenate(blocks, axis=0)
+    columns = stacked_windows(padded, tap_corners(), extent)
+    return lax.dot_general(
+        columns, grad_rows, (((0,), (0,)), ((), ())), preferred_element_type=jnp.float32
+    )
 
 
 def adam_update(master, moment, second, teacher, gradient):

time: 261 us -> 233 us (0.89)
  matrix products: 60.2 us -> 9.33 us
  local copies, waits for them, and re-layouts: 17.3 us -> 35.2 us
  waiting for transfers between devices: 7.57 us -> 1.2 us
  starting transfers between devices: 18.1 us -> 23.7 us
  blocking collectives: 146 us -> 150 us
  other arithmetic: 8.51 us -> 11.4 us
    dot_general x135 -> x4, matrix products: 60.2 us -> 9.33 us  [the longest x2 7.62 us: weight_grad(): lax.dot_general(columns, grad_rows, (((0,), (0,)), ((), ())), preferred_e...]
    unnamed x21 -> x118, local copies, waits for them, and re-layouts: 3.19 us -> 18.2 us
    ppermute x3, waiting for transfers between devices: 7.56 us -> 0.01 us  [with_halo(): lax.ppermute(head, axis, [((i + 1) % count, i) for i in range(ends)])]
    ppermute x3, starting transfers between devices: 14.2 us -> 19.8 us  [with_halo(): lax.ppermute(tail, axis, [(i, (i + 1) % count) for i in range(ends)])]
    all_to_all x4, blocking collectives: 102 us -> 106 us  [exchange_and_sum(): moved = lax.all_to_all(blocks, axes, 0, 0, tiled=True)]
    concatenate x4 -> x6, other arithmetic: 0.44 us -> 4.04 us  [with_halo(): jnp.concatenate([lax.ppermute(tail, axis, [(i, (i + 1) % count) for i in...]
  transfers between devices with their start and end apart: 6 -> 6, of which waited for: 2 -> 2; matrix products, arithmetic and copies ran while one was open for 10% -> 1% of each run, Pallas kernels for 0% -> 0%
where the time goes in v3:
time: 233 us
  blocking collectives  150 us (64%)
  local copies, waits for them, and re-layouts  35.2 us (15%)
  starting transfers between devices  23.7 us (10%)
  other arithmetic  11.4 us (5%)
  matrix products  9.33 us (4%)
    all_to_all x4, blocking collectives, exchange_and_sum(): moved = lax.all_to_all(blocks, axes, 0, 0, tiled=True)  106 us
    all_gather x1, blocking collectives, gather_rows(): gathered = lax.all_gather(fresh_weights, 'z', axis=0)  26 us
    ppermute x3, starting transfers between devices, with_halo(): lax.ppermute(tail, axis, [(i, (i + 1) % count) for i in range(ends)])  19.8 us
    unnamed x118, local copies, waits for them, and re-layouts  18.2 us
    all_gather x1, blocking collectives, gather_rows(): gathered = lax.all_gather(gathered, ('x_lo', 'core'), axis=0)  17.9 us
    dot_general x2, matrix products, weight_grad(): lax.dot_general(columns, grad_rows, (((0,), (0,)), ((), ())), preferred_e...  7.62 us
  transfers between devices with their start and end apart: 6, of which 2 were waited for; matrix products, arithmetic and copies ran while one was open for 1% of the time, Pallas kernels for 0%

profile of v3, /device:TPU:1, one launch (start us, length us, event | category | flops | bytes accessed | tf_op | source)
XLA Modules:
  0.0 232.5 jit_solution(14409098602057523702)
XLA Ops:
  0.6 1.1 fusion.28
  1.7 1.3 collective-permute-start.1
  3.0 6.1 %collective-permute-start = (bf16[8,12,1,128]{3,2,1,0:T(2,128)(2,1)S(1)}, bf16[8,12,1,128]{3,2,1,0:T(2,128)(2,1)S(1)}, u32[]{:S(2)}, u32[]{:S(2)}) collective-permute-start(bf16[8,12,1,128]{3,2,1,0:T(2,128)(2,1)S(1)} %get-tuple-element.93), channel_id=1, source_target_pairs={{0,1},{1,2},{2,3},{3,4},{4,5},{5,6},{6,7},{8,9},{9,10},{10,11},{11... | collective-permute-start | bytes 73736 | tf_op jit(solution)/shard_map/ppermute | solution.py:27
  9.1 0.7 fusion.29
  10.0 0.3 collective-permute-done
  10.3 1.1 select_maximum_fusion.4
  11.5 0.7 fusion.24
  12.7 0.2 pad_maximum_fusion.4
  13.4 0.4 copy-done.3
  13.8 0.9 convolution_multiply_fusion.2
  14.8 0.5 copy-done.4
  15.4 1.3 collective-permute-start.3
  16.7 6.4 %collective-permute-start.2 = (bf16[8,12,1,128]{3,2,1,0:T(2,128)(2,1)S(1)}, bf16[8,12,1,128]{3,2,1,0:T(2,128)(2,1)S(1)}, u32[]{:S(2)}, u32[]{:S(2)}) collective-permute-start(bf16[8,12,1,128]{3,2,1,0:T(2,128)(2,1)S(1)} %get-tuple-element.89), channel_id=1, source_target_pairs={{0,1},{1,2},{2,3},{3,4},{4,5},{5,6},{6,7},{8,9},{9,10},{10,11},{11... | collective-permute-start | bytes 73736 | tf_op jit(solution)/shard_map/ppermute | solution.py:27
  23.3 0.9 collective-permute-done.2
  24.2 0.2 select_maximum_fusion.2
  24.6 0.7 fusion.22
  25.7 0.2 pad_maximum_fusion.2
  26.6 0.9 convolution_multiply_fusion.1
  27.5 0.2 fusion.10
  27.7 0.4 copy-done
  28.1 0.7 fusion.26
  28.8 1.3 collective-permute-start.5
  30.1 7.3 %collective-permute-start.4 = (bf16[8,12,1,128]{3,2,1,0:T(2,128)(2,1)}, bf16[8,12,1,128]{3,2,1,0:T(2,128)(2,1)}, u32[]{:S(2)}, u32[]{:S(2)}) collective-permute-start(bf16[8,12,1,128]{3,2,1,0:T(2,128)(2,1)} %get-tuple-element.85), channel_id=1, source_target_pairs={{0,1},{1,2},{2,3},{3,4},{4,5},{5,6},{6,7},{8,9},{9,10},{10,11},{11... | collective-permute-start | bytes 73736 | tf_op jit(solution)/shard_map/ppermute | solution.py:27
  37.5 1.3 copy.30
  38.8 1.1 select_maximum_fusion
  40.1 1.5 fusion.20
  42.0 1.2 pad_maximum_fusion
  43.5 1.5 copy-done.5
  45.0 0.9 fusion.30
  45.9 1.4 stack.10
  47.3 0.7 constant_dynamic-update-slice_fusion.66
  48.0 1.6 constant_dynamic-update-slice_fusion.65
  49.5 1.6 constant_dynamic-update-slice_fusion.64
  51.1 1.5 constant_dynamic-update-slice_fusion.63
  52.6 1.6 constant_dynamic-update-slice_fusion.62
  54.2 1.6 constant_dynamic-update-slice_fusion.61
  55.8 1.6 constant_dynamic-update-slice_fusion.60
  57.3 0.7 constant_dynamic-update-slice_fusion.59
  58.0 0.7 constant_dynamic-update-slice_fusion.58
  58.6 0.7 constant_dynamic-update-slice_fusion.57
  59.3 0.7 constant_dynamic-update-slice_fusion.56
  60.0 0.7 constant_dynamic-update-slice_fusion.55
  60.6 0.7 constant_dynamic-update-slice_fusion.54
  61.3 6.7 %fusion.2 = f32[3456,128]{1,0:T(8,128)} fusion(bf16[384,3456]{1,0:T(8,128)(2,1)} %copy-done.4, bf16[384,3456]{1,0:T(8,128)(2,1)} %constant_dynamic-update-slice_fusion.54, bf16[3456,128]{1,0:T(8,128)(2,1)S(1)} %bitcast.125, f32[384,128]{1,0:T(8,128)S(1)} %copy-done.7, f32[384]{0:T(512)S(1)} %broadcast_multiply_fusion), kind=kOutput, calls=%fused_computation.6 | convolution fusion | flops 679968768 | bytes 8160768 | tf_op jit(solution)/shard_map/dot_general | solution.py:88
  68.0 2.7 %stack.9 = f32[1,16,2,2,54,128]{5,4,3,2,1,0:T(8,128)} reshape(f32[3456,128]{1,0:T(8,128)} %fusion.2) | data formatting | bytes 3538944 | tf_op jit(solution)/shard_map/stack | solution.py:125
  70.8 1.7 maximum_bitcast_fusion
  72.5 2.1 copy.31
  74.6 14.6 %all_to_all.20 = f32[2,2,16,2,54,128]{5,2,4,3,1,0:T(8,128)S(1)} all-to-all(f32[2,2,16,2,54,128]{5,2,4,3,1,0:T(8,128)S(1)} %copy.31), channel_id=1, replica_groups=mesh['z'=16,'x_lo'=2,'core'=2,'y'=4,'x_hi'=2] {'core'}, dimensions={0} | all-to-all | bytes 7077888 | tf_op jit(solution)/shard_map/all_to_all | solution.py:140
  89.2 1.7 reduce_sum.36
  90.9 24.8 %all_to_all.21 = f32[2,16,2,54,128]{4,1,3,2,0:T(8,128)S(1)} all-to-all(f32[2,16,2,54,128]{4,1,3,2,0:T(8,128)} %reduce_sum.36), channel_id=1, replica_groups=mesh['z'=16,'x_lo'=2,'core'=2,'y'=4,'x_hi'=2] {'x_lo'}, dimensions={0} | all-to-all | bytes 3538944 | tf_op jit(solution)/shard_map/all_to_all | solution.py:140
  115.6 0.2 reduce_sum.37
  115.8 0.7 copy.34
  116.5 48.4 %all_to_all.22 = f32[16,2,54,128]{3,1,2,0:T(2,128)S(1)} all-to-all(f32[16,2,54,128]{3,1,2,0:T(2,128)S(1)} %copy.34), channel_id=1, replica_groups=mesh['z'=16,'x_lo'=2,'core'=2,'y'=4,'x_hi'=2] {'z'}, dimensions={0} | all-to-all | bytes 1769472 | tf_op jit(solution)/shard_map/all_to_all | solution.py:140
  165.0 0.3 reduce_sum.38
  165.6 18.4 %all_to_all.23 = f32[8,1,1728]{2,1,0:T(1,128)S(1)} all-to-all(f32[8,1,1728]{2,1,0:T(1,128)S(1)} %reshape.441), channel_id=1, replica_groups=mesh['z'=16,'x_lo'=2,'core'=2,'y'=4,'x_hi'=2] {'y','x_hi'}, dimensions={0} | all-to-all | bytes 110592 | tf_op jit(solution)/shard_map/all_to_all | solution.py:140
  184.0 0.5 broadcast.127
  184.5 0.8 reduce
  185.3 0.2 reshape.442
  185.5 0.6 fusion.19
  186.1 26.0 %all-gather = bf16[32,54,16]{1,2,0:T(8,128)(2,1)S(1)} all-gather(bf16[2,54,16]{1,2,0:T(8,128)(2,1)S(1)} %get-tuple-element.5), channel_id=2, replica_groups=mesh['z'=16,'x_lo'=2,'core'=2,'y'=4,'x_hi'=2] {'z'}, dimensions={0}, use_global_device_ids=true | all-gather | bytes 58752 | tf_op jit(solution)/shard_map/all_gather | solution.py:161
  212.1 17.9 %all-gather.1 = bf16[64,2,54,16]{2,3,1,0:T(8,128)(2,1)S(1)} all-gather(bf16[16,2,54,16]{2,3,1,0:T(8,128)(2,1)S(1)} %bitcast.134), channel_id=3, replica_groups=mesh['z'=16,'x_lo'=2,'core'=2,'y'=4,'x_hi'=2] {'x_lo','core'}, dimensions={0}, use_global_device_ids=true | all-gather | bytes 276480 | tf_op jit(solution)/shard_map/all_gather | solution.py:162
  230.0 0.5 copy.37
  230.6 1.4 reshape.435
  231.9 0.6 multiply_add_fusion
  (123 shorter events, 3.4 us)
Async XLA Ops:
  1.7 8.3 %collective-permute-start.1 = (bf16[8,12,1,128]{3,2,1,0:T(2,128)(2,1)S(1)}, bf16[8,12,1,128]{3,2,1,0:T(2,128)(2,1)S(1)}, u32[]{:S(2)}, u32[]{:S(2)}) collective-permute-start(bf16[8,12,1,128]{3,2,1,0:T(2,128)(2,1)S(1)} %get-tuple-element.94), channel_id=1, source_target_pairs={{1,0},{2,1},{3,2},{4,3},{5,4},{6,5},{7,6},{9,8},{10,9},{11,10},{12... | collective-permute-start | bytes 73736 | tf_op jit(solution)/shard_map/ppermute | solution.py:29
  3.0 7.3 %collective-permute-start = (bf16[8,12,1,128]{3,2,1,0:T(2,128)(2,1)S(1)}, bf16[8,12,1,128]{3,2,1,0:T(2,128)(2,1)S(1)}, u32[]{:S(2)}, u32[]{:S(2)}) collective-permute-start(bf16[8,12,1,128]{3,2,1,0:T(2,128)(2,1)S(1)} %get-tuple-element.93), channel_id=1, source_target_pairs={{0,1},{1,2},{2,3},{3,4},{4,5},{5,6},{6,7},{8,9},{9,10},{10,11},{11... | collective-permute-start | bytes 73736 | tf_op jit(solution)/shard_map/ppermute | solution.py:27
  11.5 1.2 copy-start.8
  12.3 1.5 copy-start.3
  13.8 1.5 copy-start.4
  14.6 11.3 %copy-start.6 = (f32[384,128]{1,0:T(8,128)}, f32[384,128]{1,0:T(8,128)S(1)}, u32[]{:S(2)}) copy-start(f32[384,128]{1,0:T(8,128)S(1)} %convolution_multiply_fusion.2) | copy-start | bytes 589828
  15.4 7.9 %collective-permute-start.3 = (bf16[8,12,1,128]{3,2,1,0:T(2,128)(2,1)S(1)}, bf16[8,12,1,128]{3,2,1,0:T(2,128)(2,1)S(1)}, u32[]{:S(2)}, u32[]{:S(2)}) collective-permute-start(bf16[8,12,1,128]{3,2,1,0:T(2,128)(2,1)S(1)} %get-tuple-element.90), channel_id=1, source_target_pairs={{1,0},{2,1},{3,2},{4,3},{5,4},{6,5},{7,6},{9,8},{10,9},{11,10},{12... | collective-permute-start | bytes 73736 | tf_op jit(solution)/shard_map/ppermute | solution.py:29
  16.7 7.6 %collective-permute-start.2 = (bf16[8,12,1,128]{3,2,1,0:T(2,128)(2,1)S(1)}, bf16[8,12,1,128]{3,2,1,0:T(2,128)(2,1)S(1)}, u32[]{:S(2)}, u32[]{:S(2)}) collective-permute-start(bf16[8,12,1,128]{3,2,1,0:T(2,128)(2,1)S(1)} %get-tuple-element.89), channel_id=1, source_target_pairs={{0,1},{1,2},{2,3},{3,4},{4,5},{5,6},{6,7},{8,9},{9,10},{10,11},{11... | collective-permute-start | bytes 73736 | tf_op jit(solution)/shard_map/ppermute | solution.py:27
  26.5 0.9 copy-start.13
  26.6 1.6 copy-start
  26.6 10.9 %slice-start = ((bf16[2,3456,128]{2,1,0:T(8,128)(2,1)}), bf16[1,3456,128]{2,1,0:T(8,128)(2,1)S(1)}, s32[]{:S(2)}) async-start(bf16[2,3456,128]{2,1,0:T(8,128)(2,1)} %param.11), calls=%async_computation.4 | async-start | bytes 1769472 | tf_op jit(solution)/shard_map/slice | solution.py:115
  27.4 10.0 %copy-start.11 = (f32[384,128]{1,0:T(8,128)}, f32[384,128]{1,0:T(8,128)S(1)}, u32[]{:S(2)}) copy-start(f32[384,128]{1,0:T(8,128)S(1)} %convolution_multiply_fusion.1) | copy-start | bytes 589828
  28.1 9.3 %copy-start.9 = (bf16[8,12,4,128]{3,2,1,0:T(4,128)(2,1)}, bf16[8,12,4,128]{3,2,1,0:T(4,128)(2,1)S(1)}, u32[]{:S(2)}) copy-start(bf16[8,12,4,128]{3,2,1,0:T(4,128)(2,1)S(1)} %fusion.10) | copy-start | bytes 294916
  28.8 10.0 %collective-permute-start.5 = (bf16[8,12,1,128]{3,2,1,0:T(2,128)(2,1)}, bf16[8,12,1,128]{3,2,1,0:T(2,128)(2,1)}, u32[]{:S(2)}, u32[]{:S(2)}) collective-permute-start(bf16[8,12,1,128]{3,2,1,0:T(2,128)(2,1)} %get-tuple-element.86), channel_id=1, source_target_pairs={{1,0},{2,1},{3,2},{4,3},{5,4},{6,5},{7,6},{9,8},{10,9},{11,10},{12... | collective-permute-start | bytes 73736 | tf_op jit(solution)/shard_map/ppermute | solution.py:29
  30.1 8.7 %collective-permute-start.4 = (bf16[8,12,1,128]{3,2,1,0:T(2,128)(2,1)}, bf16[8,12,1,128]{3,2,1,0:T(2,128)(2,1)}, u32[]{:S(2)}, u32[]{:S(2)}) collective-permute-start(bf16[8,12,1,128]{3,2,1,0:T(2,128)(2,1)} %get-tuple-element.85), channel_id=1, source_target_pairs={{0,1},{1,2},{2,3},{3,4},{4,5},{5,6},{6,7},{8,9},{9,10},{10,11},{11... | collective-permute-start | bytes 73736 | tf_op jit(solution)/shard_map/ppermute | solution.py:27
  40.1 2.0 copy-start.10
  40.1 3.2 %copy-start.12 = (f32[384,128]{1,0:T(8,128)S(1)}, f32[384,128]{1,0:T(8,128)}, u32[]{:S(2)}) copy-start(f32[384,128]{1,0:T(8,128)} %copy-done.11) | copy-start | bytes 589828
  40.1 3.2 %copy-start.14 = (bf16[1,8,12,4,128]{4,3,2,1,0:T(4,128)(2,1)S(1)}, bf16[1,8,12,4,128]{4,3,2,1,0:T(4,128)(2,1)}, u32[]{:S(2)}) copy-start(bf16[1,8,12,4,128]{4,3,2,1,0:T(4,128)(2,1)} %param.10) | copy-start | bytes 294916
  41.6 3.4 %copy-start.1 = (bf16[384,3456]{1,0:T(8,128)(2,1)S(1)}, bf16[384,3456]{1,0:T(8,128)(2,1)}, u32[]{:S(2)}) copy-start(bf16[384,3456]{1,0:T(8,128)(2,1)} %copy-done) | copy-start | bytes 7962628
  43.5 1.5 copy-start.5
  45.9 15.4 %copy-start.7 = (f32[384,128]{1,0:T(8,128)S(1)}, f32[384,128]{1,0:T(8,128)}, u32[]{:S(2)}) copy-start(f32[384,128]{1,0:T(8,128)} %copy-done.6) | copy-start | bytes 589828
  68.0 2.7 %copy-start.2 = (f32[1,16,2,2,54,128]{5,4,3,2,1,0:T(8,128)S(1)}, f32[1,16,2,2,54,128]{5,4,3,2,1,0:T(8,128)}, u32[]{:S(2)}) copy-start(f32[1,16,2,2,54,128]{5,4,3,2,1,0:T(8,128)} %stack.10) | copy-start | bytes 5308420
  115.8 69.7 %copy-start.16 = (f32[2,54,16]{1,2,0:T(8,128)S(1)}, f32[2,54,16]{1,2,0:T(8,128)}, u32[]{:S(2)}) copy-start(f32[2,54,16]{1,2,0:T(8,128)} %param.12) | copy-start | bytes 20740
  115.8 69.7 %copy-start.17 = (f32[2,54,16]{1,2,0:T(8,128)S(1)}, f32[2,54,16]{1,2,0:T(8,128)}, u32[]{:S(2)}) copy-start(f32[2,54,16]{1,2,0:T(8,128)} %param.13) | copy-start | bytes 20740
  115.8 69.7 %copy-start.18 = (f32[2,54,16]{1,2,0:T(8,128)S(1)}, f32[2,54,16]{1,2,0:T(8,128)}, u32[]{:S(2)}) copy-start(f32[2,54,16]{1,2,0:T(8,128)} %param.14) | copy-start | bytes 20740
  165.0 66.9 %copy-start.19 = (f32[2,54,16]{1,2,0:T(8,128)S(1)}, f32[2,54,16]{1,2,0:T(8,128)}, u32[]{:S(2)}) copy-start(f32[2,54,16]{1,2,0:T(8,128)} %param.15) | copy-start | bytes 20740
  186.1 46.4 %copy-start.15 = (f32[2,54,16]{1,2,0:T(8,128)}, f32[2,54,16]{1,2,0:T(8,128)S(1)}, u32[]{:S(2)}) copy-start(f32[2,54,16]{1,2,0:T(8,128)S(1)} %get-tuple-element.6) | copy-start | bytes 20740

commit v4 on v3

--- a/solution.py
+++ b/solution.py
@@ -150,9 +150,13 @@
     blocks = blocks.transpose(3, 2, 1, 0, 4, 5)
     blocks = exchange_and_sum(blocks, "core")
     blocks = exchange_and_sum(blocks, "x_lo")
+    half = y * cols
+    blocks = blocks.reshape(z, layers, rows, y, x_hi, cols).transpose(4, 0, 1, 2, 3, 5)
+    blocks = blocks.reshape(x_hi, z, layers, rows * half // lanes, lanes)
+    blocks = exchange_and_sum(blocks, "x_hi")
     blocks = exchange_and_sum(blocks, "z")
-    blocks = blocks.reshape(layers, rows, y * x_hi, cols).transpose(2, 0, 1, 3)
-    blocks = exchange_and_sum(blocks, COLUMN_AXES)
+    blocks = blocks.reshape(layers, rows, y, cols).transpose(2, 0, 1, 3)
+    blocks = exchange_and_sum(blocks, "y")
     return blocks * unit_scale()
 
 

time: 233 us -> 240 us (1.030)
  local copies, waits for them, and re-layouts: 35.2 us -> 48.2 us
  blocking collectives: 150 us -> 143 us
    all_to_all x4 -> x5, blocking collectives: 106 us -> 98.6 us  [exchange_and_sum(): moved = lax.all_to_all(blocks, axes, 0, 0, tiled=True)]
    reshape x0 -> x3, local copies, waits for them, and re-layouts: none -> 7.14 us  [the longest x2 6.95 us: scatter_rows_and_columns(): blocks = blocks.reshape(x_hi, z, layers, rows * half // lanes, lanes)]
    transpose x1 -> x2, local copies, waits for them, and re-layouts: 0.01 us -> 5.79 us  [the longest x1 5.66 us: scatter_rows_and_columns(): blocks.reshape(z, layers, rows, y, x_hi, cols).transpose(4, 0, 1, 2, 3, 5)]
where the time goes in v4:
time: 240 us; the launch traced here: 239 us
  blocking collectives  143 us (60%)
  local copies, waits for them, and re-layouts  48.2 us (20%)
  starting transfers between devices  23.7 us (10%)
  other arithmetic  11.2 us (5%)
  matrix products  9.33 us (4%)
    all_to_all x5, blocking collectives, exchange_and_sum(): moved = lax.all_to_all(blocks, axes, 0, 0, tiled=True)  98.6 us
    all_gather x1, blocking collectives, gather_rows(): gathered = lax.all_gather(fresh_weights, 'z', axis=0)  26.4 us
    ppermute x3, starting transfers between devices, with_halo(): lax.ppermute(tail, axis, [(i, (i + 1) % count) for i in range(ends)])  19.8 us
    all_gather x1, blocking collectives, gather_rows(): gathered = lax.all_gather(gathered, ('x_lo', 'core'), axis=0)  18.3 us
    unnamed x118, local copies, waits for them, and re-layouts  18.1 us
    dot_general x2, matrix products, weight_grad(): lax.dot_general(columns, grad_rows, (((0,), (0,)), ((), ())), preferred_e...  7.62 us
    reshape x2, local copies, waits for them, and re-layouts, scatter_rows_and_columns(): blocks = blocks.reshape(x_hi, z, layers, rows * half // lanes, lanes)  6.95 us
    transpose x1, local copies, waits for them, and re-layouts, scatter_rows_and_columns(): blocks.reshape(z, layers, rows, y, x_hi, cols).transpose(4, 0, 1, 2, 3, 5)  5.66 us
  transfers between devices with their start and end apart: 6, of which 2 were waited for; matrix products, arithmetic and copies ran while one was open for 1% of the time, Pallas kernels for 0%

profile of v4, /device:TPU:1, one launch (start us, length us, event | category | flops | bytes accessed | tf_op | source)
XLA Modules:
  0.0 238.6 jit_solution(5395462218270999042)
XLA Ops:
  0.6 1.1 fusion.28
  1.7 1.3 collective-permute-start.1
  3.0 6.1 %collective-permute-start = (bf16[8,12,1,128]{3,2,1,0:T(2,128)(2,1)S(1)}, bf16[8,12,1,128]{3,2,1,0:T(2,128)(2,1)S(1)}, u32[]{:S(2)}, u32[]{:S(2)}) collective-permute-start(bf16[8,12,1,128]{3,2,1,0:T(2,128)(2,1)S(1)} %get-tuple-element.103), channel_id=1, source_target_pairs={{0,1},{1,2},{2,3},{3,4},{4,5},{5,6},{6,7},{8,9},{9,10},{10,11},{11... | collective-permute-start | bytes 73736 | tf_op jit(solution)/shard_map/ppermute | solution.py:27
  9.1 0.7 fusion.29
  10.0 0.3 collective-permute-done
  10.3 1.1 select_maximum_fusion.4
  11.5 0.7 fusion.24
  12.7 0.2 pad_maximum_fusion.4
  13.4 0.4 copy-done.3
  13.8 0.9 convolution_multiply_fusion.2
  14.8 0.5 copy-done.4
  15.4 1.3 collective-permute-start.3
  16.7 6.4 %collective-permute-start.2 = (bf16[8,12,1,128]{3,2,1,0:T(2,128)(2,1)S(1)}, bf16[8,12,1,128]{3,2,1,0:T(2,128)(2,1)S(1)}, u32[]{:S(2)}, u32[]{:S(2)}) collective-permute-start(bf16[8,12,1,128]{3,2,1,0:T(2,128)(2,1)S(1)} %get-tuple-element.99), channel_id=1, source_target_pairs={{0,1},{1,2},{2,3},{3,4},{4,5},{5,6},{6,7},{8,9},{9,10},{10,11},{11... | collective-permute-start | bytes 73736 | tf_op jit(solution)/shard_map/ppermute | solution.py:27
  23.3 0.9 collective-permute-done.2
  24.6 0.7 fusion.22
  25.7 0.2 pad_maximum_fusion.2
  26.6 0.9 convolution_multiply_fusion.1
  27.7 0.4 copy-done
  28.1 0.7 fusion.26
  28.8 1.3 collective-permute-start.5
  30.1 7.3 %collective-permute-start.4 = (bf16[8,12,1,128]{3,2,1,0:T(2,128)(2,1)}, bf16[8,12,1,128]{3,2,1,0:T(2,128)(2,1)}, u32[]{:S(2)}, u32[]{:S(2)}) collective-permute-start(bf16[8,12,1,128]{3,2,1,0:T(2,128)(2,1)} %get-tuple-element.95), channel_id=1, source_target_pairs={{0,1},{1,2},{2,3},{3,4},{4,5},{5,6},{6,7},{8,9},{9,10},{10,11},{11... | collective-permute-start | bytes 73736 | tf_op jit(solution)/shard_map/ppermute | solution.py:27
  37.5 1.3 copy.69
  38.8 1.1 select_maximum_fusion
  40.1 1.5 fusion.20
  42.0 1.2 pad_maximum_fusion
  43.5 1.5 copy-done.5
  45.0 0.9 fusion.30
  45.9 1.4 stack.10
  47.3 0.6 constant_dynamic-update-slice_fusion.66
  47.9 1.6 constant_dynamic-update-slice_fusion.65
  49.5 1.6 constant_dynamic-update-slice_fusion.64
  51.1 1.5 constant_dynamic-update-slice_fusion.63
  52.6 1.6 constant_dynamic-update-slice_fusion.62
  54.2 1.5 constant_dynamic-update-slice_fusion.61
  55.7 1.6 constant_dynamic-update-slice_fusion.60
  57.3 0.7 constant_dynamic-update-slice_fusion.59
  57.9 0.6 constant_dynamic-update-slice_fusion.58
  58.6 0.7 constant_dynamic-update-slice_fusion.57
  59.3 0.7 constant_dynamic-update-slice_fusion.56
  59.9 0.7 constant_dynamic-update-slice_fusion.55
  60.6 0.7 constant_dynamic-update-slice_fusion.54
  61.3 6.7 %fusion.2 = f32[3456,128]{1,0:T(8,128)} fusion(bf16[384,3456]{1,0:T(8,128)(2,1)} %copy-done.4, bf16[384,3456]{1,0:T(8,128)(2,1)} %constant_dynamic-update-slice_fusion.54, bf16[3456,128]{1,0:T(8,128)(2,1)S(1)} %bitcast.125, f32[384,128]{1,0:T(8,128)S(1)} %copy-done.7, f32[384]{0:T(512)S(1)} %broadcast_multiply_fusion), kind=kOutput, calls=%fused_computation.6 | convolution fusion | flops 679968768 | bytes 8160768 | tf_op jit(solution)/shard_map/dot_general | solution.py:88
  68.0 2.7 %stack.9 = f32[1,16,2,2,54,128]{5,4,3,2,1,0:T(8,128)} reshape(f32[3456,128]{1,0:T(8,128)} %fusion.2) | data formatting | bytes 3538944 | tf_op jit(solution)/shard_map/stack | solution.py:125
  70.7 1.7 maximum_bitcast_fusion
  72.5 2.1 copy.70
  74.5 14.5 %all_to_all.25 = f32[2,2,16,2,54,128]{5,2,4,3,1,0:T(8,128)S(1)} all-to-all(f32[2,2,16,2,54,128]{5,2,4,3,1,0:T(8,128)S(1)} %copy.70), channel_id=1, replica_groups=mesh['z'=16,'x_lo'=2,'core'=2,'y'=4,'x_hi'=2] {'core'}, dimensions={0} | all-to-all | bytes 7077888 | tf_op jit(solution)/shard_map/all_to_all | solution.py:140
  89.1 1.7 reduce_sum.45
  90.7 24.8 %all_to_all.26 = f32[2,16,2,54,128]{4,1,3,2,0:T(8,128)S(1)} all-to-all(f32[2,16,2,54,128]{4,1,3,2,0:T(8,128)} %reduce_sum.45), channel_id=1, replica_groups=mesh['z'=16,'x_lo'=2,'core'=2,'y'=4,'x_hi'=2] {'x_lo'}, dimensions={0} | all-to-all | bytes 3538944 | tf_op jit(solution)/shard_map/all_to_all | solution.py:140
  115.7 0.7 copy.73
  116.4 5.7 %copy.74 = f32[2,16,2,54,4,16]{5,4,3,2,1,0:T(4,128)} copy(f32[2,16,2,54,4,16]{3,5,0,4,2,1:T(8,128)S(1)} %bitcast.124) | data formatting | bytes 1769472 | tf_op jit(solution)/shard_map/transpose | solution.py:154
  122.0 6.4 %reshape.440 = f32[2,16,2,27,128]{4,3,2,1,0:T(8,128)S(1)} reshape(f32[2,16,2,54,4,16]{5,4,3,2,1,0:T(4,128)} %copy.74) | data formatting | bytes 1769472 | tf_op jit(solution)/shard_map/reshape | solution.py:155
  128.5 0.5 copy.75
  129.0 17.6 %all_to_all.27 = f32[2,16,2,27,128]{4,1,3,2,0:T(8,128)S(1)} all-to-all(f32[2,16,2,27,128]{4,1,3,2,0:T(8,128)S(1)} %copy.75), channel_id=1, replica_groups=mesh['z'=16,'x_lo'=2,'core'=2,'y'=4,'x_hi'=2] {'x_hi'}, dimensions={0} | all-to-all | bytes 1769472 | tf_op jit(solution)/shard_map/all_to_all | solution.py:140
  146.7 0.2 copy.76
  146.9 29.0 %all_to_all.28 = f32[16,2,27,128]{3,1,2,0:T(2,128)S(1)} all-to-all(f32[16,2,27,128]{3,1,2,0:T(2,128)S(1)} %copy.76), channel_id=1, replica_groups=mesh['z'=16,'x_lo'=2,'core'=2,'y'=4,'x_hi'=2] {'z'}, dimensions={0} | all-to-all | bytes 884736 | tf_op jit(solution)/shard_map/all_to_all | solution.py:140
  176.6 12.7 %all_to_all.29 = f32[4,1,1728]{2,1,0:T(1,128)S(1)} all-to-all(f32[4,1,1728]{2,1,0:T(1,128)S(1)} %reshape.449), channel_id=1, replica_groups=mesh['z'=16,'x_lo'=2,'core'=2,'y'=4,'x_hi'=2] {'y'}, dimensions={0} | all-to-all | bytes 55296 | tf_op jit(solution)/shard_map/all_to_all | solution.py:140
  189.3 0.5 broadcast.127
  189.8 0.7 reduce
  190.7 0.6 fusion.19
  191.3 26.4 %all-gather = bf16[32,54,16]{1,2,0:T(8,128)(2,1)S(1)} all-gather(bf16[2,54,16]{1,2,0:T(8,128)(2,1)S(1)} %get-tuple-element.15), channel_id=2, replica_groups=mesh['z'=16,'x_lo'=2,'core'=2,'y'=4,'x_hi'=2] {'z'}, dimensions={0}, use_global_device_ids=true | all-gather | bytes 58752 | tf_op jit(solution)/shard_map/all_gather | solution.py:165
  217.8 18.3 %all-gather.1 = bf16[64,2,54,16]{2,3,1,0:T(8,128)(2,1)S(1)} all-gather(bf16[16,2,54,16]{2,3,1,0:T(8,128)(2,1)S(1)} %bitcast.135), channel_id=3, replica_groups=mesh['z'=16,'x_lo'=2,'core'=2,'y'=4,'x_hi'=2] {'x_lo','core'}, dimensions={0}, use_global_device_ids=true | all-gather | bytes 276480 | tf_op jit(solution)/shard_map/all_gather | solution.py:166
  236.1 0.5 copy.83
  236.6 1.4 reshape.443
  238.0 0.6 multiply_add_fusion
  (130 shorter events, 4.5 us)
Async XLA Ops:
  1.7 8.3 %collective-permute-start.1 = (bf16[8,12,1,128]{3,2,1,0:T(2,128)(2,1)S(1)}, bf16[8,12,1,128]{3,2,1,0:T(2,128)(2,1)S(1)}, u32[]{:S(2)}, u32[]{:S(2)}) collective-permute-start(bf16[8,12,1,128]{3,2,1,0:T(2,128)(2,1)S(1)} %get-tuple-element.104), channel_id=1, source_target_pairs={{1,0},{2,1},{3,2},{4,3},{5,4},{6,5},{7,6},{9,8},{10,9},{11,10},{12... | collective-permute-start | bytes 73736 | tf_op jit(solution)/shard_map/ppermute | solution.py:29
  3.0 7.3 %collective-permute-start = (bf16[8,12,1,128]{3,2,1,0:T(2,128)(2,1)S(1)}, bf16[8,12,1,128]{3,2,1,0:T(2,128)(2,1)S(1)}, u32[]{:S(2)}, u32[]{:S(2)}) collective-permute-start(bf16[8,12,1,128]{3,2,1,0:T(2,128)(2,1)S(1)} %get-tuple-element.103), channel_id=1, source_target_pairs={{0,1},{1,2},{2,3},{3,4},{4,5},{5,6},{6,7},{8,9},{9,10},{10,11},{11... | collective-permute-start | bytes 73736 | tf_op jit(solution)/shard_map/ppermute | solution.py:27
  11.5 1.2 copy-start.8
  12.3 1.5 copy-start.3
  13.8 1.5 copy-start.4
  14.6 11.3 %copy-start.6 = (f32[384,128]{1,0:T(8,128)}, f32[384,128]{1,0:T(8,128)S(1)}, u32[]{:S(2)}) copy-start(f32[384,128]{1,0:T(8,128)S(1)} %convolution_multiply_fusion.2) | copy-start | bytes 589828
  15.4 7.9 %collective-permute-start.3 = (bf16[8,12,1,128]{3,2,1,0:T(2,128)(2,1)S(1)}, bf16[8,12,1,128]{3,2,1,0:T(2,128)(2,1)S(1)}, u32[]{:S(2)}, u32[]{:S(2)}) collective-permute-start(bf16[8,12,1,128]{3,2,1,0:T(2,128)(2,1)S(1)} %get-tuple-element.100), channel_id=1, source_target_pairs={{1,0},{2,1},{3,2},{4,3},{5,4},{6,5},{7,6},{9,8},{10,9},{11,10},{12... | collective-permute-start | bytes 73736 | tf_op jit(solution)/shard_map/ppermute | solution.py:29
  16.7 7.6 %collective-permute-start.2 = (bf16[8,12,1,128]{3,2,1,0:T(2,128)(2,1)S(1)}, bf16[8,12,1,128]{3,2,1,0:T(2,128)(2,1)S(1)}, u32[]{:S(2)}, u32[]{:S(2)}) collective-permute-start(bf16[8,12,1,128]{3,2,1,0:T(2,128)(2,1)S(1)} %get-tuple-element.99), channel_id=1, source_target_pairs={{0,1},{1,2},{2,3},{3,4},{4,5},{5,6},{6,7},{8,9},{9,10},{10,11},{11... | collective-permute-start | bytes 73736 | tf_op jit(solution)/shard_map/ppermute | solution.py:27
  26.5 0.9 copy-start.13
  26.6 1.6 copy-start
  26.6 10.9 %slice-start = ((bf16[2,3456,128]{2,1,0:T(8,128)(2,1)}), bf16[1,3456,128]{2,1,0:T(8,128)(2,1)S(1)}, s32[]{:S(2)}) async-start(bf16[2,3456,128]{2,1,0:T(8,128)(2,1)} %param.11), calls=%async_computation.5 | async-start | bytes 1769472 | tf_op jit(solution)/shard_map/slice | solution.py:115
  27.4 10.0 %copy-start.11 = (f32[384,128]{1,0:T(8,128)}, f32[384,128]{1,0:T(8,128)S(1)}, u32[]{:S(2)}) copy-start(f32[384,128]{1,0:T(8,128)S(1)} %convolution_multiply_fusion.1) | copy-start | bytes 589828
  28.1 9.3 %copy-start.9 = (bf16[8,12,4,128]{3,2,1,0:T(4,128)(2,1)}, bf16[8,12,4,128]{3,2,1,0:T(4,128)(2,1)S(1)}, u32[]{:S(2)}) copy-start(bf16[8,12,4,128]{3,2,1,0:T(4,128)(2,1)S(1)} %fusion.10) | copy-start | bytes 294916
  28.8 9.9 %collective-permute-start.5 = (bf16[8,12,1,128]{3,2,1,0:T(2,128)(2,1)}, bf16[8,12,1,128]{3,2,1,0:T(2,128)(2,1)}, u32[]{:S(2)}, u32[]{:S(2)}) collective-permute-start(bf16[8,12,1,128]{3,2,1,0:T(2,128)(2,1)} %get-tuple-element.96), channel_id=1, source_target_pairs={{1,0},{2,1},{3,2},{4,3},{5,4},{6,5},{7,6},{9,8},{10,9},{11,10},{12... | collective-permute-start | bytes 73736 | tf_op jit(solution)/shard_map/ppermute | solution.py:29
  30.1 8.7 %collective-permute-start.4 = (bf16[8,12,1,128]{3,2,1,0:T(2,128)(2,1)}, bf16[8,12,1,128]{3,2,1,0:T(2,128)(2,1)}, u32[]{:S(2)}, u32[]{:S(2)}) collective-permute-start(bf16[8,12,1,128]{3,2,1,0:T(2,128)(2,1)} %get-tuple-element.95), channel_id=1, source_target_pairs={{0,1},{1,2},{2,3},{3,4},{4,5},{5,6},{6,7},{8,9},{9,10},{10,11},{11... | collective-permute-start | bytes 73736 | tf_op jit(solution)/shard_map/ppermute | solution.py:27
  40.1 1.9 copy-start.10
  40.1 3.2 %copy-start.12 = (f32[384,128]{1,0:T(8,128)S(1)}, f32[384,128]{1,0:T(8,128)}, u32[]{:S(2)}) copy-start(f32[384,128]{1,0:T(8,128)} %copy-done.11) | copy-start | bytes 589828
  40.1 3.2 %copy-start.14 = (bf16[1,8,12,4,128]{4,3,2,1,0:T(4,128)(2,1)S(1)}, bf16[1,8,12,4,128]{4,3,2,1,0:T(4,128)(2,1)}, u32[]{:S(2)}) copy-start(bf16[1,8,12,4,128]{4,3,2,1,0:T(4,128)(2,1)} %param.10) | copy-start | bytes 294916
  41.6 3.4 %copy-start.1 = (bf16[384,3456]{1,0:T(8,128)(2,1)S(1)}, bf16[384,3456]{1,0:T(8,128)(2,1)}, u32[]{:S(2)}) copy-start(bf16[384,3456]{1,0:T(8,128)(2,1)} %copy-done) | copy-start | bytes 7962628
  43.5 1.5 copy-start.5
  45.9 15.4 %copy-start.7 = (f32[384,128]{1,0:T(8,128)S(1)}, f32[384,128]{1,0:T(8,128)}, u32[]{:S(2)}) copy-start(f32[384,128]{1,0:T(8,128)} %copy-done.6) | copy-start | bytes 589828
  68.0 2.7 %copy-start.2 = (f32[1,16,2,2,54,128]{5,4,3,2,1,0:T(8,128)S(1)}, f32[1,16,2,2,54,128]{5,4,3,2,1,0:T(8,128)}, u32[]{:S(2)}) copy-start(f32[1,16,2,2,54,128]{5,4,3,2,1,0:T(8,128)} %stack.10) | copy-start | bytes 5308420
  146.6 44.1 %copy-start.16 = (f32[2,54,16]{1,2,0:T(8,128)S(1)}, f32[2,54,16]{1,2,0:T(8,128)}, u32[]{:S(2)}) copy-start(f32[2,54,16]{1,2,0:T(8,128)} %param.12) | copy-start | bytes 20740
  146.6 44.1 %copy-start.17 = (f32[2,54,16]{1,2,0:T(8,128)S(1)}, f32[2,54,16]{1,2,0:T(8,128)}, u32[]{:S(2)}) copy-start(f32[2,54,16]{1,2,0:T(8,128)} %param.13) | copy-start | bytes 20740
  146.6 44.1 %copy-start.18 = (f32[2,54,16]{1,2,0:T(8,128)S(1)}, f32[2,54,16]{1,2,0:T(8,128)}, u32[]{:S(2)}) copy-start(f32[2,54,16]{1,2,0:T(8,128)} %param.14) | copy-start | bytes 20740
  146.9 91.1 %copy-start.19 = (f32[2,54,16]{1,2,0:T(8,128)S(1)}, f32[2,54,16]{1,2,0:T(8,128)}, u32[]{:S(2)}) copy-start(f32[2,54,16]{1,2,0:T(8,128)} %param.15) | copy-start | bytes 20740
  191.3 47.3 %copy-start.15 = (f32[2,54,16]{1,2,0:T(8,128)}, f32[2,54,16]{1,2,0:T(8,128)S(1)}, u32[]{:S(2)}) copy-start(f32[2,54,16]{1,2,0:T(8,128)S(1)} %get-tuple-element.16) | copy-start | bytes 20740

commit v5 on v3

--- a/solution.py
+++ b/solution.py
@@ -64,22 +64,27 @@
     return jnp.concatenate([take_window(padded, start, extent) for start in starts], axis=-1)
 
 
+def volume_conv(padded, kernel):
+    summed = lax.conv_general_dilated(
+        padded[None],
+        kernel,
+        (1, 1, 1),
+        "VALID",
+        dimension_numbers=("NDHWC", "DHWIO", "NDHWC"),
+        preferred_element_type=jnp.float32,
+    )
+    return summed[0] * unit_scale()
+
+
 def forward_conv(padded, weight_rows, extent):
     channels = weight_rows.shape[1]
-    columns = stacked_windows(padded, tap_corners(), extent)
-    summed = jnp.dot(columns, weight_rows, preferred_element_type=jnp.float32)
-    return (summed * unit_scale()).reshape(extent + (channels,))
+    return volume_conv(padded, weight_rows.reshape(3, 3, 3, channels, channels))
 
 
 def transposed_conv(padded_grad, weight_rows, extent):
     channels = weight_rows.shape[1]
-    starts = [(2 - a, 2 - b, 2 - c) for a, b, c in tap_corners()]
-    columns = stacked_windows(padded_grad, starts, extent)
-    flipped = weight_rows.reshape(TAPS, channels, channels).transpose(0, 2, 1)
-    summed = jnp.dot(
-        columns, flipped.reshape(TAPS * channels, channels), preferred_element_type=jnp.float32
-    )
-    return (summed * unit_scale()).reshape(extent + (channels,))
+    kernel = weight_rows.reshape(3, 3, 3, channels, channels)[::-1, ::-1, ::-1]
+    return volume_conv(padded_grad, kernel.transpose(0, 1, 2, 4, 3))
 
 
 def weight_grad(padded, grad_field, extent):

time: 233 us -> 232 us (level)
  local copies, waits for them, and re-layouts: 35.2 us -> 46.7 us
  other arithmetic: 11.4 us -> 6.61 us
  starting transfers between devices: 23.7 us -> 19.1 us
  blocking collectives: 150 us -> 146 us
    dot_general x0 -> x2, local copies, waits for them, and re-layouts: none -> 7.26 us  [weight_grad(): lax.dot_general(columns, grad_rows, (((0,), (0,)), ((), ())), preferred_e...]
    conv_general_dilated x0 -> x3, matrix products: none -> 6.98 us  [volume_conv(): lax.conv_general_dilated(padded[None], kernel, (1, 1, 1), 'VALID', dimens...]
    dot_general x2, matrix products: 7.62 us -> 2.23 us  [weight_grad(): lax.dot_general(columns, grad_rows, (((0,), (0,)), ((), ())), preferred_e...]
    ppermute x3, starting transfers between devices: 19.8 us -> 15 us  [with_halo(): lax.ppermute(tail, axis, [(i, (i + 1) % count) for i in range(ends)])]
    all_to_all x4, blocking collectives: 106 us -> 102 us  [exchange_and_sum(): moved = lax.all_to_all(blocks, axes, 0, 0, tiled=True)]
    concatenate x6 -> x4, other arithmetic: 4.04 us -> 0.33 us  [with_halo(): jnp.concatenate([lax.ppermute(tail, axis, [(i, (i + 1) % count) for i in...]
    another operation x2, local copies, waits for them, and re-layouts: 4.09 us -> 7.05 us  [local(): weight_grads = jnp.stack([wgrad_one, wgrad_two])]
    slice x2 -> x1, local copies, waits for them, and re-layouts: 0.01 us -> 2.77 us  [local(): pre_two = forward_conv(padded_act, weights[1], extent)]
  transfers between devices with their start and end apart: 6 -> 6, of which waited for: 2 -> 1; matrix products, arithmetic and copies ran while one was open for 1% -> 8% of each run, Pallas kernels for 0% -> 0%
where the time goes in v5:
time: 232 us; the launch traced here: 231 us
  blocking collectives  146 us (63%)
  local copies, waits for them, and re-layouts  46.7 us (20%)
  starting transfers between devices  19.1 us (8%)
  matrix products  9.21 us (4%)
  other arithmetic  6.61 us (3%)
    all_to_all x4, blocking collectives, exchange_and_sum(): moved = lax.all_to_all(blocks, axes, 0, 0, tiled=True)  102 us
    all_gather x1, blocking collectives, gather_rows(): gathered = lax.all_gather(fresh_weights, 'z', axis=0)  26.1 us
    unnamed x76, local copies, waits for them, and re-layouts  20 us
    all_gather x1, blocking collectives, gather_rows(): gathered = lax.all_gather(gathered, ('x_lo', 'core'), axis=0)  18.1 us
    ppermute x3, starting transfers between devices, with_halo(): lax.ppermute(tail, axis, [(i, (i + 1) % count) for i in range(ends)])  15 us
    dot_general x2, local copies, waits for them, and re-layouts, weight_grad(): lax.dot_general(columns, grad_rows, (((0,), (0,)), ((), ())), preferred_e...  7.26 us
    another operation x2, local copies, waits for them, and re-layouts  7.05 us
    conv_general_dilated x3, matrix products, volume_conv(): lax.conv_general_dilated(padded[None], kernel, (1, 1, 1), 'VALID', dimens...  6.98 us
  transfers between devices with their start and end apart: 6, of which 1 were waited for; matrix products, arithmetic and copies ran while one was open for 8% of the time, Pallas kernels for 0%

profile of v5, /device:TPU:1, one launch (start us, length us, event | category | flops | bytes accessed | tf_op | source)
XLA Modules:
  0.0 230.8 jit_solution(2411613332881008959)
XLA Ops:
  0.6 0.9 copy.451
  1.6 5.5 %collective-permute-start = (bf16[8,12,1,128]{3,1,2,0:T(8,128)(2,1)S(1)}, bf16[8,12,1,128]{3,1,2,0:T(8,128)(2,1)S(1)}, u32[]{:S(2)}, u32[]{:S(2)}) collective-permute-start(bf16[8,12,1,128]{3,1,2,0:T(8,128)(2,1)S(1)} %get-tuple-element.63), channel_id=1, source_target_pairs={{0,1},{1,2},{2,3},{3,4},{4,5},{5,6},{6,7},{8,9},{9,10},{10,11},{11... | collective-permute-start | bytes 73736 | tf_op jit(solution)/shard_map/ppermute | solution.py:27
  7.1 1.3 collective-permute-start.1
  8.4 2.8 %fusion.42 = (bf16[1,3456,128]{2,1,0:T(8,128)(2,1)}, bf16[1,3456,128]{2,1,0:T(8,128)(2,1)}) fusion(bf16[2,3456,128]{2,1,0:T(8,128)(2,1)} %param.11), kind=kLoop, calls=%fused_computation.132 | loop fusion | bytes 3538944 | tf_op jit(solution)/shard_map/slice | solution.py:120
  11.6 1.6 collective-permute-done.1
  13.4 0.6 fusion.45
  15.5 2.3 fusion.10
  18.0 4.0 %collective-permute-start.2 = (bf16[8,12,1,128]{3,0,2,1:T(8,128)(2,1)S(1)}, bf16[8,12,1,128]{3,0,2,1:T(8,128)(2,1)S(1)}, u32[]{:S(2)}, u32[]{:S(2)}) collective-permute-start(bf16[8,12,1,128]{3,0,2,1:T(8,128)(2,1)S(1)} %get-tuple-element.69), channel_id=1, source_target_pairs={{0,1},{1,2},{2,3},{3,4},{4,5},{5,6},{6,7},{8,9},{9,10},{10,11},{11... | collective-permute-start | bytes 73736 | tf_op jit(solution)/shard_map/ppermute | solution.py:27
  22.0 1.3 collective-permute-start.3
  24.2 2.8 %copy.374 = bf16[3456,384]{1,0:T(8,128)(2,1)} copy(bf16[3456,384]{0,1:T(8,128)(2,1)S(1)} %bitcast.147) | data formatting | bytes 5308416 | tf_op jit(solution)/shard_map/dot_general | solution.py:93
  27.0 2.8 %reshape.269 = bf16[16,2,2,54,384]{4,3,2,1,0:T(8,128)(2,1)S(1)} reshape(bf16[3456,384]{1,0:T(8,128)(2,1)} %copy.374) | data formatting | bytes 5308416 | tf_op jit(solution)/shard_map/reshape.33
  30.1 0.3 fusion.43
  30.6 0.6 copy-done.1
  31.2 2.4 %fusion.8 = f32[1,8,12,4,128]{4,0,3,2,1:T(1,128)S(1)} fusion(bf16[3,3,3,128,128]{4,3,2,1,0:T(8,128)(2,1)S(1)} %bitcast.153, bf16[1,10,14,6,128]{4,1,3,2,0:T(8,128)(2,1)S(1)} %fusion.58), kind=kOutput, calls=%fused_computation.19 | convolution fusion | flops 339738624 | bytes 1296384 | tf_op jit(solution)/shard_map/conv_general_dilated | solution.py:68
  33.9 5.5 %collective-permute-start.4 = (bf16[8,12,1,128]{3,0,2,1:T(8,128)(2,1)S(1)}, bf16[8,12,1,128]{3,0,2,1:T(8,128)(2,1)S(1)}, u32[]{:S(2)}, u32[]{:S(2)}) collective-permute-start(bf16[8,12,1,128]{3,0,2,1:T(8,128)(2,1)S(1)} %get-tuple-element.65), channel_id=1, source_target_pairs={{0,1},{1,2},{2,3},{3,4},{4,5},{5,6},{6,7},{8,9},{9,10},{10,11},{11... | collective-permute-start | bytes 73736 | tf_op jit(solution)/shard_map/ppermute | solution.py:27
  39.4 1.5 collective-permute-start.5
  40.9 0.7 constant_dynamic-update-slice_fusion.53
  42.2 0.7 constant_dynamic-update-slice_fusion.52
  42.9 0.7 constant_dynamic-update-slice_fusion.51
  43.5 0.7 constant_dynamic-update-slice_fusion.50
  44.2 0.7 constant_dynamic-update-slice_fusion.49
  44.9 0.6 constant_dynamic-update-slice_fusion.48
  45.5 0.7 constant_dynamic-update-slice_fusion.47
  46.2 0.7 constant_dynamic-update-slice_fusion.46
  46.9 0.7 constant_dynamic-update-slice_fusion.45
  47.5 0.7 constant_dynamic-update-slice_fusion.44
  48.2 0.7 constant_dynamic-update-slice_fusion.43
  48.9 0.7 constant_dynamic-update-slice_fusion.42
  49.6 0.7 constant_dynamic-update-slice_fusion.41
  51.1 2.3 %fusion.6 = f32[1,8,12,4,128]{4,0,3,2,1:T(1,128)S(1)} fusion(bf16[3,3,3,128,128]{4,3,2,1,0:T(8,128)(2,1)S(1)} %bitcast.154, bf16[1,10,14,6,128]{4,1,3,2,0:T(8,128)(2,1)S(1)} %fusion.12), kind=kOutput, calls=%fused_computation.17 | convolution fusion | flops 339738624 | bytes 1296384 | tf_op jit(solution)/shard_map/conv_general_dilated | solution.py:68
  53.8 0.8 constant_dynamic-update-slice_fusion.40
  54.5 0.7 constant_dynamic-update-slice_fusion.39
  55.2 0.7 constant_dynamic-update-slice_fusion.38
  55.9 0.7 constant_dynamic-update-slice_fusion.37
  56.5 0.7 constant_dynamic-update-slice_fusion.36
  57.2 0.7 constant_dynamic-update-slice_fusion.35
  57.9 0.7 constant_dynamic-update-slice_fusion.34
  58.5 0.7 constant_dynamic-update-slice_fusion.33
  59.2 0.7 constant_dynamic-update-slice_fusion.32
  59.9 0.7 constant_dynamic-update-slice_fusion.31
  60.5 0.7 constant_dynamic-update-slice_fusion.30
  61.2 0.6 constant_dynamic-update-slice_fusion.29
  61.8 0.7 constant_dynamic-update-slice_fusion.28
  62.5 0.7 constant_dynamic-update-slice_fusion.27
  63.2 4.4 %copy.413 = bf16[3456,384]{1,0:T(8,128)(2,1)} copy(bf16[3456,384]{0,1:T(8,128)(2,1)} %bitcast.69) | data formatting | bytes 5308416 | tf_op jit(solution)/shard_map/dot_general | solution.py:93
  67.6 4.3 %reshape.296 = bf16[16,2,2,54,384]{4,3,2,1,0:T(8,128)(2,1)} reshape(bf16[3456,384]{1,0:T(8,128)(2,1)} %copy.413) | data formatting | bytes 5308416 | tf_op jit(solution)/shard_map/reshape.37
  71.9 1.1 convolution_bitcast_fusion.1
  73.0 0.7 copy-done
  73.6 1.1 convolution_bitcast_fusion
  75.0 2.1 copy.416
  77.1 9.9 %all_to_all.20 = f32[2,2,16,2,54,128]{5,2,4,3,1,0:T(8,128)S(1)} all-to-all(f32[2,2,16,2,54,128]{5,2,4,3,1,0:T(8,128)S(1)} %copy.416), channel_id=1, replica_groups=mesh['z'=16,'x_lo'=2,'core'=2,'y'=4,'x_hi'=2] {'core'}, dimensions={0} | all-to-all | bytes 7077888 | tf_op jit(solution)/shard_map/all_to_all | solution.py:145
  87.0 1.7 reduce_sum.36
  88.6 24.8 %all_to_all.21 = f32[2,16,2,54,128]{4,1,3,2,0:T(8,128)S(1)} all-to-all(f32[2,16,2,54,128]{4,1,3,2,0:T(8,128)} %reduce_sum.36), channel_id=1, replica_groups=mesh['z'=16,'x_lo'=2,'core'=2,'y'=4,'x_hi'=2] {'x_lo'}, dimensions={0} | all-to-all | bytes 3538944 | tf_op jit(solution)/shard_map/all_to_all | solution.py:145
  113.6 0.7 copy.419
  114.3 52.8 %all_to_all.22 = f32[16,2,54,128]{3,1,2,0:T(2,128)S(1)} all-to-all(f32[16,2,54,128]{3,1,2,0:T(2,128)S(1)} %copy.419), channel_id=1, replica_groups=mesh['z'=16,'x_lo'=2,'core'=2,'y'=4,'x_hi'=2] {'z'}, dimensions={0} | all-to-all | bytes 1769472 | tf_op jit(solution)/shard_map/all_to_all | solution.py:145
  167.7 14.2 %all_to_all.23 = f32[8,1,1728]{2,1,0:T(1,128)S(1)} all-to-all(f32[8,1,1728]{2,1,0:T(1,128)S(1)} %reshape.306), channel_id=1, replica_groups=mesh['z'=16,'x_lo'=2,'core'=2,'y'=4,'x_hi'=2] {'y','x_hi'}, dimensions={0} | all-to-all | bytes 110592 | tf_op jit(solution)/shard_map/all_to_all | solution.py:145
  181.9 0.5 broadcast.246
  182.5 0.8 reduce
  183.5 0.6 fusion.41
  184.1 26.1 %all-gather = bf16[32,54,16]{1,2,0:T(8,128)(2,1)S(1)} all-gather(bf16[2,54,16]{1,2,0:T(8,128)(2,1)S(1)} %get-tuple-element.5), channel_id=2, replica_groups=mesh['z'=16,'x_lo'=2,'core'=2,'y'=4,'x_hi'=2] {'z'}, dimensions={0}, use_global_device_ids=true | all-gather | bytes 58752 | tf_op jit(solution)/shard_map/all_gather | solution.py:166
  210.2 18.1 %all-gather.1 = bf16[64,2,54,16]{2,3,1,0:T(8,128)(2,1)S(1)} all-gather(bf16[16,2,54,16]{2,3,1,0:T(8,128)(2,1)S(1)} %bitcast.157), channel_id=3, replica_groups=mesh['z'=16,'x_lo'=2,'core'=2,'y'=4,'x_hi'=2] {'x_lo','core'}, dimensions={0}, use_global_device_ids=true | all-gather | bytes 276480 | tf_op jit(solution)/shard_map/all_gather | solution.py:167
  228.3 0.5 copy.422
  228.9 1.4 reshape.299
  230.2 0.6 multiply_add_fusion
  (137 shorter events, 6.3 us)
Async XLA Ops:
  0.6 10.5 %copy-start.6 = (s32[1,8,12,4]{2,3,1,0:T(4,128)S(1)}, s32[1,8,12,4]{2,3,1,0:T(4,128)}, u32[]{:S(2)}) copy-start(s32[1,8,12,4]{2,3,1,0:T(4,128)} %param.9) | copy-start | bytes 4612
  1.6 10.0 %collective-permute-start = (bf16[8,12,1,128]{3,1,2,0:T(8,128)(2,1)S(1)}, bf16[8,12,1,128]{3,1,2,0:T(8,128)(2,1)S(1)}, u32[]{:S(2)}, u32[]{:S(2)}) collective-permute-start(bf16[8,12,1,128]{3,1,2,0:T(8,128)(2,1)S(1)} %get-tuple-element.63), channel_id=1, source_target_pairs={{0,1},{1,2},{2,3},{3,4},{4,5},{5,6},{6,7},{8,9},{9,10},{10,11},{11... | collective-permute-start | bytes 73736 | tf_op jit(solution)/shard_map/ppermute | solution.py:27
  7.1 6.2 %collective-permute-start.1 = (bf16[8,12,1,128]{3,1,2,0:T(8,128)(2,1)S(1)}, bf16[8,12,1,128]{3,1,2,0:T(8,128)(2,1)S(1)}, u32[]{:S(2)}, u32[]{:S(2)}) collective-permute-start(bf16[8,12,1,128]{3,1,2,0:T(8,128)(2,1)S(1)} %get-tuple-element.64), channel_id=1, source_target_pairs={{1,0},{2,1},{3,2},{4,3},{5,4},{6,5},{7,6},{9,8},{10,9},{11,10},{12... | collective-permute-start | bytes 73736 | tf_op jit(solution)/shard_map/ppermute | solution.py:29
  14.4 1.2 copy-start.2
  17.8 5.9 %copy-start.3 = (bf16[1,8,12,4,128]{4,3,2,1,0:T(4,128)(2,1)S(1)}, bf16[1,8,12,4,128]{4,3,2,1,0:T(4,128)(2,1)}, u32[]{:S(2)}) copy-start(bf16[1,8,12,4,128]{4,3,2,1,0:T(4,128)(2,1)} %param.8) | copy-start | bytes 294916
  18.0 11.9 %collective-permute-start.2 = (bf16[8,12,1,128]{3,0,2,1:T(8,128)(2,1)S(1)}, bf16[8,12,1,128]{3,0,2,1:T(8,128)(2,1)S(1)}, u32[]{:S(2)}, u32[]{:S(2)}) collective-permute-start(bf16[8,12,1,128]{3,0,2,1:T(8,128)(2,1)S(1)} %get-tuple-element.69), channel_id=1, source_target_pairs={{0,1},{1,2},{2,3},{3,4},{4,5},{5,6},{6,7},{8,9},{9,10},{10,11},{11... | collective-permute-start | bytes 73736 | tf_op jit(solution)/shard_map/ppermute | solution.py:27
  22.0 7.8 %collective-permute-start.3 = (bf16[8,12,1,128]{3,0,2,1:T(8,128)(2,1)S(1)}, bf16[8,12,1,128]{3,0,2,1:T(8,128)(2,1)S(1)}, u32[]{:S(2)}, u32[]{:S(2)}) collective-permute-start(bf16[8,12,1,128]{3,0,2,1:T(8,128)(2,1)S(1)} %get-tuple-element.70), channel_id=1, source_target_pairs={{1,0},{2,1},{3,2},{4,3},{5,4},{6,5},{7,6},{9,8},{10,9},{11,10},{12... | collective-permute-start | bytes 73736 | tf_op jit(solution)/shard_map/ppermute | solution.py:29
  30.0 1.2 copy-start.1
  30.6 3.0 %copy-start.4 = (bf16[1,8,12,4,128]{4,3,2,1,0:T(4,128)(2,1)S(1)}, bf16[1,8,12,4,128]{4,3,2,1,0:T(4,128)(2,1)}, u32[]{:S(2)}) copy-start(bf16[1,8,12,4,128]{4,3,2,1,0:T(4,128)(2,1)} %param.10) | copy-start | bytes 294916
  33.9 17.0 %collective-permute-start.4 = (bf16[8,12,1,128]{3,0,2,1:T(8,128)(2,1)S(1)}, bf16[8,12,1,128]{3,0,2,1:T(8,128)(2,1)S(1)}, u32[]{:S(2)}, u32[]{:S(2)}) collective-permute-start(bf16[8,12,1,128]{3,0,2,1:T(8,128)(2,1)S(1)} %get-tuple-element.65), channel_id=1, source_target_pairs={{0,1},{1,2},{2,3},{3,4},{4,5},{5,6},{6,7},{8,9},{9,10},{10,11},{11... | collective-permute-start | bytes 73736 | tf_op jit(solution)/shard_map/ppermute | solution.py:27
  39.4 11.5 %collective-permute-start.5 = (bf16[8,12,1,128]{3,0,2,1:T(8,128)(2,1)S(1)}, bf16[8,12,1,128]{3,0,2,1:T(8,128)(2,1)S(1)}, u32[]{:S(2)}, u32[]{:S(2)}) collective-permute-start(bf16[8,12,1,128]{3,0,2,1:T(8,128)(2,1)S(1)} %get-tuple-element.66), channel_id=1, source_target_pairs={{1,0},{2,1},{3,2},{4,3},{5,4},{6,5},{7,6},{9,8},{10,9},{11,10},{12... | collective-permute-start | bytes 73736 | tf_op jit(solution)/shard_map/ppermute | solution.py:29
  71.9 1.8 copy-start
  113.6 69.9 %copy-start.7 = (f32[2,54,16]{1,2,0:T(8,128)S(1)}, f32[2,54,16]{1,2,0:T(8,128)}, u32[]{:S(2)}) copy-start(f32[2,54,16]{1,2,0:T(8,128)} %param.12) | copy-start | bytes 20740
  113.6 69.9 %copy-start.8 = (f32[2,54,16]{1,2,0:T(8,128)S(1)}, f32[2,54,16]{1,2,0:T(8,128)}, u32[]{:S(2)}) copy-start(f32[2,54,16]{1,2,0:T(8,128)} %param.13) | copy-start | bytes 20740
  113.6 69.9 %copy-start.9 = (f32[2,54,16]{1,2,0:T(8,128)S(1)}, f32[2,54,16]{1,2,0:T(8,128)}, u32[]{:S(2)}) copy-start(f32[2,54,16]{1,2,0:T(8,128)} %param.14) | copy-start | bytes 20740
  167.1 63.1 %copy-start.10 = (f32[2,54,16]{1,2,0:T(8,128)S(1)}, f32[2,54,16]{1,2,0:T(8,128)}, u32[]{:S(2)}) copy-start(f32[2,54,16]{1,2,0:T(8,128)} %param.15) | copy-start | bytes 20740
  184.1 46.7 %copy-start.5 = (f32[2,54,16]{1,2,0:T(8,128)}, f32[2,54,16]{1,2,0:T(8,128)S(1)}, u32[]{:S(2)}) copy-start(f32[2,54,16]{1,2,0:T(8,128)S(1)} %get-tuple-element.6) | copy-start | bytes 20740

commit v6 on v5

--- a/solution.py
+++ b/solution.py
@@ -123,11 +123,11 @@
     )
     rim_grad = with_halo(grad_two, ((COLUMN_AXES, 2),), 1)
     padded_grad = jnp.pad(rim_grad, plane_pad)
-    wgrad_two = weight_grad(padded_act, grad_two, extent)
+    wgrad_two = first_row_stages(weight_grad(padded_act, grad_two, extent), master.shape[1])
     back_one = transposed_conv(padded_grad, weights[1], extent)
     grad_one = (back_one * occupied * silu_slope(pre_one)).astype(jnp.bfloat16)
-    wgrad_one = weight_grad(padded_in, grad_one, extent)
-    weight_grads = jnp.stack([wgrad_one, wgrad_two])
+    wgrad_one = first_row_stages(weight_grad(padded_in, grad_one, extent), master.shape[1])
+    weight_grads = jnp.stack([wgrad_one, wgrad_two], axis=1)
     gradient = scatter_rows_and_columns(weight_grads, master.shape)
     new_master, new_moment, new_second, new_teacher = adam_update(
         master, moment, second, teacher, gradient
@@ -146,16 +146,18 @@
     return moved.sum(axis=0)
 
 
+def first_row_stages(weight_rows, rows):
+    lanes = weight_rows.shape[-1]
+    z, x_lo, core = (lax.axis_size(name) for name in ROW_AXES)
+    blocks = weight_rows.reshape(z, x_lo, core, rows, lanes).transpose(2, 1, 0, 3, 4)
+    blocks = exchange_and_sum(blocks, "core")
+    return exchange_and_sum(blocks, "x_lo")
+
+
 def scatter_rows_and_columns(weight_grads, own_shape):
     layers, rows, cols = own_shape
-    lanes = weight_grads.shape[-1]
-    z, x_lo, core = (lax.axis_size(name) for name in ROW_AXES)
     y, x_hi = (lax.axis_size(name) for name in COLUMN_AXES)
-    blocks = weight_grads.reshape(layers, z, x_lo, core, rows, lanes)
-    blocks = blocks.transpose(3, 2, 1, 0, 4, 5)
-    blocks = exchange_and_sum(blocks, "core")
-    blocks = exchange_and_sum(blocks, "x_lo")
-    blocks = exchange_and_sum(blocks, "z")
+    blocks = exchange_and_sum(weight_grads, "z")
     blocks = blocks.reshape(layers, rows, y * x_hi, cols).transpose(2, 0, 1, 3)
     blocks = exchange_and_sum(blocks, COLUMN_AXES)
     return blocks * unit_scale()

time: 232 us -> 247 us (1.065)
  blocking collectives: 146 us -> 111 us
  waiting for transfers between devices: 1.61 us -> 22.9 us
  starting transfers between devices: 19.1 us -> 39 us
  local copies, waits for them, and re-layouts: 46.7 us -> 54.2 us
    all_to_all x4 -> x2, blocking collectives: 102 us -> 67.3 us  [exchange_and_sum(): moved = lax.all_to_all(blocks, axes, 0, 0, tiled=True)]
    all_to_all x0 -> x4, waiting for transfers between devices: none -> 21.9 us  [exchange_and_sum(): moved = lax.all_to_all(blocks, axes, 0, 0, tiled=True)]
    all_to_all x0 -> x4, starting transfers between devices: none -> 19.4 us  [exchange_and_sum(): moved = lax.all_to_all(blocks, axes, 0, 0, tiled=True)]
    another operation x2 -> x1, local copies, waits for them, and re-layouts: 7.05 us -> 0.68 us  [local(): weight_grads = jnp.stack([wgrad_one, wgrad_two], axis=1)]
    slice x56, local copies, waits for them, and re-layouts: 3.09 us -> 8.78 us  [take_window(): padded[start[0]:start[0] + extent[0], start[1]:start[1] + extent[1], star...]
    dot_general x2 -> x4, local copies, waits for them, and re-layouts: 7.26 us -> 12.9 us  [weight_grad(): lax.dot_general(columns, grad_rows, (((0,), (0,)), ((), ())), preferred_e...]
    transpose x1 -> x2, local copies, waits for them, and re-layouts: 2.05 us -> 4.6 us  [first_row_stages(): weight_rows.reshape(z, x_lo, core, rows, lanes).transpose(2, 1, 0, 3, 4)]
    unnamed x76 -> x96, local copies, waits for them, and re-layouts: 20 us -> 19.4 us
  transfers between devices with their start and end apart: 6 -> 10, of which waited for: 1 -> 3; matrix products, arithmetic and copies ran while one was open for 8% -> 20% of each run, Pallas kernels for 0% -> 0%
where the time goes in v6:
time: 247 us; the launch traced here: 246 us
  blocking collectives  111 us (45%)
  local copies, waits for them, and re-layouts  54.2 us (22%)
  starting transfers between devices  39 us (16%)
  waiting for transfers between devices  22.9 us (9%)
  matrix products  9.21 us (4%)
  other arithmetic  8.44 us (3%)
    all_to_all x2, blocking collectives, exchange_and_sum(): moved = lax.all_to_all(blocks, axes, 0, 0, tiled=True)  67.3 us
    all_gather x1, blocking collectives, gather_rows(): gathered = lax.all_gather(fresh_weights, 'z', axis=0)  25.5 us
    all_to_all x4, waiting for transfers between devices, exchange_and_sum(): moved = lax.all_to_all(blocks, axes, 0, 0, tiled=True)  21.9 us
    all_to_all x4, starting transfers between devices, exchange_and_sum(): moved = lax.all_to_all(blocks, axes, 0, 0, tiled=True)  19.4 us
    unnamed x96, local copies, waits for them, and re-layouts  19.4 us
    all_gather x1, blocking collectives, gather_rows(): gathered = lax.all_gather(gathered, ('x_lo', 'core'), axis=0)  18 us
    ppermute x3, starting transfers between devices, with_halo(): lax.ppermute(tail, axis, [(i, (i + 1) % count) for i in range(ends)])  15.5 us
    dot_general x4, local copies, waits for them, and re-layouts, weight_grad(): lax.dot_general(columns, grad_rows, (((0,), (0,)), ((), ())), preferred_e...  12.9 us
  transfers between devices with their start and end apart: 10, of which 3 were waited for; matrix products, arithmetic and copies ran while one was open for 20% of the time, Pallas kernels for 0%

profile of v6, /device:TPU:1, one launch (start us, length us, event | category | flops | bytes accessed | tf_op | source)
XLA Modules:
  0.0 246.3 jit_solution(9072767084712139806)
XLA Ops:
  0.6 0.9 copy.544
  1.6 5.5 %collective-permute-start = (bf16[8,12,1,128]{3,1,2,0:T(8,128)(2,1)S(1)}, bf16[8,12,1,128]{3,1,2,0:T(8,128)(2,1)S(1)}, u32[]{:S(2)}, u32[]{:S(2)}) collective-permute-start(bf16[8,12,1,128]{3,1,2,0:T(8,128)(2,1)S(1)} %get-tuple-element.63), channel_id=1, source_target_pairs={{0,1},{1,2},{2,3},{3,4},{4,5},{5,6},{6,7},{8,9},{9,10},{10,11},{11... | collective-permute-start | bytes 73736 | tf_op jit(solution)/shard_map/ppermute | solution.py:27
  7.1 1.3 collective-permute-start.1
  8.4 2.8 %fusion.42 = (bf16[1,3456,128]{2,1,0:T(8,128)(2,1)}, bf16[1,3456,128]{2,1,0:T(8,128)(2,1)}) fusion(bf16[2,3456,128]{2,1,0:T(8,128)(2,1)} %param.11), kind=kLoop, calls=%fused_computation.132 | loop fusion | bytes 3538944 | tf_op jit(solution)/shard_map/slice | solution.py:120
  11.3 0.7 copy.471
  12.2 1.0 collective-permute-done.1
  15.5 2.3 fusion.10
  18.0 4.5 %collective-permute-start.2 = (bf16[8,12,1,128]{3,0,2,1:T(8,128)(2,1)S(1)}, bf16[8,12,1,128]{3,0,2,1:T(8,128)(2,1)S(1)}, u32[]{:S(2)}, u32[]{:S(2)}) collective-permute-start(bf16[8,12,1,128]{3,0,2,1:T(8,128)(2,1)S(1)} %get-tuple-element.69), channel_id=1, source_target_pairs={{0,1},{1,2},{2,3},{3,4},{4,5},{5,6},{6,7},{8,9},{9,10},{10,11},{11... | collective-permute-start | bytes 73736 | tf_op jit(solution)/shard_map/ppermute | solution.py:27
  22.5 1.3 collective-permute-start.3
  24.7 2.9 %copy.463 = bf16[3456,384]{1,0:T(8,128)(2,1)} copy(bf16[3456,384]{0,1:T(8,128)(2,1)S(1)} %bitcast.147) | data formatting | bytes 5308416 | tf_op jit(solution)/shard_map/dot_general | solution.py:93
  27.5 2.8 %dot_general.15 = bf16[16,2,2,54,384]{4,3,2,1,0:T(8,128)(2,1)S(1)} reshape(bf16[3456,384]{1,0:T(8,128)(2,1)} %copy.463) | data formatting | bytes 5308416 | tf_op jit(solution)/shard_map/dot_general | solution.py:93
  31.7 2.4 fusion.8
  34.4 5.5 %collective-permute-start.4 = (bf16[8,12,1,128]{3,0,2,1:T(8,128)(2,1)S(1)}, bf16[8,12,1,128]{3,0,2,1:T(8,128)(2,1)S(1)}, u32[]{:S(2)}, u32[]{:S(2)}) collective-permute-start(bf16[8,12,1,128]{3,0,2,1:T(8,128)(2,1)S(1)} %get-tuple-element.65), channel_id=1, source_target_pairs={{0,1},{1,2},{2,3},{3,4},{4,5},{5,6},{6,7},{8,9},{9,10},{10,11},{11... | collective-permute-start | bytes 73736 | tf_op jit(solution)/shard_map/ppermute | solution.py:27
  39.9 1.5 collective-permute-start.5
  41.4 0.7 constant_dynamic-update-slice_fusion.53
  43.4 0.7 constant_dynamic-update-slice_fusion.51
  44.7 0.7 constant_dynamic-update-slice_fusion.49
  45.4 0.7 constant_dynamic-update-slice_fusion.48
  46.0 0.7 constant_dynamic-update-slice_fusion.47
  46.7 0.7 constant_dynamic-update-slice_fusion.46
  48.7 0.7 constant_dynamic-update-slice_fusion.43
  49.3 0.7 constant_dynamic-update-slice_fusion.42
  50.0 0.7 constant_dynamic-update-slice_fusion.41
  50.7 0.7 copy.492
  51.3 0.7 copy.493
  52.7 0.7 copy.495
  53.3 0.7 copy.496
  54.0 0.7 copy.497
  54.7 0.7 copy.498
  55.4 0.7 copy.499
  56.0 0.7 copy.500
  56.9 0.7 copy.507
  57.7 2.3 fusion.6
  60.4 1.1 convolution_bitcast_fusion.1
  61.5 2.3 copy.474
  63.9 8.6 %all-to-all-start = ((f32[2,2,16,54,128]{4,2,3,1,0:T(8,128)}), f32[2,2,16,54,128]{4,2,3,1,0:T(8,128)}, u32[]{:S(2)}, u32[]{:S(2)}) async-start(f32[2,2,16,54,128]{4,2,3,1,0:T(8,128)} %copy.474), calls=%async_computation | async-start | bytes 3538944 | tf_op jit(solution)/shard_map/all_to_all | solution.py:145
  72.5 0.8 constant_dynamic-update-slice_fusion.40
  74.0 0.7 constant_dynamic-update-slice_fusion.38
  74.6 0.7 constant_dynamic-update-slice_fusion.37
  75.3 0.7 constant_dynamic-update-slice_fusion.36
  76.0 0.7 constant_dynamic-update-slice_fusion.35
  76.7 0.7 constant_dynamic-update-slice_fusion.34
  77.4 0.7 constant_dynamic-update-slice_fusion.33
  78.0 0.7 constant_dynamic-update-slice_fusion.32
  78.7 0.7 constant_dynamic-update-slice_fusion.31
  81.4 0.7 constant_dynamic-update-slice_fusion.27
  82.0 4.4 %copy.505 = bf16[3456,384]{1,0:T(8,128)(2,1)} copy(bf16[3456,384]{0,1:T(8,128)(2,1)} %bitcast.70) | data formatting | bytes 5308416 | tf_op jit(solution)/shard_map/dot_general | solution.py:93
  86.5 2.8 %dot_general.18 = bf16[16,2,2,54,384]{4,3,2,1,0:T(8,128)(2,1)S(1)} reshape(bf16[3456,384]{1,0:T(8,128)(2,1)} %copy.505) | data formatting | bytes 5308416 | tf_op jit(solution)/shard_map/dot_general | solution.py:93
  89.3 1.1 convolution_bitcast_fusion
  90.5 2.3 copy.508
  92.7 3.7 %all-to-all-start.2 = ((f32[2,2,16,54,128]{4,2,3,1,0:T(8,128)}), f32[2,2,16,54,128]{4,2,3,1,0:T(8,128)S(1)}, u32[]{:S(2)}, u32[]{:S(2)}) async-start(f32[2,2,16,54,128]{4,2,3,1,0:T(8,128)} %copy.508), calls=%async_computation.2 | async-start | bytes 3538944 | tf_op jit(solution)/shard_map/all_to_all | solution.py:145
  96.5 2.6 %reduce_sum.54 = f32[2,16,54,128]{3,1,2,0:T(8,128)} reduce(f32[2,2,16,54,128]{4,2,3,1,0:T(8,128)} %all-to-all-done, f32[]{:T(128)} %constant.8.clone.1), dimensions={0}, to_apply=%region_0.1 | reduce | flops 221184 | bytes 2654212 | tf_op jit(solution)/shard_map/reduce_sum | solution.py:146
  99.1 3.6 %all-to-all-start.1 = ((f32[2,16,54,128]{3,1,2,0:T(8,128)}), f32[2,16,54,128]{3,1,2,0:T(8,128)S(1)}, u32[]{:S(2)}, u32[]{:S(2)}) async-start(f32[2,16,54,128]{3,1,2,0:T(8,128)} %reduce_sum.54), calls=%async_computation.1 | async-start | bytes 1769472 | tf_op jit(solution)/shard_map/all_to_all | solution.py:145
  102.6 1.1 reduce_sum.56
  103.8 10.8 %all-to-all-done.1 = f32[2,16,54,128]{3,1,2,0:T(8,128)S(1)} async-done(((f32[2,16,54,128]{3,1,2,0:T(8,128)}), f32[2,16,54,128]{3,1,2,0:T(8,128)S(1)}, u32[]{:S(2)}, u32[]{:S(2)}) %all-to-all-start.1) | async-done | bytes 884768 | tf_op jit(solution)/shard_map/all_to_all | solution.py:145
  114.6 3.6 %all-to-all-start.3 = ((f32[2,16,54,128]{3,1,2,0:T(8,128)}), f32[2,16,54,128]{3,1,2,0:T(8,128)S(1)}, u32[]{:S(2)}, u32[]{:S(2)}) async-start(f32[2,16,54,128]{3,1,2,0:T(8,128)} %reduce_sum.56), calls=%async_computation.3 | async-start | bytes 1769472 | tf_op jit(solution)/shard_map/all_to_all | solution.py:145
  118.2 11.0 %all-to-all-done.3 = f32[2,16,54,128]{3,1,2,0:T(8,128)S(1)} async-done(((f32[2,16,54,128]{3,1,2,0:T(8,128)}), f32[2,16,54,128]{3,1,2,0:T(8,128)S(1)}, u32[]{:S(2)}, u32[]{:S(2)}) %all-to-all-start.3) | async-done | bytes 884768 | tf_op jit(solution)/shard_map/all_to_all | solution.py:145
  129.4 0.7 copy.511
  130.1 50.9 %all_to_all.30 = f32[16,2,54,128]{3,1,2,0:T(2,128)S(1)} all-to-all(f32[16,2,54,128]{3,1,2,0:T(2,128)S(1)} %copy.511), channel_id=1, replica_groups=mesh['z'=16,'x_lo'=2,'core'=2,'y'=4,'x_hi'=2] {'z'}, dimensions={0} | all-to-all | bytes 1769472 | tf_op jit(solution)/shard_map/all_to_all | solution.py:145
  181.6 16.4 %all_to_all.31 = f32[8,1,1728]{2,1,0:T(1,128)S(1)} all-to-all(f32[8,1,1728]{2,1,0:T(1,128)S(1)} %reshape.287), channel_id=1, replica_groups=mesh['z'=16,'x_lo'=2,'core'=2,'y'=4,'x_hi'=2] {'y','x_hi'}, dimensions={0} | all-to-all | bytes 110592 | tf_op jit(solution)/shard_map/all_to_all | solution.py:145
  198.5 0.8 reduce
  200.2 25.5 %all-gather = bf16[32,54,16]{1,2,0:T(8,128)(2,1)S(1)} all-gather(bf16[2,54,16]{1,2,0:T(8,128)(2,1)S(1)} %get-tuple-element.5), channel_id=2, replica_groups=mesh['z'=16,'x_lo'=2,'core'=2,'y'=4,'x_hi'=2] {'z'}, dimensions={0}, use_global_device_ids=true | all-gather | bytes 58752 | tf_op jit(solution)/shard_map/all_gather | solution.py:168
  225.7 18.0 %all-gather.1 = bf16[64,2,54,16]{2,3,1,0:T(8,128)(2,1)S(1)} all-gather(bf16[16,2,54,16]{2,3,1,0:T(8,128)(2,1)S(1)} %bitcast.159), channel_id=3, replica_groups=mesh['z'=16,'x_lo'=2,'core'=2,'y'=4,'x_hi'=2] {'x_lo','core'}, dimensions={0}, use_global_device_ids=true | all-gather | bytes 276480 | tf_op jit(solution)/shard_map/all_gather | solution.py:169
  244.3 1.4 reshape.280
  (166 shorter events, 15.2 us)
Async XLA Ops:
  0.6 10.5 %copy-start.16 = (s32[1,8,12,4]{2,3,1,0:T(4,128)S(1)}, s32[1,8,12,4]{2,3,1,0:T(4,128)}, u32[]{:S(2)}) copy-start(s32[1,8,12,4]{2,3,1,0:T(4,128)} %param.9) | copy-start | bytes 4612
  1.6 10.7 %collective-permute-start = (bf16[8,12,1,128]{3,1,2,0:T(8,128)(2,1)S(1)}, bf16[8,12,1,128]{3,1,2,0:T(8,128)(2,1)S(1)}, u32[]{:S(2)}, u32[]{:S(2)}) collective-permute-start(bf16[8,12,1,128]{3,1,2,0:T(8,128)(2,1)S(1)} %get-tuple-element.63), channel_id=1, source_target_pairs={{0,1},{1,2},{2,3},{3,4},{4,5},{5,6},{6,7},{8,9},{9,10},{10,11},{11... | collective-permute-start | bytes 73736 | tf_op jit(solution)/shard_map/ppermute | solution.py:27
  7.1 6.2 %collective-permute-start.1 = (bf16[8,12,1,128]{3,1,2,0:T(8,128)(2,1)S(1)}, bf16[8,12,1,128]{3,1,2,0:T(8,128)(2,1)S(1)}, u32[]{:S(2)}, u32[]{:S(2)}) collective-permute-start(bf16[8,12,1,128]{3,1,2,0:T(8,128)(2,1)S(1)} %get-tuple-element.64), channel_id=1, source_target_pairs={{1,0},{2,1},{3,2},{4,3},{5,4},{6,5},{7,6},{9,8},{10,9},{11,10},{12... | collective-permute-start | bytes 73736 | tf_op jit(solution)/shard_map/ppermute | solution.py:29
  14.4 1.2 copy-start.1
  17.8 6.4 %copy-start.2 = (bf16[1,8,12,4,128]{4,3,2,1,0:T(4,128)(2,1)S(1)}, bf16[1,8,12,4,128]{4,3,2,1,0:T(4,128)(2,1)}, u32[]{:S(2)}) copy-start(bf16[1,8,12,4,128]{4,3,2,1,0:T(4,128)(2,1)} %param.8) | copy-start | bytes 294916
  18.0 12.4 %collective-permute-start.2 = (bf16[8,12,1,128]{3,0,2,1:T(8,128)(2,1)S(1)}, bf16[8,12,1,128]{3,0,2,1:T(8,128)(2,1)S(1)}, u32[]{:S(2)}, u32[]{:S(2)}) collective-permute-start(bf16[8,12,1,128]{3,0,2,1:T(8,128)(2,1)S(1)} %get-tuple-element.69), channel_id=1, source_target_pairs={{0,1},{1,2},{2,3},{3,4},{4,5},{5,6},{6,7},{8,9},{9,10},{10,11},{11... | collective-permute-start | bytes 73736 | tf_op jit(solution)/shard_map/ppermute | solution.py:27
  22.5 7.8 %collective-permute-start.3 = (bf16[8,12,1,128]{3,0,2,1:T(8,128)(2,1)S(1)}, bf16[8,12,1,128]{3,0,2,1:T(8,128)(2,1)S(1)}, u32[]{:S(2)}, u32[]{:S(2)}) collective-permute-start(bf16[8,12,1,128]{3,0,2,1:T(8,128)(2,1)S(1)} %get-tuple-element.70), channel_id=1, source_target_pairs={{1,0},{2,1},{3,2},{4,3},{5,4},{6,5},{7,6},{9,8},{10,9},{11,10},{12... | collective-permute-start | bytes 73736 | tf_op jit(solution)/shard_map/ppermute | solution.py:29
  30.5 1.2 copy-start
  31.1 3.0 %copy-start.12 = (bf16[1,8,12,4,128]{4,3,2,1,0:T(4,128)(2,1)S(1)}, bf16[1,8,12,4,128]{4,3,2,1,0:T(4,128)(2,1)}, u32[]{:S(2)}) copy-start(bf16[1,8,12,4,128]{4,3,2,1,0:T(4,128)(2,1)} %param.10) | copy-start | bytes 294916
  34.4 23.2 %collective-permute-start.4 = (bf16[8,12,1,128]{3,0,2,1:T(8,128)(2,1)S(1)}, bf16[8,12,1,128]{3,0,2,1:T(8,128)(2,1)S(1)}, u32[]{:S(2)}, u32[]{:S(2)}) collective-permute-start(bf16[8,12,1,128]{3,0,2,1:T(8,128)(2,1)S(1)} %get-tuple-element.65), channel_id=1, source_target_pairs={{0,1},{1,2},{2,3},{3,4},{4,5},{5,6},{6,7},{8,9},{9,10},{10,11},{11... | collective-permute-start | bytes 73736 | tf_op jit(solution)/shard_map/ppermute | solution.py:27
  39.9 17.7 %collective-permute-start.5 = (bf16[8,12,1,128]{3,0,2,1:T(8,128)(2,1)S(1)}, bf16[8,12,1,128]{3,0,2,1:T(8,128)(2,1)S(1)}, u32[]{:S(2)}, u32[]{:S(2)}) collective-permute-start(bf16[8,12,1,128]{3,0,2,1:T(8,128)(2,1)S(1)} %get-tuple-element.66), channel_id=1, source_target_pairs={{1,0},{2,1},{3,2},{4,3},{5,4},{6,5},{7,6},{9,8},{10,9},{11,10},{12... | collective-permute-start | bytes 73736 | tf_op jit(solution)/shard_map/ppermute | solution.py:29
  57.7 2.4 copy-start.14
  63.8 9.5 %copy-start.11 = (bf16[8,12,4,128]{3,2,1,0:T(4,128)(2,1)S(1)}, bf16[8,12,4,128]{3,2,1,0:T(4,128)(2,1)}, u32[]{:S(2)}) copy-start(bf16[8,12,4,128]{3,2,1,0:T(4,128)(2,1)} %copy.492) | copy-start | bytes 294916
  63.8 10.2 %copy-start.10 = (bf16[8,12,4,128]{3,2,1,0:T(4,128)(2,1)S(1)}, bf16[8,12,4,128]{3,2,1,0:T(4,128)(2,1)}, u32[]{:S(2)}) copy-start(bf16[8,12,4,128]{3,2,1,0:T(4,128)(2,1)} %copy.493) | copy-start | bytes 294916
  63.8 10.8 %copy-start.9 = (bf16[8,12,4,128]{3,2,1,0:T(4,128)(2,1)S(1)}, bf16[8,12,4,128]{3,2,1,0:T(4,128)(2,1)}, u32[]{:S(2)}) copy-start(bf16[8,12,4,128]{3,2,1,0:T(4,128)(2,1)} %copy.494) | copy-start | bytes 294916
  63.8 11.5 %copy-start.8 = (bf16[8,12,4,128]{3,2,1,0:T(4,128)(2,1)S(1)}, bf16[8,12,4,128]{3,2,1,0:T(4,128)(2,1)}, u32[]{:S(2)}) copy-start(bf16[8,12,4,128]{3,2,1,0:T(4,128)(2,1)} %copy.495) | copy-start | bytes 294916
  63.8 12.2 %copy-start.7 = (bf16[8,12,4,128]{3,2,1,0:T(4,128)(2,1)S(1)}, bf16[8,12,4,128]{3,2,1,0:T(4,128)(2,1)}, u32[]{:S(2)}) copy-start(bf16[8,12,4,128]{3,2,1,0:T(4,128)(2,1)} %copy.496) | copy-start | bytes 294916
  63.8 12.9 %copy-start.6 = (bf16[8,12,4,128]{3,2,1,0:T(4,128)(2,1)S(1)}, bf16[8,12,4,128]{3,2,1,0:T(4,128)(2,1)}, u32[]{:S(2)}) copy-start(bf16[8,12,4,128]{3,2,1,0:T(4,128)(2,1)} %copy.497) | copy-start | bytes 294916
  63.8 13.5 %copy-start.5 = (bf16[8,12,4,128]{3,2,1,0:T(4,128)(2,1)S(1)}, bf16[8,12,4,128]{3,2,1,0:T(4,128)(2,1)}, u32[]{:S(2)}) copy-start(bf16[8,12,4,128]{3,2,1,0:T(4,128)(2,1)} %copy.498) | copy-start | bytes 294916
  63.8 14.2 %copy-start.4 = (bf16[8,12,4,128]{3,2,1,0:T(4,128)(2,1)S(1)}, bf16[8,12,4,128]{3,2,1,0:T(4,128)(2,1)}, u32[]{:S(2)}) copy-start(bf16[8,12,4,128]{3,2,1,0:T(4,128)(2,1)} %copy.499) | copy-start | bytes 294916
  63.8 14.9 %copy-start.3 = (bf16[8,12,4,128]{3,2,1,0:T(4,128)(2,1)S(1)}, bf16[8,12,4,128]{3,2,1,0:T(4,128)(2,1)}, u32[]{:S(2)}) copy-start(bf16[8,12,4,128]{3,2,1,0:T(4,128)(2,1)} %copy.500) | copy-start | bytes 294916
  63.9 28.9 %all-to-all-start = ((f32[2,2,16,54,128]{4,2,3,1,0:T(8,128)}), f32[2,2,16,54,128]{4,2,3,1,0:T(8,128)}, u32[]{:S(2)}, u32[]{:S(2)}) async-start(f32[2,2,16,54,128]{4,2,3,1,0:T(8,128)} %copy.474), calls=%async_computation | async-start | bytes 3538944 | tf_op jit(solution)/shard_map/all_to_all | solution.py:145
  86.5 2.8 %copy-start.13 = (bf16[1,8,12,4,128]{4,3,2,1,0:T(4,128)(2,1)S(1)}, bf16[1,8,12,4,128]{4,3,2,1,0:T(4,128)(2,1)}, u32[]{:S(2)}) copy-start(bf16[1,8,12,4,128]{4,3,2,1,0:T(4,128)(2,1)} %copy.507) | copy-start | bytes 294916
  92.7 6.3 %all-to-all-start.2 = ((f32[2,2,16,54,128]{4,2,3,1,0:T(8,128)}), f32[2,2,16,54,128]{4,2,3,1,0:T(8,128)S(1)}, u32[]{:S(2)}, u32[]{:S(2)}) async-start(f32[2,2,16,54,128]{4,2,3,1,0:T(8,128)} %copy.508), calls=%async_computation.2 | async-start | bytes 3538944 | tf_op jit(solution)/shard_map/all_to_all | solution.py:145
  99.1 15.5 %all-to-all-start.1 = ((f32[2,16,54,128]{3,1,2,0:T(8,128)}), f32[2,16,54,128]{3,1,2,0:T(8,128)S(1)}, u32[]{:S(2)}, u32[]{:S(2)}) async-start(f32[2,16,54,128]{3,1,2,0:T(8,128)} %reduce_sum.54), calls=%async_computation.1 | async-start | bytes 1769472 | tf_op jit(solution)/shard_map/all_to_all | solution.py:145
  114.6 14.6 %all-to-all-start.3 = ((f32[2,16,54,128]{3,1,2,0:T(8,128)}), f32[2,16,54,128]{3,1,2,0:T(8,128)S(1)}, u32[]{:S(2)}, u32[]{:S(2)}) async-start(f32[2,16,54,128]{3,1,2,0:T(8,128)} %reduce_sum.56), calls=%async_computation.3 | async-start | bytes 1769472 | tf_op jit(solution)/shard_map/all_to_all | solution.py:145
  129.4 70.1 %copy-start.17 = (f32[2,54,16]{1,2,0:T(8,128)S(1)}, f32[2,54,16]{1,2,0:T(8,128)}, u32[]{:S(2)}) copy-start(f32[2,54,16]{1,2,0:T(8,128)} %param.12) | copy-start | bytes 20740
  129.4 70.1 %copy-start.18 = (f32[2,54,16]{1,2,0:T(8,128)S(1)}, f32[2,54,16]{1,2,0:T(8,128)}, u32[]{:S(2)}) copy-start(f32[2,54,16]{1,2,0:T(8,128)} %param.13) | copy-start | bytes 20740
  129.4 70.1 %copy-start.19 = (f32[2,54,16]{1,2,0:T(8,128)S(1)}, f32[2,54,16]{1,2,0:T(8,128)}, u32[]{:S(2)}) copy-start(f32[2,54,16]{1,2,0:T(8,128)} %param.14) | copy-start | bytes 20740
  181.0 64.7 %copy-start.20 = (f32[2,54,16]{1,2,0:T(8,128)S(1)}, f32[2,54,16]{1,2,0:T(8,128)}, u32[]{:S(2)}) copy-start(f32[2,54,16]{1,2,0:T(8,128)} %param.15) | copy-start | bytes 20740
  200.2 46.1 %copy-start.15 = (f32[2,54,16]{1,2,0:T(8,128)}, f32[2,54,16]{1,2,0:T(8,128)S(1)}, u32[]{:S(2)}) copy-start(f32[2,54,16]{1,2,0:T(8,128)S(1)} %get-tuple-element.6) | copy-start | bytes 20740

commit v7 on v5

--- a/solution.py
+++ b/solution.py
@@ -137,7 +137,7 @@
     return (new_master, new_moment, new_second, new_teacher, new_weights)
 
 
-ROW_AXES = ("z", "x_lo", "core")
+ROW_AXES = ("z_hi", "z_lo", "x_lo", "core")
 COLUMN_AXES = ("y", "x_hi")
 
 
@@ -149,13 +149,14 @@
 def scatter_rows_and_columns(weight_grads, own_shape):
     layers, rows, cols = own_shape
     lanes = weight_grads.shape[-1]
-    z, x_lo, core = (lax.axis_size(name) for name in ROW_AXES)
+    z_hi, z_lo, x_lo, core = (lax.axis_size(name) for name in ROW_AXES)
     y, x_hi = (lax.axis_size(name) for name in COLUMN_AXES)
-    blocks = weight_grads.reshape(layers, z, x_lo, core, rows, lanes)
-    blocks = blocks.transpose(3, 2, 1, 0, 4, 5)
+    blocks = weight_grads.reshape(layers, z_hi, z_lo, x_lo, core, rows, lanes)
+    blocks = blocks.transpose(4, 3, 2, 1, 0, 5, 6)
     blocks = exchange_and_sum(blocks, "core")
     blocks = exchange_and_sum(blocks, "x_lo")
-    blocks = exchange_and_sum(blocks, "z")
+    blocks = exchange_and_sum(blocks, "z_lo")
+    blocks = exchange_and_sum(blocks, "z_hi")
     blocks = blocks.reshape(layers, rows, y * x_hi, cols).transpose(2, 0, 1, 3)
     blocks = exchange_and_sum(blocks, COLUMN_AXES)
     return blocks * unit_scale()
@@ -163,7 +164,7 @@
 
 def gather_rows(fresh_weights):
     layers, rows, cols = fresh_weights.shape
-    gathered = lax.all_gather(fresh_weights, "z", axis=0)
+    gathered = lax.all_gather(fresh_weights, ("z_hi", "z_lo"), axis=0)
     gathered = lax.all_gather(gathered, ("x_lo", "core"), axis=0)
     gathered = gathered.reshape((-1,) + gathered.shape[1:])
     x_lo, core = lax.axis_size("x_lo"), lax.axis_size("core")
@@ -175,7 +176,7 @@
 def solution(mesh):
     rows_over, columns_over = mesh.shape["dp"], mesh.shape["slab"]
     fine = jax.sharding.Mesh(
-        mesh.devices.reshape(rows_over // 4, 2, 2, columns_over // 2, 2), ROW_AXES + COLUMN_AXES
+        mesh.devices.reshape(rows_over // 16, 4, 2, 2, columns_over // 2, 2), ROW_AXES + COLUMN_AXES
     )
     dp, slab = ROW_AXES, COLUMN_AXES
     in_specs = (

time: 232 us -> 231 us (level)
  blocking collectives: 146 us -> 143 us
    all_gather x1, blocking collectives: 26.1 us -> 23.7 us  [gather_rows(): gathered = lax.all_gather(fresh_weights, ('z_hi', 'z_lo'), axis=0)]
    all_to_all x4 -> x5, blocking collectives: 102 us -> 102 us  [exchange_and_sum(): moved = lax.all_to_all(blocks, axes, 0, 0, tiled=True)]
where the time goes in v7:
time: 231 us; the launch traced here: 230 us
  blocking collectives  143 us (62%)
  local copies, waits for them, and re-layouts  46.4 us (20%)
  starting transfers between devices  19.1 us (8%)
  matrix products  9.21 us (4%)
  other arithmetic  8.54 us (4%)
    all_to_all x5, blocking collectives, exchange_and_sum(): moved = lax.all_to_all(blocks, axes, 0, 0, tiled=True)  102 us
    all_gather x1, blocking collectives, gather_rows(): gathered = lax.all_gather(fresh_weights, ('z_hi', 'z_lo'), axis=0)  23.7 us
    unnamed x76, local copies, waits for them, and re-layouts  20 us
    all_gather x1, blocking collectives, gather_rows(): gathered = lax.all_gather(gathered, ('x_lo', 'core'), axis=0)  17.9 us
    ppermute x3, starting transfers between devices, with_halo(): lax.ppermute(tail, axis, [(i, (i + 1) % count) for i in range(ends)])  15 us
    dot_general x2, local copies, waits for them, and re-layouts, weight_grad(): lax.dot_general(columns, grad_rows, (((0,), (0,)), ((), ())), preferred_e...  7.24 us
    another operation x2, local copies, waits for them, and re-layouts  7.07 us
    conv_general_dilated x3, matrix products, volume_conv(): lax.conv_general_dilated(padded[None], kernel, (1, 1, 1), 'VALID', dimens...  6.98 us
  transfers between devices with their start and end apart: 6, of which 1 were waited for; matrix products, arithmetic and copies ran while one was open for 8% of the time, Pallas kernels for 0%

profile of v7, /device:TPU:1, one launch (start us, length us, event | category | flops | bytes accessed | tf_op | source)
XLA Modules:
  0.0 229.9 jit_solution(9511674866621030502)
XLA Ops:
  0.6 0.9 copy.451
  1.6 5.5 %collective-permute-start = (bf16[8,12,1,128]{3,1,2,0:T(8,128)(2,1)S(1)}, bf16[8,12,1,128]{3,1,2,0:T(8,128)(2,1)S(1)}, u32[]{:S(2)}, u32[]{:S(2)}) collective-permute-start(bf16[8,12,1,128]{3,1,2,0:T(8,128)(2,1)S(1)} %get-tuple-element.63), channel_id=1, source_target_pairs={{0,1},{1,2},{2,3},{3,4},{4,5},{5,6},{6,7},{8,9},{9,10},{10,11},{11... | collective-permute-start | bytes 73736 | tf_op jit(solution)/shard_map/ppermute | solution.py:27
  7.1 1.3 collective-permute-start.1
  8.4 2.8 %fusion.42 = (bf16[1,3456,128]{2,1,0:T(8,128)(2,1)}, bf16[1,3456,128]{2,1,0:T(8,128)(2,1)}) fusion(bf16[2,3456,128]{2,1,0:T(8,128)(2,1)} %param.11), kind=kLoop, calls=%fused_computation.132 | loop fusion | bytes 3538944 | tf_op jit(solution)/shard_map/slice | solution.py:120
  11.6 1.6 collective-permute-done.1
  13.4 0.6 fusion.45
  15.5 2.3 fusion.10
  18.0 4.0 %collective-permute-start.2 = (bf16[8,12,1,128]{3,0,2,1:T(8,128)(2,1)S(1)}, bf16[8,12,1,128]{3,0,2,1:T(8,128)(2,1)S(1)}, u32[]{:S(2)}, u32[]{:S(2)}) collective-permute-start(bf16[8,12,1,128]{3,0,2,1:T(8,128)(2,1)S(1)} %get-tuple-element.69), channel_id=1, source_target_pairs={{0,1},{1,2},{2,3},{3,4},{4,5},{5,6},{6,7},{8,9},{9,10},{10,11},{11... | collective-permute-start | bytes 73736 | tf_op jit(solution)/shard_map/ppermute | solution.py:27
  22.0 1.3 collective-permute-start.3
  24.2 2.8 %copy.374 = bf16[3456,384]{1,0:T(8,128)(2,1)} copy(bf16[3456,384]{0,1:T(8,128)(2,1)S(1)} %bitcast.147) | data formatting | bytes 5308416 | tf_op jit(solution)/shard_map/dot_general | solution.py:93
  27.0 2.8 %reshape.269 = bf16[4,4,2,2,54,384]{5,4,3,2,1,0:T(8,128)(2,1)S(1)} reshape(bf16[3456,384]{1,0:T(8,128)(2,1)} %copy.374) | data formatting | bytes 5308416 | tf_op jit(solution)/shard_map/reshape.33
  30.6 0.6 copy-done.1
  31.2 2.4 %fusion.8 = f32[1,8,12,4,128]{4,0,3,2,1:T(1,128)S(1)} fusion(bf16[3,3,3,128,128]{4,3,2,1,0:T(8,128)(2,1)S(1)} %bitcast.153, bf16[1,10,14,6,128]{4,1,3,2,0:T(8,128)(2,1)S(1)} %fusion.58), kind=kOutput, calls=%fused_computation.19 | convolution fusion | flops 339738624 | bytes 1296384 | tf_op jit(solution)/shard_map/conv_general_dilated | solution.py:68
  33.9 5.5 %collective-permute-start.4 = (bf16[8,12,1,128]{3,0,2,1:T(8,128)(2,1)S(1)}, bf16[8,12,1,128]{3,0,2,1:T(8,128)(2,1)S(1)}, u32[]{:S(2)}, u32[]{:S(2)}) collective-permute-start(bf16[8,12,1,128]{3,0,2,1:T(8,128)(2,1)S(1)} %get-tuple-element.65), channel_id=1, source_target_pairs={{0,1},{1,2},{2,3},{3,4},{4,5},{5,6},{6,7},{8,9},{9,10},{10,11},{11... | collective-permute-start | bytes 73736 | tf_op jit(solution)/shard_map/ppermute | solution.py:27
  39.4 1.5 collective-permute-start.5
  40.9 0.7 constant_dynamic-update-slice_fusion.53
  42.2 0.7 constant_dynamic-update-slice_fusion.52
  42.9 0.7 constant_dynamic-update-slice_fusion.51
  43.5 0.7 constant_dynamic-update-slice_fusion.50
  44.2 0.7 constant_dynamic-update-slice_fusion.49
  44.9 0.7 constant_dynamic-update-slice_fusion.48
  45.5 0.7 constant_dynamic-update-slice_fusion.47
  46.2 0.7 constant_dynamic-update-slice_fusion.46
  46.9 0.7 constant_dynamic-update-slice_fusion.45
  47.6 0.7 constant_dynamic-update-slice_fusion.44
  48.3 0.7 constant_dynamic-update-slice_fusion.43
  48.9 0.7 constant_dynamic-update-slice_fusion.42
  49.6 0.7 constant_dynamic-update-slice_fusion.41
  51.1 2.3 %fusion.6 = f32[1,8,12,4,128]{4,0,3,2,1:T(1,128)S(1)} fusion(bf16[3,3,3,128,128]{4,3,2,1,0:T(8,128)(2,1)S(1)} %bitcast.154, bf16[1,10,14,6,128]{4,1,3,2,0:T(8,128)(2,1)S(1)} %fusion.12), kind=kOutput, calls=%fused_computation.17 | convolution fusion | flops 339738624 | bytes 1296384 | tf_op jit(solution)/shard_map/conv_general_dilated | solution.py:68
  53.8 0.8 constant_dynamic-update-slice_fusion.40
  54.6 0.7 constant_dynamic-update-slice_fusion.39
  55.2 0.7 constant_dynamic-update-slice_fusion.38
  55.9 0.7 constant_dynamic-update-slice_fusion.37
  56.6 0.7 constant_dynamic-update-slice_fusion.36
  57.2 0.7 constant_dynamic-update-slice_fusion.35
  57.9 0.7 constant_dynamic-update-slice_fusion.34
  58.6 0.7 constant_dynamic-update-slice_fusion.33
  59.2 0.6 constant_dynamic-update-slice_fusion.32
  59.9 0.7 constant_dynamic-update-slice_fusion.31
  60.5 0.7 constant_dynamic-update-slice_fusion.30
  61.2 0.7 constant_dynamic-update-slice_fusion.29
  61.9 0.7 constant_dynamic-update-slice_fusion.28
  62.5 0.7 constant_dynamic-update-slice_fusion.27
  63.2 4.4 %copy.413 = bf16[3456,384]{1,0:T(8,128)(2,1)} copy(bf16[3456,384]{0,1:T(8,128)(2,1)} %bitcast.69) | data formatting | bytes 5308416 | tf_op jit(solution)/shard_map/dot_general | solution.py:93
  67.6 4.3 %reshape.296 = bf16[4,4,2,2,54,384]{5,4,3,2,1,0:T(8,128)(2,1)} reshape(bf16[3456,384]{1,0:T(8,128)(2,1)} %copy.413) | data formatting | bytes 5308416 | tf_op jit(solution)/shard_map/reshape.37
  71.9 1.1 convolution_bitcast_fusion.1
  73.0 0.7 copy-done
  73.7 1.1 convolution_bitcast_fusion
  75.1 2.3 copy.416
  77.4 9.9 %all_to_all.25 = f32[2,2,4,4,2,54,128]{6,3,5,4,2,1,0:T(4,128)S(1)} all-to-all(f32[2,2,4,4,2,54,128]{6,3,5,4,2,1,0:T(4,128)S(1)} %copy.416), channel_id=1, replica_groups=mesh['z_hi'=4,'z_lo'=4,'x_lo'=2,'core'=2,'y'=4,'x_hi'=2] {'core'}, dimensions={0} | all-to-all | bytes 7077888 | tf_op jit(solution)/shard_map/all_to_all | solution.py:145
  87.3 2.9 %reduce_sum.45 = f32[2,4,4,2,54,128]{5,2,4,3,1,0:T(4,128)} reduce(f32[2,2,4,4,2,54,128]{6,3,5,4,2,1,0:T(4,128)S(1)} %all_to_all.25, f32[]{:T(128)} %constant.8.clone.1), dimensions={0}, to_apply=%region_0.1 | reduce | flops 442368 | bytes 5308420 | tf_op jit(solution)/shard_map/reduce_sum | solution.py:146
  90.2 24.8 %all_to_all.26 = f32[2,4,4,2,54,128]{5,2,4,3,1,0:T(4,128)S(1)} all-to-all(f32[2,4,4,2,54,128]{5,2,4,3,1,0:T(4,128)} %reduce_sum.45), channel_id=1, replica_groups=mesh['z_hi'=4,'z_lo'=4,'x_lo'=2,'core'=2,'y'=4,'x_hi'=2] {'x_lo'}, dimensions={0} | all-to-all | bytes 3538944 | tf_op jit(solution)/shard_map/all_to_all | solution.py:145
  114.9 0.8 reduce_sum.46
  115.8 26.3 %all_to_all.27 = f32[4,4,2,54,128]{4,1,3,2,0:T(4,128)S(1)} all-to-all(f32[4,4,2,54,128]{4,1,3,2,0:T(4,128)S(1)} %reduce_sum.46), channel_id=1, replica_groups=mesh['z_hi'=4,'z_lo'=4,'x_lo'=2,'core'=2,'y'=4,'x_hi'=2] {'z_lo'}, dimensions={0} | all-to-all | bytes 1769472 | tf_op jit(solution)/shard_map/all_to_all | solution.py:145
  142.4 25.9 %all_to_all.28 = f32[4,2,54,128]{3,1,2,0:T(2,128)S(1)} all-to-all(f32[4,2,54,128]{3,1,2,0:T(2,128)S(1)} %copy.419), channel_id=1, replica_groups=mesh['z_hi'=4,'z_lo'=4,'x_lo'=2,'core'=2,'y'=4,'x_hi'=2] {'z_hi'}, dimensions={0} | all-to-all | bytes 442368 | tf_op jit(solution)/shard_map/all_to_all | solution.py:145
  168.7 14.9 %all_to_all.29 = f32[8,1,1728]{2,1,0:T(1,128)S(1)} all-to-all(f32[8,1,1728]{2,1,0:T(1,128)S(1)} %reshape.306), channel_id=1, replica_groups=mesh['z_hi'=4,'z_lo'=4,'x_lo'=2,'core'=2,'y'=4,'x_hi'=2] {'y','x_hi'}, dimensions={0} | all-to-all | bytes 110592 | tf_op jit(solution)/shard_map/all_to_all | solution.py:145
  183.6 0.5 broadcast.246
  184.1 0.8 reduce
  185.1 0.6 fusion.41
  185.7 23.7 %all-gather = bf16[32,54,16]{1,2,0:T(8,128)(2,1)S(1)} all-gather(bf16[2,54,16]{1,2,0:T(8,128)(2,1)S(1)} %get-tuple-element.5), channel_id=2, replica_groups=mesh['z_hi'=4,'z_lo'=4,'x_lo'=2,'core'=2,'y'=4,'x_hi'=2] {'z_hi','z_lo'}, dimensions={0}, use_global_device_ids=true | all-gather | bytes 58752 | tf_op jit(solution)/shard_map/all_gather | solution.py:167
  209.5 17.9 %all-gather.1 = bf16[64,2,54,16]{2,3,1,0:T(8,128)(2,1)S(1)} all-gather(bf16[16,2,54,16]{2,3,1,0:T(8,128)(2,1)S(1)} %bitcast.157), channel_id=3, replica_groups=mesh['z_hi'=4,'z_lo'=4,'x_lo'=2,'core'=2,'y'=4,'x_hi'=2] {'x_lo','core'}, dimensions={0}, use_global_device_ids=true | all-gather | bytes 276480 | tf_op jit(solution)/shard_map/all_gather | solution.py:168
  227.4 0.5 copy.422
  227.9 1.4 reshape.299
  229.3 0.6 multiply_add_fusion
  (139 shorter events, 6.6 us)
Async XLA Ops:
  0.6 10.5 %copy-start.6 = (s32[1,8,12,4]{2,3,1,0:T(4,128)S(1)}, s32[1,8,12,4]{2,3,1,0:T(4,128)}, u32[]{:S(2)}) copy-start(s32[1,8,12,4]{2,3,1,0:T(4,128)} %param.9) | copy-start | bytes 4612
  1.6 10.0 %collective-permute-start = (bf16[8,12,1,128]{3,1,2,0:T(8,128)(2,1)S(1)}, bf16[8,12,1,128]{3,1,2,0:T(8,128)(2,1)S(1)}, u32[]{:S(2)}, u32[]{:S(2)}) collective-permute-start(bf16[8,12,1,128]{3,1,2,0:T(8,128)(2,1)S(1)} %get-tuple-element.63), channel_id=1, source_target_pairs={{0,1},{1,2},{2,3},{3,4},{4,5},{5,6},{6,7},{8,9},{9,10},{10,11},{11... | collective-permute-start | bytes 73736 | tf_op jit(solution)/shard_map/ppermute | solution.py:27
  7.1 6.2 %collective-permute-start.1 = (bf16[8,12,1,128]{3,1,2,0:T(8,128)(2,1)S(1)}, bf16[8,12,1,128]{3,1,2,0:T(8,128)(2,1)S(1)}, u32[]{:S(2)}, u32[]{:S(2)}) collective-permute-start(bf16[8,12,1,128]{3,1,2,0:T(8,128)(2,1)S(1)} %get-tuple-element.64), channel_id=1, source_target_pairs={{1,0},{2,1},{3,2},{4,3},{5,4},{6,5},{7,6},{9,8},{10,9},{11,10},{12... | collective-permute-start | bytes 73736 | tf_op jit(solution)/shard_map/ppermute | solution.py:29
  14.4 1.2 copy-start.2
  17.8 5.9 %copy-start.3 = (bf16[1,8,12,4,128]{4,3,2,1,0:T(4,128)(2,1)S(1)}, bf16[1,8,12,4,128]{4,3,2,1,0:T(4,128)(2,1)}, u32[]{:S(2)}) copy-start(bf16[1,8,12,4,128]{4,3,2,1,0:T(4,128)(2,1)} %param.8) | copy-start | bytes 294916
  18.0 11.9 %collective-permute-start.2 = (bf16[8,12,1,128]{3,0,2,1:T(8,128)(2,1)S(1)}, bf16[8,12,1,128]{3,0,2,1:T(8,128)(2,1)S(1)}, u32[]{:S(2)}, u32[]{:S(2)}) collective-permute-start(bf16[8,12,1,128]{3,0,2,1:T(8,128)(2,1)S(1)} %get-tuple-element.69), channel_id=1, source_target_pairs={{0,1},{1,2},{2,3},{3,4},{4,5},{5,6},{6,7},{8,9},{9,10},{10,11},{11... | collective-permute-start | bytes 73736 | tf_op jit(solution)/shard_map/ppermute | solution.py:27
  22.0 7.8 %collective-permute-start.3 = (bf16[8,12,1,128]{3,0,2,1:T(8,128)(2,1)S(1)}, bf16[8,12,1,128]{3,0,2,1:T(8,128)(2,1)S(1)}, u32[]{:S(2)}, u32[]{:S(2)}) collective-permute-start(bf16[8,12,1,128]{3,0,2,1:T(8,128)(2,1)S(1)} %get-tuple-element.70), channel_id=1, source_target_pairs={{1,0},{2,1},{3,2},{4,3},{5,4},{6,5},{7,6},{9,8},{10,9},{11,10},{12... | collective-permute-start | bytes 73736 | tf_op jit(solution)/shard_map/ppermute | solution.py:29
  30.0 1.2 copy-start.1
  30.6 3.0 %copy-start.4 = (bf16[1,8,12,4,128]{4,3,2,1,0:T(4,128)(2,1)S(1)}, bf16[1,8,12,4,128]{4,3,2,1,0:T(4,128)(2,1)}, u32[]{:S(2)}) copy-start(bf16[1,8,12,4,128]{4,3,2,1,0:T(4,128)(2,1)} %param.10) | copy-start | bytes 294916
  33.9 17.0 %collective-permute-start.4 = (bf16[8,12,1,128]{3,0,2,1:T(8,128)(2,1)S(1)}, bf16[8,12,1,128]{3,0,2,1:T(8,128)(2,1)S(1)}, u32[]{:S(2)}, u32[]{:S(2)}) collective-permute-start(bf16[8,12,1,128]{3,0,2,1:T(8,128)(2,1)S(1)} %get-tuple-element.65), channel_id=1, source_target_pairs={{0,1},{1,2},{2,3},{3,4},{4,5},{5,6},{6,7},{8,9},{9,10},{10,11},{11... | collective-permute-start | bytes 73736 | tf_op jit(solution)/shard_map/ppermute | solution.py:27
  39.4 11.5 %collective-permute-start.5 = (bf16[8,12,1,128]{3,0,2,1:T(8,128)(2,1)S(1)}, bf16[8,12,1,128]{3,0,2,1:T(8,128)(2,1)S(1)}, u32[]{:S(2)}, u32[]{:S(2)}) collective-permute-start(bf16[8,12,1,128]{3,0,2,1:T(8,128)(2,1)S(1)} %get-tuple-element.66), channel_id=1, source_target_pairs={{1,0},{2,1},{3,2},{4,3},{5,4},{6,5},{7,6},{9,8},{10,9},{11,10},{12... | collective-permute-start | bytes 73736 | tf_op jit(solution)/shard_map/ppermute | solution.py:29
  71.9 1.8 copy-start
  115.8 69.3 %copy-start.7 = (f32[2,54,16]{1,2,0:T(8,128)S(1)}, f32[2,54,16]{1,2,0:T(8,128)}, u32[]{:S(2)}) copy-start(f32[2,54,16]{1,2,0:T(8,128)} %param.12) | copy-start | bytes 20740
  115.8 69.3 %copy-start.8 = (f32[2,54,16]{1,2,0:T(8,128)S(1)}, f32[2,54,16]{1,2,0:T(8,128)}, u32[]{:S(2)}) copy-start(f32[2,54,16]{1,2,0:T(8,128)} %param.13) | copy-start | bytes 20740
  115.8 69.3 %copy-start.9 = (f32[2,54,16]{1,2,0:T(8,128)S(1)}, f32[2,54,16]{1,2,0:T(8,128)}, u32[]{:S(2)}) copy-start(f32[2,54,16]{1,2,0:T(8,128)} %param.14) | copy-start | bytes 20740
  142.3 87.0 %copy-start.10 = (f32[2,54,16]{1,2,0:T(8,128)S(1)}, f32[2,54,16]{1,2,0:T(8,128)}, u32[]{:S(2)}) copy-start(f32[2,54,16]{1,2,0:T(8,128)} %param.15) | copy-start | bytes 20740
  185.7 44.2 %copy-start.5 = (f32[2,54,16]{1,2,0:T(8,128)}, f32[2,54,16]{1,2,0:T(8,128)S(1)}, u32[]{:S(2)}) copy-start(f32[2,54,16]{1,2,0:T(8,128)S(1)} %get-tuple-element.6) | copy-start | bytes 20740

commit v8 on v7

--- a/solution.py
+++ b/solution.py
@@ -156,9 +156,9 @@
     blocks = exchange_and_sum(blocks, "core")
     blocks = exchange_and_sum(blocks, "x_lo")
     blocks = exchange_and_sum(blocks, "z_lo")
-    blocks = exchange_and_sum(blocks, "z_hi")
-    blocks = blocks.reshape(layers, rows, y * x_hi, cols).transpose(2, 0, 1, 3)
-    blocks = exchange_and_sum(blocks, COLUMN_AXES)
+    blocks = blocks.reshape(z_hi, layers, rows, y * x_hi, cols).transpose(0, 3, 1, 2, 4)
+    blocks = blocks.reshape((z_hi * y * x_hi,) + blocks.shape[2:])
+    blocks = exchange_and_sum(blocks, ("z_hi",) + COLUMN_AXES)
     return blocks * unit_scale()
 
 

time: 231 us -> 226 us (0.978)
  blocking collectives: 143 us -> 137 us
    all_to_all x5 -> x4, blocking collectives: 102 us -> 97.4 us  [exchange_and_sum(): moved = lax.all_to_all(blocks, axes, 0, 0, tiled=True)]
    all_gather x1, blocking collectives: 17.9 us -> 14.7 us  [gather_rows(): gathered = lax.all_gather(gathered, ('x_lo', 'core'), axis=0)]
  transfers between devices with their start and end apart: 6 -> 6, of which waited for: 1 -> 1; matrix products, arithmetic and copies ran while one was open for 8% -> 9% of each run, Pallas kernels for 0% -> 0%
where the time goes in v8:
time: 226 us; the launch traced here: 225 us
  blocking collectives  137 us (61%)
  local copies, waits for them, and re-layouts  47.5 us (21%)
  starting transfers between devices  19.1 us (8%)
  matrix products  9.21 us (4%)
  other arithmetic  8.91 us (4%)
    all_to_all x4, blocking collectives, exchange_and_sum(): moved = lax.all_to_all(blocks, axes, 0, 0, tiled=True)  97.4 us
    all_gather x1, blocking collectives, gather_rows(): gathered = lax.all_gather(fresh_weights, ('z_hi', 'z_lo'), axis=0)  25.1 us
    unnamed x76, local copies, waits for them, and re-layouts  21.1 us
    ppermute x3, starting transfers between devices, with_halo(): lax.ppermute(tail, axis, [(i, (i + 1) % count) for i in range(ends)])  15 us
    all_gather x1, blocking collectives, gather_rows(): gathered = lax.all_gather(gathered, ('x_lo', 'core'), axis=0)  14.7 us
    dot_general x2, local copies, waits for them, and re-layouts, weight_grad(): lax.dot_general(columns, grad_rows, (((0,), (0,)), ((), ())), preferred_e...  7.26 us
    another operation x2, local copies, waits for them, and re-layouts  7.05 us
    conv_general_dilated x3, matrix products, volume_conv(): lax.conv_general_dilated(padded[None], kernel, (1, 1, 1), 'VALID', dimens...  6.98 us
  transfers between devices with their start and end apart: 6, of which 1 were waited for; matrix products, arithmetic and copies ran while one was open for 9% of the time, Pallas kernels for 0%

profile of v8, /device:TPU:1, one launch (start us, length us, event | category | flops | bytes accessed | tf_op | source)
XLA Modules:
  0.0 225.3 jit_solution(8206182962331914483)
XLA Ops:
  0.6 0.9 copy.449
  1.6 5.5 %collective-permute-start = (bf16[8,12,1,128]{3,1,2,0:T(8,128)(2,1)S(1)}, bf16[8,12,1,128]{3,1,2,0:T(8,128)(2,1)S(1)}, u32[]{:S(2)}, u32[]{:S(2)}) collective-permute-start(bf16[8,12,1,128]{3,1,2,0:T(8,128)(2,1)S(1)} %get-tuple-element.63), channel_id=1, source_target_pairs={{0,1},{1,2},{2,3},{3,4},{4,5},{5,6},{6,7},{8,9},{9,10},{10,11},{11... | collective-permute-start | bytes 73736 | tf_op jit(solution)/shard_map/ppermute | solution.py:27
  7.1 1.3 collective-permute-start.1
  8.4 2.8 %fusion.42 = (bf16[1,3456,128]{2,1,0:T(8,128)(2,1)}, bf16[1,3456,128]{2,1,0:T(8,128)(2,1)}) fusion(bf16[2,3456,128]{2,1,0:T(8,128)(2,1)} %param.11), kind=kLoop, calls=%fused_computation.132 | loop fusion | bytes 3538944 | tf_op jit(solution)/shard_map/slice | solution.py:120
  11.6 1.6 collective-permute-done.1
  13.4 0.6 fusion.45
  15.5 2.3 %fusion.10 = f32[1,8,12,4,128]{4,0,3,2,1:T(1,128)S(1)} fusion(bf16[3,3,3,128,128]{4,3,2,1,0:T(8,128)(2,1)S(1)} %bitcast.156, bf16[1,10,14,6,128]{4,2,3,1,0:T(8,128)(2,1)S(1)} %fusion.59), kind=kOutput, calls=%fused_computation.21 | convolution fusion | flops 339738624 | bytes 1296384 | tf_op jit(solution)/shard_map/conv_general_dilated | solution.py:68
  18.0 4.0 %collective-permute-start.2 = (bf16[8,12,1,128]{3,0,2,1:T(8,128)(2,1)S(1)}, bf16[8,12,1,128]{3,0,2,1:T(8,128)(2,1)S(1)}, u32[]{:S(2)}, u32[]{:S(2)}) collective-permute-start(bf16[8,12,1,128]{3,0,2,1:T(8,128)(2,1)S(1)} %get-tuple-element.69), channel_id=1, source_target_pairs={{0,1},{1,2},{2,3},{3,4},{4,5},{5,6},{6,7},{8,9},{9,10},{10,11},{11... | collective-permute-start | bytes 73736 | tf_op jit(solution)/shard_map/ppermute | solution.py:27
  22.0 1.3 collective-permute-start.3
  24.2 2.8 %copy.374 = bf16[3456,384]{1,0:T(8,128)(2,1)} copy(bf16[3456,384]{0,1:T(8,128)(2,1)S(1)} %bitcast.146) | data formatting | bytes 5308416 | tf_op jit(solution)/shard_map/dot_general | solution.py:93
  27.0 2.8 %reshape.272 = bf16[4,4,2,2,54,384]{5,4,3,2,1,0:T(8,128)(2,1)S(1)} reshape(bf16[3456,384]{1,0:T(8,128)(2,1)} %copy.374) | data formatting | bytes 5308416 | tf_op jit(solution)/shard_map/reshape.33
  30.6 0.6 copy-done.1
  31.2 2.4 %fusion.8 = f32[1,8,12,4,128]{4,0,3,2,1:T(1,128)S(1)} fusion(bf16[3,3,3,128,128]{4,3,2,1,0:T(8,128)(2,1)S(1)} %bitcast.154, bf16[1,10,14,6,128]{4,1,3,2,0:T(8,128)(2,1)S(1)} %fusion.58), kind=kOutput, calls=%fused_computation.19 | convolution fusion | flops 339738624 | bytes 1296384 | tf_op jit(solution)/shard_map/conv_general_dilated | solution.py:68
  33.9 5.5 %collective-permute-start.4 = (bf16[8,12,1,128]{3,0,2,1:T(8,128)(2,1)S(1)}, bf16[8,12,1,128]{3,0,2,1:T(8,128)(2,1)S(1)}, u32[]{:S(2)}, u32[]{:S(2)}) collective-permute-start(bf16[8,12,1,128]{3,0,2,1:T(8,128)(2,1)S(1)} %get-tuple-element.65), channel_id=1, source_target_pairs={{0,1},{1,2},{2,3},{3,4},{4,5},{5,6},{6,7},{8,9},{9,10},{10,11},{11... | collective-permute-start | bytes 73736 | tf_op jit(solution)/shard_map/ppermute | solution.py:27
  39.4 1.5 collective-permute-start.5
  40.9 0.7 constant_dynamic-update-slice_fusion.53
  42.2 0.7 constant_dynamic-update-slice_fusion.52
  42.9 0.7 constant_dynamic-update-slice_fusion.51
  43.5 0.7 constant_dynamic-update-slice_fusion.50
  44.2 0.7 constant_dynamic-update-slice_fusion.49
  44.9 0.6 constant_dynamic-update-slice_fusion.48
  45.5 0.7 constant_dynamic-update-slice_fusion.47
  46.2 0.7 constant_dynamic-update-slice_fusion.46
  46.9 0.7 constant_dynamic-update-slice_fusion.45
  47.5 0.7 constant_dynamic-update-slice_fusion.44
  48.2 0.7 constant_dynamic-update-slice_fusion.43
  48.9 0.7 constant_dynamic-update-slice_fusion.42
  49.6 0.7 constant_dynamic-update-slice_fusion.41
  51.1 2.3 %fusion.6 = f32[1,8,12,4,128]{4,0,3,2,1:T(1,128)S(1)} fusion(bf16[3,3,3,128,128]{4,3,2,1,0:T(8,128)(2,1)S(1)} %bitcast.155, bf16[1,10,14,6,128]{4,1,3,2,0:T(8,128)(2,1)S(1)} %fusion.12), kind=kOutput, calls=%fused_computation.17 | convolution fusion | flops 339738624 | bytes 1296384 | tf_op jit(solution)/shard_map/conv_general_dilated | solution.py:68
  53.8 0.8 constant_dynamic-update-slice_fusion.40
  54.5 0.7 constant_dynamic-update-slice_fusion.39
  55.2 0.7 constant_dynamic-update-slice_fusion.38
  55.9 0.7 constant_dynamic-update-slice_fusion.37
  56.5 0.7 constant_dynamic-update-slice_fusion.36
  57.2 0.7 constant_dynamic-update-slice_fusion.35
  57.9 0.7 constant_dynamic-update-slice_fusion.34
  58.5 0.7 constant_dynamic-update-slice_fusion.33
  59.2 0.7 constant_dynamic-update-slice_fusion.32
  59.9 0.7 constant_dynamic-update-slice_fusion.31
  60.5 0.7 constant_dynamic-update-slice_fusion.30
  61.2 0.6 constant_dynamic-update-slice_fusion.29
  61.8 0.7 constant_dynamic-update-slice_fusion.28
  62.5 0.7 constant_dynamic-update-slice_fusion.27
  63.2 4.4 %copy.413 = bf16[3456,384]{1,0:T(8,128)(2,1)} copy(bf16[3456,384]{0,1:T(8,128)(2,1)} %bitcast.69) | data formatting | bytes 5308416 | tf_op jit(solution)/shard_map/dot_general | solution.py:93
  67.6 4.3 %reshape.299 = bf16[4,4,2,2,54,384]{5,4,3,2,1,0:T(8,128)(2,1)} reshape(bf16[3456,384]{1,0:T(8,128)(2,1)} %copy.413) | data formatting | bytes 5308416 | tf_op jit(solution)/shard_map/reshape.37
  71.9 1.1 convolution_bitcast_fusion.1
  73.0 0.7 copy-done
  73.6 1.1 convolution_bitcast_fusion
  75.1 2.3 %copy.416 = f32[2,2,4,4,2,54,128]{6,3,5,4,2,1,0:T(4,128)S(1)} copy(f32[2,2,4,4,2,54,128]{6,5,0,1,2,3,4:T(8,128)S(1)} %maximum_bitcast_fusion) | data formatting | bytes 7077888 | tf_op jit(solution)/shard_map/transpose | solution.py:155
  77.4 9.9 %all_to_all.20 = f32[2,2,4,4,2,54,128]{6,3,5,4,2,1,0:T(4,128)S(1)} all-to-all(f32[2,2,4,4,2,54,128]{6,3,5,4,2,1,0:T(4,128)S(1)} %copy.416), channel_id=1, replica_groups=mesh['z_hi'=4,'z_lo'=4,'x_lo'=2,'core'=2,'y'=4,'x_hi'=2] {'core'}, dimensions={0} | all-to-all | bytes 7077888 | tf_op jit(solution)/shard_map/all_to_all | solution.py:145
  87.3 2.9 %reduce_sum.36 = f32[2,4,4,2,54,128]{5,2,4,3,1,0:T(4,128)} reduce(f32[2,2,4,4,2,54,128]{6,3,5,4,2,1,0:T(4,128)S(1)} %all_to_all.20, f32[]{:T(128)} %constant.8.clone.1), dimensions={0}, to_apply=%region_0.1 | reduce | flops 442368 | bytes 5308420 | tf_op jit(solution)/shard_map/reduce_sum | solution.py:146
  90.2 24.8 %all_to_all.21 = f32[2,4,4,2,54,128]{5,2,4,3,1,0:T(4,128)S(1)} all-to-all(f32[2,4,4,2,54,128]{5,2,4,3,1,0:T(4,128)} %reduce_sum.36), channel_id=1, replica_groups=mesh['z_hi'=4,'z_lo'=4,'x_lo'=2,'core'=2,'y'=4,'x_hi'=2] {'x_lo'}, dimensions={0} | all-to-all | bytes 3538944 | tf_op jit(solution)/shard_map/all_to_all | solution.py:145
  114.9 0.8 reduce_sum.37
  115.8 26.1 %all_to_all.22 = f32[4,4,2,54,128]{4,1,3,2,0:T(4,128)S(1)} all-to-all(f32[4,4,2,54,128]{4,1,3,2,0:T(4,128)S(1)} %reduce_sum.37), channel_id=1, replica_groups=mesh['z_hi'=4,'z_lo'=4,'x_lo'=2,'core'=2,'y'=4,'x_hi'=2] {'z_lo'}, dimensions={0} | all-to-all | bytes 1769472 | tf_op jit(solution)/shard_map/all_to_all | solution.py:145
  142.4 0.7 reshape.310
  143.1 36.6 %all_to_all.23 = f32[32,1,1728]{2,1,0:T(1,128)S(1)} all-to-all(f32[32,1,1728]{2,1,0:T(1,128)S(1)} %reshape.310), channel_id=1, replica_groups=mesh['z_hi'=4,'z_lo'=4,'x_lo'=2,'core'=2,'y'=4,'x_hi'=2] {'z_hi','y','x_..., dimensions={0} | all-to-all | bytes 442368 | tf_op jit(solution)/shard_map/all_to_all | solution.py:145
  180.2 1.2 reduce
  181.4 0.7 reshape.311
  182.3 0.6 fusion.41
  182.9 25.1 %all-gather = bf16[32,54,16]{1,2,0:T(8,128)(2,1)S(1)} all-gather(bf16[2,54,16]{1,2,0:T(8,128)(2,1)S(1)} %get-tuple-element.5), channel_id=2, replica_groups=mesh['z_hi'=4,'z_lo'=4,'x_lo'=2,'core'=2,'y'=4,'x_hi'=2] {'z_hi','z_lo'}, dimensions={0}, use_global_device_ids=true | all-gather | bytes 58752 | tf_op jit(solution)/shard_map/all_gather | solution.py:167
  208.0 14.7 %all-gather.1 = bf16[64,2,54,16]{2,3,1,0:T(8,128)(2,1)S(1)} all-gather(bf16[16,2,54,16]{2,3,1,0:T(8,128)(2,1)S(1)} %bitcast.158), channel_id=3, replica_groups=mesh['z_hi'=4,'z_lo'=4,'x_lo'=2,'core'=2,'y'=4,'x_hi'=2] {'x_lo','core'}, dimensions={0}, use_global_device_ids=true | all-gather | bytes 276480 | tf_op jit(solution)/shard_map/all_gather | solution.py:168
  222.8 0.5 copy.421
  223.3 1.4 reshape.303
  224.7 0.6 multiply_add_fusion
  (136 shorter events, 6.8 us)
Async XLA Ops:
  0.6 10.5 %copy-start.6 = (s32[1,8,12,4]{2,3,1,0:T(4,128)S(1)}, s32[1,8,12,4]{2,3,1,0:T(4,128)}, u32[]{:S(2)}) copy-start(s32[1,8,12,4]{2,3,1,0:T(4,128)} %param.9) | copy-start | bytes 4612
  1.6 10.0 %collective-permute-start = (bf16[8,12,1,128]{3,1,2,0:T(8,128)(2,1)S(1)}, bf16[8,12,1,128]{3,1,2,0:T(8,128)(2,1)S(1)}, u32[]{:S(2)}, u32[]{:S(2)}) collective-permute-start(bf16[8,12,1,128]{3,1,2,0:T(8,128)(2,1)S(1)} %get-tuple-element.63), channel_id=1, source_target_pairs={{0,1},{1,2},{2,3},{3,4},{4,5},{5,6},{6,7},{8,9},{9,10},{10,11},{11... | collective-permute-start | bytes 73736 | tf_op jit(solution)/shard_map/ppermute | solution.py:27
  7.1 6.2 %collective-permute-start.1 = (bf16[8,12,1,128]{3,1,2,0:T(8,128)(2,1)S(1)}, bf16[8,12,1,128]{3,1,2,0:T(8,128)(2,1)S(1)}, u32[]{:S(2)}, u32[]{:S(2)}) collective-permute-start(bf16[8,12,1,128]{3,1,2,0:T(8,128)(2,1)S(1)} %get-tuple-element.64), channel_id=1, source_target_pairs={{1,0},{2,1},{3,2},{4,3},{5,4},{6,5},{7,6},{9,8},{10,9},{11,10},{12... | collective-permute-start | bytes 73736 | tf_op jit(solution)/shard_map/ppermute | solution.py:29
  14.4 1.2 copy-start.2
  17.8 5.9 %copy-start.3 = (bf16[1,8,12,4,128]{4,3,2,1,0:T(4,128)(2,1)S(1)}, bf16[1,8,12,4,128]{4,3,2,1,0:T(4,128)(2,1)}, u32[]{:S(2)}) copy-start(bf16[1,8,12,4,128]{4,3,2,1,0:T(4,128)(2,1)} %param.8) | copy-start | bytes 294916
  18.0 11.9 %collective-permute-start.2 = (bf16[8,12,1,128]{3,0,2,1:T(8,128)(2,1)S(1)}, bf16[8,12,1,128]{3,0,2,1:T(8,128)(2,1)S(1)}, u32[]{:S(2)}, u32[]{:S(2)}) collective-permute-start(bf16[8,12,1,128]{3,0,2,1:T(8,128)(2,1)S(1)} %get-tuple-element.69), channel_id=1, source_target_pairs={{0,1},{1,2},{2,3},{3,4},{4,5},{5,6},{6,7},{8,9},{9,10},{10,11},{11... | collective-permute-start | bytes 73736 | tf_op jit(solution)/shard_map/ppermute | solution.py:27
  22.0 7.8 %collective-permute-start.3 = (bf16[8,12,1,128]{3,0,2,1:T(8,128)(2,1)S(1)}, bf16[8,12,1,128]{3,0,2,1:T(8,128)(2,1)S(1)}, u32[]{:S(2)}, u32[]{:S(2)}) collective-permute-start(bf16[8,12,1,128]{3,0,2,1:T(8,128)(2,1)S(1)} %get-tuple-element.70), channel_id=1, source_target_pairs={{1,0},{2,1},{3,2},{4,3},{5,4},{6,5},{7,6},{9,8},{10,9},{11,10},{12... | collective-permute-start | bytes 73736 | tf_op jit(solution)/shard_map/ppermute | solution.py:29
  30.0 1.2 copy-start.1
  30.6 3.0 %copy-start.4 = (bf16[1,8,12,4,128]{4,3,2,1,0:T(4,128)(2,1)S(1)}, bf16[1,8,12,4,128]{4,3,2,1,0:T(4,128)(2,1)}, u32[]{:S(2)}) copy-start(bf16[1,8,12,4,128]{4,3,2,1,0:T(4,128)(2,1)} %param.10) | copy-start | bytes 294916
  33.9 17.0 %collective-permute-start.4 = (bf16[8,12,1,128]{3,0,2,1:T(8,128)(2,1)S(1)}, bf16[8,12,1,128]{3,0,2,1:T(8,128)(2,1)S(1)}, u32[]{:S(2)}, u32[]{:S(2)}) collective-permute-start(bf16[8,12,1,128]{3,0,2,1:T(8,128)(2,1)S(1)} %get-tuple-element.65), channel_id=1, source_target_pairs={{0,1},{1,2},{2,3},{3,4},{4,5},{5,6},{6,7},{8,9},{9,10},{10,11},{11... | collective-permute-start | bytes 73736 | tf_op jit(solution)/shard_map/ppermute | solution.py:27
  39.4 11.5 %collective-permute-start.5 = (bf16[8,12,1,128]{3,0,2,1:T(8,128)(2,1)S(1)}, bf16[8,12,1,128]{3,0,2,1:T(8,128)(2,1)S(1)}, u32[]{:S(2)}, u32[]{:S(2)}) collective-permute-start(bf16[8,12,1,128]{3,0,2,1:T(8,128)(2,1)S(1)} %get-tuple-element.66), channel_id=1, source_target_pairs={{1,0},{2,1},{3,2},{4,3},{5,4},{6,5},{7,6},{9,8},{10,9},{11,10},{12... | collective-permute-start | bytes 73736 | tf_op jit(solution)/shard_map/ppermute | solution.py:29
  71.9 1.8 copy-start
  142.1 40.1 %copy-start.7 = (f32[2,54,16]{1,2,0:T(8,128)S(1)}, f32[2,54,16]{1,2,0:T(8,128)}, u32[]{:S(2)}) copy-start(f32[2,54,16]{1,2,0:T(8,128)} %param.12) | copy-start | bytes 20740
  142.1 40.1 %copy-start.8 = (f32[2,54,16]{1,2,0:T(8,128)S(1)}, f32[2,54,16]{1,2,0:T(8,128)}, u32[]{:S(2)}) copy-start(f32[2,54,16]{1,2,0:T(8,128)} %param.13) | copy-start | bytes 20740
  142.1 40.1 %copy-start.9 = (f32[2,54,16]{1,2,0:T(8,128)S(1)}, f32[2,54,16]{1,2,0:T(8,128)}, u32[]{:S(2)}) copy-start(f32[2,54,16]{1,2,0:T(8,128)} %param.14) | copy-start | bytes 20740
  143.1 81.5 %copy-start.10 = (f32[2,54,16]{1,2,0:T(8,128)S(1)}, f32[2,54,16]{1,2,0:T(8,128)}, u32[]{:S(2)}) copy-start(f32[2,54,16]{1,2,0:T(8,128)} %param.15) | copy-start | bytes 20740
  182.9 42.4 %copy-start.5 = (f32[2,54,16]{1,2,0:T(8,128)}, f32[2,54,16]{1,2,0:T(8,128)S(1)}, u32[]{:S(2)}) copy-start(f32[2,54,16]{1,2,0:T(8,128)S(1)} %get-tuple-element.6) | copy-start | bytes 20740

commit v9 on v8

--- a/solution.py
+++ b/solution.py
@@ -154,8 +154,8 @@
     blocks = weight_grads.reshape(layers, z_hi, z_lo, x_lo, core, rows, lanes)
     blocks = blocks.transpose(4, 3, 2, 1, 0, 5, 6)
     blocks = exchange_and_sum(blocks, "core")
-    blocks = exchange_and_sum(blocks, "x_lo")
-    blocks = exchange_and_sum(blocks, "z_lo")
+    blocks = blocks.reshape((x_lo * z_lo,) + blocks.shape[2:])
+    blocks = exchange_and_sum(blocks, ("x_lo", "z_lo"))
     blocks = blocks.reshape(z_hi, layers, rows, y * x_hi, cols).transpose(0, 3, 1, 2, 4)
     blocks = blocks.reshape((z_hi * y * x_hi,) + blocks.shape[2:])
     blocks = exchange_and_sum(blocks, ("z_hi",) + COLUMN_AXES)

time: 226 us -> 224 us (level)
  blocking collectives: 137 us -> 132 us
  local copies, waits for them, and re-layouts: 47.5 us -> 50.7 us
    all_to_all x4 -> x3, blocking collectives: 97.4 us -> 92.7 us  [exchange_and_sum(): moved = lax.all_to_all(blocks, axes, 0, 0, tiled=True)]
    all_gather x1, blocking collectives: 25.1 us -> 22.1 us  [gather_rows(): gathered = lax.all_gather(fresh_weights, ('z_hi', 'z_lo'), axis=0)]
    all_gather x1, blocking collectives: 14.7 us -> 17.2 us  [gather_rows(): gathered = lax.all_gather(gathered, ('x_lo', 'core'), axis=0)]
where the time goes in v9:
time: 224 us; the launch traced here: 223 us
  blocking collectives  132 us (59%)
  local copies, waits for them, and re-layouts  50.7 us (23%)
  starting transfers between devices  19.1 us (9%)
  matrix products  9.21 us (4%)
  other arithmetic  8.31 us (4%)
    all_to_all x3, blocking collectives, exchange_and_sum(): moved = lax.all_to_all(blocks, axes, 0, 0, tiled=True)  92.7 us
    all_gather x1, blocking collectives, gather_rows(): gathered = lax.all_gather(fresh_weights, ('z_hi', 'z_lo'), axis=0)  22.1 us
    unnamed x76, local copies, waits for them, and re-layouts  21 us
    all_gather x1, blocking collectives, gather_rows(): gathered = lax.all_gather(gathered, ('x_lo', 'core'), axis=0)  17.2 us
    ppermute x3, starting transfers between devices, with_halo(): lax.ppermute(tail, axis, [(i, (i + 1) % count) for i in range(ends)])  15 us
    dot_general x2, local copies, waits for them, and re-layouts, weight_grad(): lax.dot_general(columns, grad_rows, (((0,), (0,)), ((), ())), preferred_e...  7.23 us
    another operation x2, local copies, waits for them, and re-layouts  7.07 us
    conv_general_dilated x3, matrix products, volume_conv(): lax.conv_general_dilated(padded[None], kernel, (1, 1, 1), 'VALID', dimens...  6.98 us
  transfers between devices with their start and end apart: 6, of which 1 were waited for; matrix products, arithmetic and copies ran while one was open for 9% of the time, Pallas kernels for 0%

profile of v9, /device:TPU:1, one launch (start us, length us, event | category | flops | bytes accessed | tf_op | source)
XLA Modules:
  0.0 222.7 jit_solution(8818472988749992532)
XLA Ops:
  0.6 0.9 copy.529
  1.6 5.5 %collective-permute-start = (bf16[8,12,1,128]{3,1,2,0:T(8,128)(2,1)S(1)}, bf16[8,12,1,128]{3,1,2,0:T(8,128)(2,1)S(1)}, u32[]{:S(2)}, u32[]{:S(2)}) collective-permute-start(bf16[8,12,1,128]{3,1,2,0:T(8,128)(2,1)S(1)} %get-tuple-element.63), channel_id=1, source_target_pairs={{0,1},{1,2},{2,3},{3,4},{4,5},{5,6},{6,7},{8,9},{9,10},{10,11},{11... | collective-permute-start | bytes 73736 | tf_op jit(solution)/shard_map/ppermute | solution.py:27
  7.1 1.3 collective-permute-start.1
  8.4 2.8 %fusion.42 = (bf16[1,3456,128]{2,1,0:T(8,128)(2,1)}, bf16[1,3456,128]{2,1,0:T(8,128)(2,1)}) fusion(bf16[2,3456,128]{2,1,0:T(8,128)(2,1)} %param.11), kind=kLoop, calls=%fused_computation.132 | loop fusion | bytes 3538944 | tf_op jit(solution)/shard_map/slice | solution.py:120
  11.6 1.6 collective-permute-done.1
  13.4 0.6 fusion.45
  15.5 2.3 %fusion.10 = f32[1,8,12,4,128]{4,0,3,2,1:T(1,128)S(1)} fusion(bf16[3,3,3,128,128]{4,3,2,1,0:T(8,128)(2,1)S(1)} %bitcast.158, bf16[1,10,14,6,128]{4,2,3,1,0:T(8,128)(2,1)S(1)} %fusion.59), kind=kOutput, calls=%fused_computation.21 | convolution fusion | flops 339738624 | bytes 1296384 | tf_op jit(solution)/shard_map/conv_general_dilated | solution.py:68
  18.0 4.0 %collective-permute-start.2 = (bf16[8,12,1,128]{3,0,2,1:T(8,128)(2,1)S(1)}, bf16[8,12,1,128]{3,0,2,1:T(8,128)(2,1)S(1)}, u32[]{:S(2)}, u32[]{:S(2)}) collective-permute-start(bf16[8,12,1,128]{3,0,2,1:T(8,128)(2,1)S(1)} %get-tuple-element.69), channel_id=1, source_target_pairs={{0,1},{1,2},{2,3},{3,4},{4,5},{5,6},{6,7},{8,9},{9,10},{10,11},{11... | collective-permute-start | bytes 73736 | tf_op jit(solution)/shard_map/ppermute | solution.py:27
  22.0 1.3 collective-permute-start.3
  24.2 2.8 %copy.452 = bf16[3456,384]{1,0:T(8,128)(2,1)} copy(bf16[3456,384]{0,1:T(8,128)(2,1)S(1)} %bitcast.148) | data formatting | bytes 5308416 | tf_op jit(solution)/shard_map/dot_general | solution.py:93
  27.0 2.8 %reshape.275 = bf16[4,4,2,2,54,384]{5,4,3,2,1,0:T(8,128)(2,1)S(1)} reshape(bf16[3456,384]{1,0:T(8,128)(2,1)} %copy.452) | data formatting | bytes 5308416 | tf_op jit(solution)/shard_map/reshape.33
  30.6 0.6 copy-done.1
  31.2 2.4 %fusion.8 = f32[1,8,12,4,128]{4,0,3,2,1:T(1,128)S(1)} fusion(bf16[3,3,3,128,128]{4,3,2,1,0:T(8,128)(2,1)S(1)} %bitcast.156, bf16[1,10,14,6,128]{4,1,3,2,0:T(8,128)(2,1)S(1)} %fusion.58), kind=kOutput, calls=%fused_computation.19 | convolution fusion | flops 339738624 | bytes 1296384 | tf_op jit(solution)/shard_map/conv_general_dilated | solution.py:68
  33.9 5.5 %collective-permute-start.4 = (bf16[8,12,1,128]{3,0,2,1:T(8,128)(2,1)S(1)}, bf16[8,12,1,128]{3,0,2,1:T(8,128)(2,1)S(1)}, u32[]{:S(2)}, u32[]{:S(2)}) collective-permute-start(bf16[8,12,1,128]{3,0,2,1:T(8,128)(2,1)S(1)} %get-tuple-element.65), channel_id=1, source_target_pairs={{0,1},{1,2},{2,3},{3,4},{4,5},{5,6},{6,7},{8,9},{9,10},{10,11},{11... | collective-permute-start | bytes 73736 | tf_op jit(solution)/shard_map/ppermute | solution.py:27
  39.4 1.5 collective-permute-start.5
  40.9 0.6 constant_dynamic-update-slice_fusion.53
  42.2 0.7 constant_dynamic-update-slice_fusion.52
  42.8 0.7 constant_dynamic-update-slice_fusion.51
  43.5 0.7 constant_dynamic-update-slice_fusion.50
  44.2 0.7 constant_dynamic-update-slice_fusion.49
  44.8 0.7 constant_dynamic-update-slice_fusion.48
  45.5 0.7 constant_dynamic-update-slice_fusion.47
  46.1 0.7 constant_dynamic-update-slice_fusion.46
  46.8 0.6 constant_dynamic-update-slice_fusion.45
  47.5 0.7 constant_dynamic-update-slice_fusion.44
  48.1 0.7 constant_dynamic-update-slice_fusion.43
  48.8 0.7 constant_dynamic-update-slice_fusion.42
  49.5 0.7 constant_dynamic-update-slice_fusion.41
  51.0 2.3 %fusion.6 = f32[1,8,12,4,128]{4,0,3,2,1:T(1,128)S(1)} fusion(bf16[3,3,3,128,128]{4,3,2,1,0:T(8,128)(2,1)S(1)} %bitcast.157, bf16[1,10,14,6,128]{4,1,3,2,0:T(8,128)(2,1)S(1)} %fusion.12), kind=kOutput, calls=%fused_computation.17 | convolution fusion | flops 339738624 | bytes 1296384 | tf_op jit(solution)/shard_map/conv_general_dilated | solution.py:68
  53.7 0.8 constant_dynamic-update-slice_fusion.40
  54.5 0.7 constant_dynamic-update-slice_fusion.39
  55.1 0.7 constant_dynamic-update-slice_fusion.38
  55.8 0.7 constant_dynamic-update-slice_fusion.37
  56.5 0.7 constant_dynamic-update-slice_fusion.36
  57.1 0.7 constant_dynamic-update-slice_fusion.35
  57.8 0.7 constant_dynamic-update-slice_fusion.34
  58.5 0.7 constant_dynamic-update-slice_fusion.33
  59.2 0.6 constant_dynamic-update-slice_fusion.32
  59.8 0.7 constant_dynamic-update-slice_fusion.31
  60.5 0.7 constant_dynamic-update-slice_fusion.30
  61.1 0.7 constant_dynamic-update-slice_fusion.29
  61.8 0.7 constant_dynamic-update-slice_fusion.28
  62.5 0.7 constant_dynamic-update-slice_fusion.27
  63.1 4.4 %copy.491 = bf16[3456,384]{1,0:T(8,128)(2,1)} copy(bf16[3456,384]{0,1:T(8,128)(2,1)} %bitcast.69) | data formatting | bytes 5308416 | tf_op jit(solution)/shard_map/dot_general | solution.py:93
  67.6 4.3 %reshape.302 = bf16[4,4,2,2,54,384]{5,4,3,2,1,0:T(8,128)(2,1)} reshape(bf16[3456,384]{1,0:T(8,128)(2,1)} %copy.491) | data formatting | bytes 5308416 | tf_op jit(solution)/shard_map/reshape.37
  71.8 1.1 convolution_bitcast_fusion.1
  73.0 0.7 copy-done
  73.6 1.1 convolution_bitcast_fusion
  75.1 2.3 %copy.494 = f32[2,2,4,4,2,54,128]{6,3,5,4,2,1,0:T(4,128)S(1)} copy(f32[2,2,4,4,2,54,128]{6,5,0,1,2,3,4:T(8,128)S(1)} %maximum_bitcast_fusion) | data formatting | bytes 7077888 | tf_op jit(solution)/shard_map/transpose | solution.py:155
  77.3 10.0 %all_to_all.15 = f32[2,2,4,4,2,54,128]{6,3,5,4,2,1,0:T(4,128)S(1)} all-to-all(f32[2,2,4,4,2,54,128]{6,3,5,4,2,1,0:T(4,128)S(1)} %copy.494), channel_id=1, replica_groups=mesh['z_hi'=4,'z_lo'=4,'x_lo'=2,'core'=2,'y'=4,'x_hi'=2] {'core'}, dimensions={0} | all-to-all | bytes 7077888 | tf_op jit(solution)/shard_map/all_to_all | solution.py:145
  87.3 2.9 %reduce_sum.27 = f32[2,4,4,2,54,128]{5,2,4,3,1,0:T(4,128)} reduce(f32[2,2,4,4,2,54,128]{6,3,5,4,2,1,0:T(4,128)S(1)} %all_to_all.15, f32[]{:T(128)} %constant.8.clone.1), dimensions={0}, to_apply=%region_0.1 | reduce | flops 442368 | bytes 5308420 | tf_op jit(solution)/shard_map/reduce_sum | solution.py:146
  90.3 2.2 copy.496
  92.4 1.1 copy.497
  93.6 47.2 %all_to_all.16 = f32[8,4,2,54,128]{4,1,3,2,0:T(4,128)S(1)} all-to-all(f32[8,4,2,54,128]{4,1,3,2,0:T(4,128)S(1)} %copy.497), channel_id=1, replica_groups=mesh['z_hi'=4,'z_lo'=4,'x_lo'=2,'core'=2,'y'=4,'x_hi'=2] {'x_lo','z_lo'}, dimensions={0} | all-to-all | bytes 3538944 | tf_op jit(solution)/shard_map/all_to_all | solution.py:145
  141.4 0.7 reshape.314
  142.1 35.6 %all_to_all.17 = f32[32,1,1728]{2,1,0:T(1,128)S(1)} all-to-all(f32[32,1,1728]{2,1,0:T(1,128)S(1)} %reshape.314), channel_id=1, replica_groups=mesh['z_hi'=4,'z_lo'=4,'x_lo'=2,'core'=2,'y'=4,'x_hi'=2] {'z_hi','y','x_..., dimensions={0} | all-to-all | bytes 442368 | tf_op jit(solution)/shard_map/all_to_all | solution.py:145
  178.2 1.2 reduce
  179.4 0.7 reshape.315
  180.3 0.6 fusion.41
  180.9 22.1 %all-gather = bf16[32,54,16]{1,2,0:T(8,128)(2,1)S(1)} all-gather(bf16[2,54,16]{1,2,0:T(8,128)(2,1)S(1)} %get-tuple-element.5), channel_id=2, replica_groups=mesh['z_hi'=4,'z_lo'=4,'x_lo'=2,'core'=2,'y'=4,'x_hi'=2] {'z_hi','z_lo'}, dimensions={0}, use_global_device_ids=true | all-gather | bytes 58752 | tf_op jit(solution)/shard_map/all_gather | solution.py:167
  203.0 17.2 %all-gather.1 = bf16[64,2,54,16]{2,3,1,0:T(8,128)(2,1)S(1)} all-gather(bf16[16,2,54,16]{2,3,1,0:T(8,128)(2,1)S(1)} %bitcast.160), channel_id=3, replica_groups=mesh['z_hi'=4,'z_lo'=4,'x_lo'=2,'core'=2,'y'=4,'x_hi'=2] {'x_lo','core'}, dimensions={0}, use_global_device_ids=true | all-gather | bytes 276480 | tf_op jit(solution)/shard_map/all_gather | solution.py:168
  220.2 0.5 copy.500
  220.7 1.4 reshape.307
  222.1 0.6 multiply_add_fusion
  (136 shorter events, 6.9 us)
Async XLA Ops:
  0.6 10.5 %copy-start.6 = (s32[1,8,12,4]{2,3,1,0:T(4,128)S(1)}, s32[1,8,12,4]{2,3,1,0:T(4,128)}, u32[]{:S(2)}) copy-start(s32[1,8,12,4]{2,3,1,0:T(4,128)} %param.9) | copy-start | bytes 4612
  1.6 10.0 %collective-permute-start = (bf16[8,12,1,128]{3,1,2,0:T(8,128)(2,1)S(1)}, bf16[8,12,1,128]{3,1,2,0:T(8,128)(2,1)S(1)}, u32[]{:S(2)}, u32[]{:S(2)}) collective-permute-start(bf16[8,12,1,128]{3,1,2,0:T(8,128)(2,1)S(1)} %get-tuple-element.63), channel_id=1, source_target_pairs={{0,1},{1,2},{2,3},{3,4},{4,5},{5,6},{6,7},{8,9},{9,10},{10,11},{11... | collective-permute-start | bytes 73736 | tf_op jit(solution)/shard_map/ppermute | solution.py:27
  7.1 6.2 %collective-permute-start.1 = (bf16[8,12,1,128]{3,1,2,0:T(8,128)(2,1)S(1)}, bf16[8,12,1,128]{3,1,2,0:T(8,128)(2,1)S(1)}, u32[]{:S(2)}, u32[]{:S(2)}) collective-permute-start(bf16[8,12,1,128]{3,1,2,0:T(8,128)(2,1)S(1)} %get-tuple-element.64), channel_id=1, source_target_pairs={{1,0},{2,1},{3,2},{4,3},{5,4},{6,5},{7,6},{9,8},{10,9},{11,10},{12... | collective-permute-start | bytes 73736 | tf_op jit(solution)/shard_map/ppermute | solution.py:29
  14.4 1.2 copy-start.2
  17.8 5.9 %copy-start.3 = (bf16[1,8,12,4,128]{4,3,2,1,0:T(4,128)(2,1)S(1)}, bf16[1,8,12,4,128]{4,3,2,1,0:T(4,128)(2,1)}, u32[]{:S(2)}) copy-start(bf16[1,8,12,4,128]{4,3,2,1,0:T(4,128)(2,1)} %param.8) | copy-start | bytes 294916
  18.0 11.8 %collective-permute-start.2 = (bf16[8,12,1,128]{3,0,2,1:T(8,128)(2,1)S(1)}, bf16[8,12,1,128]{3,0,2,1:T(8,128)(2,1)S(1)}, u32[]{:S(2)}, u32[]{:S(2)}) collective-permute-start(bf16[8,12,1,128]{3,0,2,1:T(8,128)(2,1)S(1)} %get-tuple-element.69), channel_id=1, source_target_pairs={{0,1},{1,2},{2,3},{3,4},{4,5},{5,6},{6,7},{8,9},{9,10},{10,11},{11... | collective-permute-start | bytes 73736 | tf_op jit(solution)/shard_map/ppermute | solution.py:27
  22.0 7.8 %collective-permute-start.3 = (bf16[8,12,1,128]{3,0,2,1:T(8,128)(2,1)S(1)}, bf16[8,12,1,128]{3,0,2,1:T(8,128)(2,1)S(1)}, u32[]{:S(2)}, u32[]{:S(2)}) collective-permute-start(bf16[8,12,1,128]{3,0,2,1:T(8,128)(2,1)S(1)} %get-tuple-element.70), channel_id=1, source_target_pairs={{1,0},{2,1},{3,2},{4,3},{5,4},{6,5},{7,6},{9,8},{10,9},{11,10},{12... | collective-permute-start | bytes 73736 | tf_op jit(solution)/shard_map/ppermute | solution.py:29
  30.0 1.2 copy-start.1
  30.6 3.0 %copy-start.4 = (bf16[1,8,12,4,128]{4,3,2,1,0:T(4,128)(2,1)S(1)}, bf16[1,8,12,4,128]{4,3,2,1,0:T(4,128)(2,1)}, u32[]{:S(2)}) copy-start(bf16[1,8,12,4,128]{4,3,2,1,0:T(4,128)(2,1)} %param.10) | copy-start | bytes 294916
  33.9 16.9 %collective-permute-start.4 = (bf16[8,12,1,128]{3,0,2,1:T(8,128)(2,1)S(1)}, bf16[8,12,1,128]{3,0,2,1:T(8,128)(2,1)S(1)}, u32[]{:S(2)}, u32[]{:S(2)}) collective-permute-start(bf16[8,12,1,128]{3,0,2,1:T(8,128)(2,1)S(1)} %get-tuple-element.65), channel_id=1, source_target_pairs={{0,1},{1,2},{2,3},{3,4},{4,5},{5,6},{6,7},{8,9},{9,10},{10,11},{11... | collective-permute-start | bytes 73736 | tf_op jit(solution)/shard_map/ppermute | solution.py:27
  39.4 11.4 %collective-permute-start.5 = (bf16[8,12,1,128]{3,0,2,1:T(8,128)(2,1)S(1)}, bf16[8,12,1,128]{3,0,2,1:T(8,128)(2,1)S(1)}, u32[]{:S(2)}, u32[]{:S(2)}) collective-permute-start(bf16[8,12,1,128]{3,0,2,1:T(8,128)(2,1)S(1)} %get-tuple-element.66), channel_id=1, source_target_pairs={{1,0},{2,1},{3,2},{4,3},{5,4},{6,5},{7,6},{9,8},{10,9},{11,10},{12... | collective-permute-start | bytes 73736 | tf_op jit(solution)/shard_map/ppermute | solution.py:29
  71.8 1.8 copy-start
  141.1 39.2 %copy-start.7 = (f32[2,54,16]{1,2,0:T(8,128)S(1)}, f32[2,54,16]{1,2,0:T(8,128)}, u32[]{:S(2)}) copy-start(f32[2,54,16]{1,2,0:T(8,128)} %param.12) | copy-start | bytes 20740
  141.1 39.1 %copy-start.8 = (f32[2,54,16]{1,2,0:T(8,128)S(1)}, f32[2,54,16]{1,2,0:T(8,128)}, u32[]{:S(2)}) copy-start(f32[2,54,16]{1,2,0:T(8,128)} %param.13) | copy-start | bytes 20740
  141.1 39.1 %copy-start.9 = (f32[2,54,16]{1,2,0:T(8,128)S(1)}, f32[2,54,16]{1,2,0:T(8,128)}, u32[]{:S(2)}) copy-start(f32[2,54,16]{1,2,0:T(8,128)} %param.14) | copy-start | bytes 20740
  142.1 80.0 %copy-start.10 = (f32[2,54,16]{1,2,0:T(8,128)S(1)}, f32[2,54,16]{1,2,0:T(8,128)}, u32[]{:S(2)}) copy-start(f32[2,54,16]{1,2,0:T(8,128)} %param.15) | copy-start | bytes 20740
  180.9 41.8 %copy-start.5 = (f32[2,54,16]{1,2,0:T(8,128)}, f32[2,54,16]{1,2,0:T(8,128)S(1)}, u32[]{:S(2)}) copy-start(f32[2,54,16]{1,2,0:T(8,128)S(1)} %get-tuple-element.6) | copy-start | bytes 20740

commit v10 on v9

--- a/solution.py
+++ b/solution.py
@@ -164,13 +164,9 @@
 
 def gather_rows(fresh_weights):
     layers, rows, cols = fresh_weights.shape
-    gathered = lax.all_gather(fresh_weights, ("z_hi", "z_lo"), axis=0)
-    gathered = lax.all_gather(gathered, ("x_lo", "core"), axis=0)
-    gathered = gathered.reshape((-1,) + gathered.shape[1:])
-    x_lo, core = lax.axis_size("x_lo"), lax.axis_size("core")
-    gathered = gathered.reshape((x_lo, core) + gathered.shape[1:])
-    gathered = gathered.transpose(3, 2, 0, 1, 4, 5)
-    return gathered.reshape(layers, -1, cols)
+    gathered = lax.all_gather(fresh_weights, "z_hi", axis=0)
+    gathered = lax.all_gather(gathered, ("z_lo", "x_lo", "core"), axis=0)
+    return gathered.transpose(2, 1, 0, 3, 4).reshape(layers, -1, cols)
 
 
 def solution(mesh):

time: 224 us -> 226 us (level)
    all_gather x2, blocking collectives: 39.3 us -> 41.8 us  [the longest x1 26.9 us: gather_rows(): gathered = lax.all_gather(gathered, ('z_lo', 'x_lo', 'core'), axis=0)]
where the time goes in v10:
time: 226 us; the launch traced here: 225 us
  blocking collectives  134 us (59%)
  local copies, waits for them, and re-layouts  50.5 us (22%)
  starting transfers between devices  19.1 us (8%)
  matrix products  9.21 us (4%)
  other arithmetic  8.31 us (4%)
    all_to_all x3, blocking collectives, exchange_and_sum(): moved = lax.all_to_all(blocks, axes, 0, 0, tiled=True)  92.7 us
    all_gather x1, blocking collectives, gather_rows(): gathered = lax.all_gather(gathered, ('z_lo', 'x_lo', 'core'), axis=0)  26.9 us
    unnamed x76, local copies, waits for them, and re-layouts  21 us
    ppermute x3, starting transfers between devices, with_halo(): lax.ppermute(tail, axis, [(i, (i + 1) % count) for i in range(ends)])  15 us
    all_gather x1, blocking collectives, gather_rows(): gathered = lax.all_gather(fresh_weights, 'z_hi', axis=0)  14.8 us
    dot_general x2, local copies, waits for them, and re-layouts, weight_grad(): lax.dot_general(columns, grad_rows, (((0,), (0,)), ((), ())), preferred_e...  7.23 us
    another operation x2, local copies, waits for them, and re-layouts  7.07 us
    conv_general_dilated x3, matrix products, volume_conv(): lax.conv_general_dilated(padded[None], kernel, (1, 1, 1), 'VALID', dimens...  6.98 us
  transfers between devices with their start and end apart: 6, of which 1 were waited for; matrix products, arithmetic and copies ran while one was open for 9% of the time, Pallas kernels for 0%

profile of v10, /device:TPU:1, one launch (start us, length us, event | category | flops | bytes accessed | tf_op | source)
XLA Modules:
  0.0 225.0 jit_solution(10277134481450333494)
XLA Ops:
  0.6 0.9 copy.529
  1.6 5.5 %collective-permute-start = (bf16[8,12,1,128]{3,1,2,0:T(8,128)(2,1)S(1)}, bf16[8,12,1,128]{3,1,2,0:T(8,128)(2,1)S(1)}, u32[]{:S(2)}, u32[]{:S(2)}) collective-permute-start(bf16[8,12,1,128]{3,1,2,0:T(8,128)(2,1)S(1)} %get-tuple-element.63), channel_id=1, source_target_pairs={{0,1},{1,2},{2,3},{3,4},{4,5},{5,6},{6,7},{8,9},{9,10},{10,11},{11... | collective-permute-start | bytes 73736 | tf_op jit(solution)/shard_map/ppermute | solution.py:27
  7.1 1.3 collective-permute-start.1
  8.4 2.8 %fusion.42 = (bf16[1,3456,128]{2,1,0:T(8,128)(2,1)}, bf16[1,3456,128]{2,1,0:T(8,128)(2,1)}) fusion(bf16[2,3456,128]{2,1,0:T(8,128)(2,1)} %param.11), kind=kLoop, calls=%fused_computation.132 | loop fusion | bytes 3538944 | tf_op jit(solution)/shard_map/slice | solution.py:120
  11.6 1.6 collective-permute-done.1
  13.4 0.6 fusion.45
  15.5 2.3 %fusion.10 = f32[1,8,12,4,128]{4,0,3,2,1:T(1,128)S(1)} fusion(bf16[3,3,3,128,128]{4,3,2,1,0:T(8,128)(2,1)S(1)} %bitcast.160, bf16[1,10,14,6,128]{4,2,3,1,0:T(8,128)(2,1)S(1)} %fusion.59), kind=kOutput, calls=%fused_computation.21 | convolution fusion | flops 339738624 | bytes 1296384 | tf_op jit(solution)/shard_map/conv_general_dilated | solution.py:68
  18.0 4.0 %collective-permute-start.2 = (bf16[8,12,1,128]{3,0,2,1:T(8,128)(2,1)S(1)}, bf16[8,12,1,128]{3,0,2,1:T(8,128)(2,1)S(1)}, u32[]{:S(2)}, u32[]{:S(2)}) collective-permute-start(bf16[8,12,1,128]{3,0,2,1:T(8,128)(2,1)S(1)} %get-tuple-element.69), channel_id=1, source_target_pairs={{0,1},{1,2},{2,3},{3,4},{4,5},{5,6},{6,7},{8,9},{9,10},{10,11},{11... | collective-permute-start | bytes 73736 | tf_op jit(solution)/shard_map/ppermute | solution.py:27
  22.0 1.3 collective-permute-start.3
  24.2 2.8 %copy.452 = bf16[3456,384]{1,0:T(8,128)(2,1)} copy(bf16[3456,384]{0,1:T(8,128)(2,1)S(1)} %bitcast.150) | data formatting | bytes 5308416 | tf_op jit(solution)/shard_map/dot_general | solution.py:93
  27.0 2.8 %reshape.272 = bf16[4,4,2,2,54,384]{5,4,3,2,1,0:T(8,128)(2,1)S(1)} reshape(bf16[3456,384]{1,0:T(8,128)(2,1)} %copy.452) | data formatting | bytes 5308416 | tf_op jit(solution)/shard_map/reshape.33
  30.6 0.6 copy-done.1
  31.2 2.4 %fusion.8 = f32[1,8,12,4,128]{4,0,3,2,1:T(1,128)S(1)} fusion(bf16[3,3,3,128,128]{4,3,2,1,0:T(8,128)(2,1)S(1)} %bitcast.158, bf16[1,10,14,6,128]{4,1,3,2,0:T(8,128)(2,1)S(1)} %fusion.58), kind=kOutput, calls=%fused_computation.19 | convolution fusion | flops 339738624 | bytes 1296384 | tf_op jit(solution)/shard_map/conv_general_dilated | solution.py:68
  33.9 5.5 %collective-permute-start.4 = (bf16[8,12,1,128]{3,0,2,1:T(8,128)(2,1)S(1)}, bf16[8,12,1,128]{3,0,2,1:T(8,128)(2,1)S(1)}, u32[]{:S(2)}, u32[]{:S(2)}) collective-permute-start(bf16[8,12,1,128]{3,0,2,1:T(8,128)(2,1)S(1)} %get-tuple-element.65), channel_id=1, source_target_pairs={{0,1},{1,2},{2,3},{3,4},{4,5},{5,6},{6,7},{8,9},{9,10},{10,11},{11... | collective-permute-start | bytes 73736 | tf_op jit(solution)/shard_map/ppermute | solution.py:27
  39.4 1.5 collective-permute-start.5
  40.9 0.6 constant_dynamic-update-slice_fusion.53
  42.2 0.7 constant_dynamic-update-slice_fusion.52
  42.8 0.7 constant_dynamic-update-slice_fusion.51
  43.5 0.7 constant_dynamic-update-slice_fusion.50
  44.2 0.7 constant_dynamic-update-slice_fusion.49
  44.8 0.7 constant_dynamic-update-slice_fusion.48
  45.5 0.7 constant_dynamic-update-slice_fusion.47
  46.1 0.7 constant_dynamic-update-slice_fusion.46
  46.8 0.6 constant_dynamic-update-slice_fusion.45
  47.5 0.7 constant_dynamic-update-slice_fusion.44
  48.1 0.7 constant_dynamic-update-slice_fusion.43
  48.8 0.7 constant_dynamic-update-slice_fusion.42
  49.5 0.7 constant_dynamic-update-slice_fusion.41
  51.0 2.3 %fusion.6 = f32[1,8,12,4,128]{4,0,3,2,1:T(1,128)S(1)} fusion(bf16[3,3,3,128,128]{4,3,2,1,0:T(8,128)(2,1)S(1)} %bitcast.159, bf16[1,10,14,6,128]{4,1,3,2,0:T(8,128)(2,1)S(1)} %fusion.12), kind=kOutput, calls=%fused_computation.17 | convolution fusion | flops 339738624 | bytes 1296384 | tf_op jit(solution)/shard_map/conv_general_dilated | solution.py:68
  53.7 0.8 constant_dynamic-update-slice_fusion.40
  54.5 0.7 constant_dynamic-update-slice_fusion.39
  55.1 0.7 constant_dynamic-update-slice_fusion.38
  55.8 0.7 constant_dynamic-update-slice_fusion.37
  56.5 0.7 constant_dynamic-update-slice_fusion.36
  57.1 0.7 constant_dynamic-update-slice_fusion.35
  57.8 0.7 constant_dynamic-update-slice_fusion.34
  58.5 0.7 constant_dynamic-update-slice_fusion.33
  59.2 0.6 constant_dynamic-update-slice_fusion.32
  59.8 0.7 constant_dynamic-update-slice_fusion.31
  60.5 0.7 constant_dynamic-update-slice_fusion.30
  61.1 0.7 constant_dynamic-update-slice_fusion.29
  61.8 0.7 constant_dynamic-update-slice_fusion.28
  62.5 0.7 constant_dynamic-update-slice_fusion.27
  63.1 4.4 %copy.491 = bf16[3456,384]{1,0:T(8,128)(2,1)} copy(bf16[3456,384]{0,1:T(8,128)(2,1)} %bitcast.69) | data formatting | bytes 5308416 | tf_op jit(solution)/shard_map/dot_general | solution.py:93
  67.6 4.3 %reshape.299 = bf16[4,4,2,2,54,384]{5,4,3,2,1,0:T(8,128)(2,1)} reshape(bf16[3456,384]{1,0:T(8,128)(2,1)} %copy.491) | data formatting | bytes 5308416 | tf_op jit(solution)/shard_map/reshape.37
  71.8 1.1 convolution_bitcast_fusion.1
  73.0 0.7 copy-done
  73.6 1.1 convolution_bitcast_fusion
  75.1 2.3 %copy.494 = f32[2,2,4,4,2,54,128]{6,3,5,4,2,1,0:T(4,128)S(1)} copy(f32[2,2,4,4,2,54,128]{6,5,0,1,2,3,4:T(8,128)S(1)} %maximum_bitcast_fusion) | data formatting | bytes 7077888 | tf_op jit(solution)/shard_map/transpose | solution.py:155
  77.3 10.0 %all_to_all.15 = f32[2,2,4,4,2,54,128]{6,3,5,4,2,1,0:T(4,128)S(1)} all-to-all(f32[2,2,4,4,2,54,128]{6,3,5,4,2,1,0:T(4,128)S(1)} %copy.494), channel_id=1, replica_groups=mesh['z_hi'=4,'z_lo'=4,'x_lo'=2,'core'=2,'y'=4,'x_hi'=2] {'core'}, dimensions={0} | all-to-all | bytes 7077888 | tf_op jit(solution)/shard_map/all_to_all | solution.py:145
  87.3 2.9 %reduce_sum.27 = f32[2,4,4,2,54,128]{5,2,4,3,1,0:T(4,128)} reduce(f32[2,2,4,4,2,54,128]{6,3,5,4,2,1,0:T(4,128)S(1)} %all_to_all.15, f32[]{:T(128)} %constant.8.clone.1), dimensions={0}, to_apply=%region_0.1 | reduce | flops 442368 | bytes 5308420 | tf_op jit(solution)/shard_map/reduce_sum | solution.py:146
  90.3 2.2 copy.496
  92.4 1.1 copy.497
  93.6 47.2 %all_to_all.16 = f32[8,4,2,54,128]{4,1,3,2,0:T(4,128)S(1)} all-to-all(f32[8,4,2,54,128]{4,1,3,2,0:T(4,128)S(1)} %copy.497), channel_id=1, replica_groups=mesh['z_hi'=4,'z_lo'=4,'x_lo'=2,'core'=2,'y'=4,'x_hi'=2] {'x_lo','z_lo'}, dimensions={0} | all-to-all | bytes 3538944 | tf_op jit(solution)/shard_map/all_to_all | solution.py:145
  141.4 0.7 reshape.309
  142.1 35.6 %all_to_all.17 = f32[32,1,1728]{2,1,0:T(1,128)S(1)} all-to-all(f32[32,1,1728]{2,1,0:T(1,128)S(1)} %reshape.309), channel_id=1, replica_groups=mesh['z_hi'=4,'z_lo'=4,'x_lo'=2,'core'=2,'y'=4,'x_hi'=2] {'z_hi','y','x_..., dimensions={0} | all-to-all | bytes 442368 | tf_op jit(solution)/shard_map/all_to_all | solution.py:145
  177.7 0.5 broadcast.246
  178.2 1.2 reduce
  179.4 0.7 reshape.310
  180.3 0.6 fusion.41
  180.9 14.8 %all-gather = bf16[8,54,16]{1,2,0:T(8,128)(2,1)S(1)} all-gather(bf16[2,54,16]{1,2,0:T(8,128)(2,1)S(1)} %get-tuple-element.5), channel_id=2, replica_groups=mesh['z_hi'=4,'z_lo'=4,'x_lo'=2,'core'=2,'y'=4,'x_hi'=2] {'z_hi'}, dimensions={0}, use_global_device_ids=true | all-gather | bytes 17280 | tf_op jit(solution)/shard_map/all_gather | solution.py:167
  195.7 26.9 %all-gather.1 = bf16[64,2,54,16]{2,3,1,0:T(8,128)(2,1)S(1)} all-gather(bf16[4,2,54,16]{2,3,1,0:T(8,128)(2,1)S(1)} %bitcast.217), channel_id=3, replica_groups=mesh['z_hi'=4,'z_lo'=4,'x_lo'=2,'core'=2,'y'=4,'x_hi'=2] {'z_lo','x_lo',..., dimensions={0}, use_global_device_ids=true | all-gather | bytes 235008 | tf_op jit(solution)/shard_map/all_gather | solution.py:168
  223.0 1.4 reshape.303
  224.3 0.6 multiply_add_fusion
  (136 shorter events, 6.8 us)
Async XLA Ops:
  0.6 10.5 %copy-start.6 = (s32[1,8,12,4]{2,3,1,0:T(4,128)S(1)}, s32[1,8,12,4]{2,3,1,0:T(4,128)}, u32[]{:S(2)}) copy-start(s32[1,8,12,4]{2,3,1,0:T(4,128)} %param.9) | copy-start | bytes 4612
  1.6 10.0 %collective-permute-start = (bf16[8,12,1,128]{3,1,2,0:T(8,128)(2,1)S(1)}, bf16[8,12,1,128]{3,1,2,0:T(8,128)(2,1)S(1)}, u32[]{:S(2)}, u32[]{:S(2)}) collective-permute-start(bf16[8,12,1,128]{3,1,2,0:T(8,128)(2,1)S(1)} %get-tuple-element.63), channel_id=1, source_target_pairs={{0,1},{1,2},{2,3},{3,4},{4,5},{5,6},{6,7},{8,9},{9,10},{10,11},{11... | collective-permute-start | bytes 73736 | tf_op jit(solution)/shard_map/ppermute | solution.py:27
  7.1 6.2 %collective-permute-start.1 = (bf16[8,12,1,128]{3,1,2,0:T(8,128)(2,1)S(1)}, bf16[8,12,1,128]{3,1,2,0:T(8,128)(2,1)S(1)}, u32[]{:S(2)}, u32[]{:S(2)}) collective-permute-start(bf16[8,12,1,128]{3,1,2,0:T(8,128)(2,1)S(1)} %get-tuple-element.64), channel_id=1, source_target_pairs={{1,0},{2,1},{3,2},{4,3},{5,4},{6,5},{7,6},{9,8},{10,9},{11,10},{12... | collective-permute-start | bytes 73736 | tf_op jit(solution)/shard_map/ppermute | solution.py:29
  14.4 1.2 copy-start.2
  17.8 5.9 %copy-start.3 = (bf16[1,8,12,4,128]{4,3,2,1,0:T(4,128)(2,1)S(1)}, bf16[1,8,12,4,128]{4,3,2,1,0:T(4,128)(2,1)}, u32[]{:S(2)}) copy-start(bf16[1,8,12,4,128]{4,3,2,1,0:T(4,128)(2,1)} %param.8) | copy-start | bytes 294916
  18.0 11.8 %collective-permute-start.2 = (bf16[8,12,1,128]{3,0,2,1:T(8,128)(2,1)S(1)}, bf16[8,12,1,128]{3,0,2,1:T(8,128)(2,1)S(1)}, u32[]{:S(2)}, u32[]{:S(2)}) collective-permute-start(bf16[8,12,1,128]{3,0,2,1:T(8,128)(2,1)S(1)} %get-tuple-element.69), channel_id=1, source_target_pairs={{0,1},{1,2},{2,3},{3,4},{4,5},{5,6},{6,7},{8,9},{9,10},{10,11},{11... | collective-permute-start | bytes 73736 | tf_op jit(solution)/shard_map/ppermute | solution.py:27
  22.0 7.8 %collective-permute-start.3 = (bf16[8,12,1,128]{3,0,2,1:T(8,128)(2,1)S(1)}, bf16[8,12,1,128]{3,0,2,1:T(8,128)(2,1)S(1)}, u32[]{:S(2)}, u32[]{:S(2)}) collective-permute-start(bf16[8,12,1,128]{3,0,2,1:T(8,128)(2,1)S(1)} %get-tuple-element.70), channel_id=1, source_target_pairs={{1,0},{2,1},{3,2},{4,3},{5,4},{6,5},{7,6},{9,8},{10,9},{11,10},{12... | collective-permute-start | bytes 73736 | tf_op jit(solution)/shard_map/ppermute | solution.py:29
  30.0 1.2 copy-start.1
  30.6 3.0 %copy-start.4 = (bf16[1,8,12,4,128]{4,3,2,1,0:T(4,128)(2,1)S(1)}, bf16[1,8,12,4,128]{4,3,2,1,0:T(4,128)(2,1)}, u32[]{:S(2)}) copy-start(bf16[1,8,12,4,128]{4,3,2,1,0:T(4,128)(2,1)} %param.10) | copy-start | bytes 294916
  33.9 16.9 %collective-permute-start.4 = (bf16[8,12,1,128]{3,0,2,1:T(8,128)(2,1)S(1)}, bf16[8,12,1,128]{3,0,2,1:T(8,128)(2,1)S(1)}, u32[]{:S(2)}, u32[]{:S(2)}) collective-permute-start(bf16[8,12,1,128]{3,0,2,1:T(8,128)(2,1)S(1)} %get-tuple-element.65), channel_id=1, source_target_pairs={{0,1},{1,2},{2,3},{3,4},{4,5},{5,6},{6,7},{8,9},{9,10},{10,11},{11... | collective-permute-start | bytes 73736 | tf_op jit(solution)/shard_map/ppermute | solution.py:27
  39.4 11.4 %collective-permute-start.5 = (bf16[8,12,1,128]{3,0,2,1:T(8,128)(2,1)S(1)}, bf16[8,12,1,128]{3,0,2,1:T(8,128)(2,1)S(1)}, u32[]{:S(2)}, u32[]{:S(2)}) collective-permute-start(bf16[8,12,1,128]{3,0,2,1:T(8,128)(2,1)S(1)} %get-tuple-element.66), channel_id=1, source_target_pairs={{1,0},{2,1},{3,2},{4,3},{5,4},{6,5},{7,6},{9,8},{10,9},{11,10},{12... | collective-permute-start | bytes 73736 | tf_op jit(solution)/shard_map/ppermute | solution.py:29
  71.8 1.8 copy-start
  141.1 39.1 %copy-start.7 = (f32[2,54,16]{1,2,0:T(8,128)S(1)}, f32[2,54,16]{1,2,0:T(8,128)}, u32[]{:S(2)}) copy-start(f32[2,54,16]{1,2,0:T(8,128)} %param.12) | copy-start | bytes 20740
  141.1 39.1 %copy-start.8 = (f32[2,54,16]{1,2,0:T(8,128)S(1)}, f32[2,54,16]{1,2,0:T(8,128)}, u32[]{:S(2)}) copy-start(f32[2,54,16]{1,2,0:T(8,128)} %param.13) | copy-start | bytes 20740
  141.1 39.1 %copy-start.9 = (f32[2,54,16]{1,2,0:T(8,128)S(1)}, f32[2,54,16]{1,2,0:T(8,128)}, u32[]{:S(2)}) copy-start(f32[2,54,16]{1,2,0:T(8,128)} %param.14) | copy-start | bytes 20740
  141.4 82.9 %copy-start.10 = (f32[2,54,16]{1,2,0:T(8,128)S(1)}, f32[2,54,16]{1,2,0:T(8,128)}, u32[]{:S(2)}) copy-start(f32[2,54,16]{1,2,0:T(8,128)} %param.15) | copy-start | bytes 20740
  180.9 44.1 %copy-start.5 = (f32[2,54,16]{1,2,0:T(8,128)}, f32[2,54,16]{1,2,0:T(8,128)S(1)}, u32[]{:S(2)}) copy-start(f32[2,54,16]{1,2,0:T(8,128)S(1)} %get-tuple-element.6) | copy-start | bytes 20740

commit v11 on v10

--- a/solution.py
+++ b/solution.py
@@ -164,9 +164,11 @@
 
 def gather_rows(fresh_weights):
     layers, rows, cols = fresh_weights.shape
-    gathered = lax.all_gather(fresh_weights, "z_hi", axis=0)
-    gathered = lax.all_gather(gathered, ("z_lo", "x_lo", "core"), axis=0)
-    return gathered.transpose(2, 1, 0, 3, 4).reshape(layers, -1, cols)
+    z_hi, z_lo, x_lo, core = (lax.axis_size(name) for name in ROW_AXES)
+    gathered = lax.all_gather(fresh_weights, ("x_lo", "z_lo"), axis=0)
+    gathered = lax.all_gather(gathered, ("z_hi", "core"), axis=0)
+    gathered = gathered.reshape((z_hi, core, x_lo, z_lo) + fresh_weights.shape)
+    return gathered.transpose(4, 0, 3, 2, 1, 5, 6).reshape(layers, -1, cols)
 
 
 def solution(mesh):

time: 226 us -> 241 us (1.066)
  blocking collectives: 134 us -> 149 us
    all_gather x2, blocking collectives: 41.8 us -> 56.3 us  [the longest x1 31.8 us: gather_rows(): gathered = lax.all_gather(gathered, ('z_hi', 'core'), axis=0)]
  transfers between devices with their start and end apart: 6 -> 6, of which waited for: 1 -> 1; matrix products, arithmetic and copies ran while one was open for 9% -> 8% of each run, Pallas kernels for 0% -> 0%
where the time goes in v11:
time: 241 us; the launch traced here: 240 us
  blocking collectives  149 us (62%)
  local copies, waits for them, and re-layouts  50.7 us (21%)
  starting transfers between devices  19.1 us (8%)
  matrix products  9.21 us (4%)
  other arithmetic  8.31 us (3%)
    all_to_all x3, blocking collectives, exchange_and_sum(): moved = lax.all_to_all(blocks, axes, 0, 0, tiled=True)  92.7 us
    all_gather x1, blocking collectives, gather_rows(): gathered = lax.all_gather(gathered, ('z_hi', 'core'), axis=0)  31.8 us
    all_gather x1, blocking collectives, gather_rows(): gathered = lax.all_gather(fresh_weights, ('x_lo', 'z_lo'), axis=0)  24.5 us
    unnamed x76, local copies, waits for them, and re-layouts  21 us
    ppermute x3, starting transfers between devices, with_halo(): lax.ppermute(tail, axis, [(i, (i + 1) % count) for i in range(ends)])  15 us
    dot_general x2, local copies, waits for them, and re-layouts, weight_grad(): lax.dot_general(columns, grad_rows, (((0,), (0,)), ((), ())), preferred_e...  7.23 us
    another operation x2, local copies, waits for them, and re-layouts  7.07 us
    conv_general_dilated x3, matrix products, volume_conv(): lax.conv_general_dilated(padded[None], kernel, (1, 1, 1), 'VALID', dimens...  6.98 us
  transfers between devices with their start and end apart: 6, of which 1 were waited for; matrix products, arithmetic and copies ran while one was open for 8% of the time, Pallas kernels for 0%

profile of v11, /device:TPU:1, one launch (start us, length us, event | category | flops | bytes accessed | tf_op | source)
XLA Modules:
  0.0 239.7 jit_solution(9061179788854772521)
XLA Ops:
  0.6 0.9 copy.529
  1.6 5.5 %collective-permute-start = (bf16[8,12,1,128]{3,1,2,0:T(8,128)(2,1)S(1)}, bf16[8,12,1,128]{3,1,2,0:T(8,128)(2,1)S(1)}, u32[]{:S(2)}, u32[]{:S(2)}) collective-permute-start(bf16[8,12,1,128]{3,1,2,0:T(8,128)(2,1)S(1)} %get-tuple-element.63), channel_id=1, source_target_pairs={{0,1},{1,2},{2,3},{3,4},{4,5},{5,6},{6,7},{8,9},{9,10},{10,11},{11... | collective-permute-start | bytes 73736 | tf_op jit(solution)/shard_map/ppermute | solution.py:27
  7.1 1.3 collective-permute-start.1
  8.4 2.8 %fusion.42 = (bf16[1,3456,128]{2,1,0:T(8,128)(2,1)}, bf16[1,3456,128]{2,1,0:T(8,128)(2,1)}) fusion(bf16[2,3456,128]{2,1,0:T(8,128)(2,1)} %param.11), kind=kLoop, calls=%fused_computation.132 | loop fusion | bytes 3538944 | tf_op jit(solution)/shard_map/slice | solution.py:120
  11.6 1.6 collective-permute-done.1
  13.4 0.6 fusion.45
  15.5 2.3 fusion.10
  18.0 4.0 %collective-permute-start.2 = (bf16[8,12,1,128]{3,0,2,1:T(8,128)(2,1)S(1)}, bf16[8,12,1,128]{3,0,2,1:T(8,128)(2,1)S(1)}, u32[]{:S(2)}, u32[]{:S(2)}) collective-permute-start(bf16[8,12,1,128]{3,0,2,1:T(8,128)(2,1)S(1)} %get-tuple-element.69), channel_id=1, source_target_pairs={{0,1},{1,2},{2,3},{3,4},{4,5},{5,6},{6,7},{8,9},{9,10},{10,11},{11... | collective-permute-start | bytes 73736 | tf_op jit(solution)/shard_map/ppermute | solution.py:27
  22.0 1.3 collective-permute-start.3
  24.2 2.8 %copy.452 = bf16[3456,384]{1,0:T(8,128)(2,1)} copy(bf16[3456,384]{0,1:T(8,128)(2,1)S(1)} %bitcast.148) | data formatting | bytes 5308416 | tf_op jit(solution)/shard_map/dot_general | solution.py:93
  27.0 2.8 %reshape.275 = bf16[4,4,2,2,54,384]{5,4,3,2,1,0:T(8,128)(2,1)S(1)} reshape(bf16[3456,384]{1,0:T(8,128)(2,1)} %copy.452) | data formatting | bytes 5308416 | tf_op jit(solution)/shard_map/reshape.33
  30.6 0.6 copy-done.1
  31.2 2.4 fusion.8
  33.9 5.5 %collective-permute-start.4 = (bf16[8,12,1,128]{3,0,2,1:T(8,128)(2,1)S(1)}, bf16[8,12,1,128]{3,0,2,1:T(8,128)(2,1)S(1)}, u32[]{:S(2)}, u32[]{:S(2)}) collective-permute-start(bf16[8,12,1,128]{3,0,2,1:T(8,128)(2,1)S(1)} %get-tuple-element.65), channel_id=1, source_target_pairs={{0,1},{1,2},{2,3},{3,4},{4,5},{5,6},{6,7},{8,9},{9,10},{10,11},{11... | collective-permute-start | bytes 73736 | tf_op jit(solution)/shard_map/ppermute | solution.py:27
  39.4 1.5 collective-permute-start.5
  40.9 0.6 constant_dynamic-update-slice_fusion.53
  42.2 0.7 constant_dynamic-update-slice_fusion.52
  42.8 0.7 constant_dynamic-update-slice_fusion.51
  43.5 0.7 constant_dynamic-update-slice_fusion.50
  44.2 0.7 constant_dynamic-update-slice_fusion.49
  44.8 0.7 constant_dynamic-update-slice_fusion.48
  45.5 0.7 constant_dynamic-update-slice_fusion.47
  46.1 0.7 constant_dynamic-update-slice_fusion.46
  46.8 0.6 constant_dynamic-update-slice_fusion.45
  47.5 0.7 constant_dynamic-update-slice_fusion.44
  48.1 0.7 constant_dynamic-update-slice_fusion.43
  48.8 0.7 constant_dynamic-update-slice_fusion.42
  49.5 0.7 constant_dynamic-update-slice_fusion.41
  51.0 2.3 fusion.6
  53.7 0.8 constant_dynamic-update-slice_fusion.40
  54.5 0.7 constant_dynamic-update-slice_fusion.39
  55.1 0.7 constant_dynamic-update-slice_fusion.38
  55.8 0.7 constant_dynamic-update-slice_fusion.37
  56.5 0.7 constant_dynamic-update-slice_fusion.36
  57.1 0.7 constant_dynamic-update-slice_fusion.35
  57.8 0.7 constant_dynamic-update-slice_fusion.34
  58.5 0.7 constant_dynamic-update-slice_fusion.33
  59.2 0.6 constant_dynamic-update-slice_fusion.32
  59.8 0.7 constant_dynamic-update-slice_fusion.31
  60.5 0.7 constant_dynamic-update-slice_fusion.30
  61.1 0.7 constant_dynamic-update-slice_fusion.29
  61.8 0.7 constant_dynamic-update-slice_fusion.28
  62.5 0.7 constant_dynamic-update-slice_fusion.27
  63.1 4.4 %copy.491 = bf16[3456,384]{1,0:T(8,128)(2,1)} copy(bf16[3456,384]{0,1:T(8,128)(2,1)} %bitcast.69) | data formatting | bytes 5308416 | tf_op jit(solution)/shard_map/dot_general | solution.py:93
  67.6 4.3 %reshape.302 = bf16[4,4,2,2,54,384]{5,4,3,2,1,0:T(8,128)(2,1)} reshape(bf16[3456,384]{1,0:T(8,128)(2,1)} %copy.491) | data formatting | bytes 5308416 | tf_op jit(solution)/shard_map/reshape.37
  71.8 1.1 convolution_bitcast_fusion.1
  73.0 0.7 copy-done
  73.6 1.1 convolution_bitcast_fusion
  75.1 2.3 copy.494
  77.3 10.0 %all_to_all.15 = f32[2,2,4,4,2,54,128]{6,3,5,4,2,1,0:T(4,128)S(1)} all-to-all(f32[2,2,4,4,2,54,128]{6,3,5,4,2,1,0:T(4,128)S(1)} %copy.494), channel_id=1, replica_groups=mesh['z_hi'=4,'z_lo'=4,'x_lo'=2,'core'=2,'y'=4,'x_hi'=2] {'core'}, dimensions={0} | all-to-all | bytes 7077888 | tf_op jit(solution)/shard_map/all_to_all | solution.py:145
  87.3 2.9 %reduce_sum.27 = f32[2,4,4,2,54,128]{5,2,4,3,1,0:T(4,128)} reduce(f32[2,2,4,4,2,54,128]{6,3,5,4,2,1,0:T(4,128)S(1)} %all_to_all.15, f32[]{:T(128)} %constant.8.clone.1), dimensions={0}, to_apply=%region_0.1 | reduce | flops 442368 | bytes 5308420 | tf_op jit(solution)/shard_map/reduce_sum | solution.py:146
  90.3 2.2 copy.496
  92.4 1.1 copy.497
  93.6 47.2 %all_to_all.16 = f32[8,4,2,54,128]{4,1,3,2,0:T(4,128)S(1)} all-to-all(f32[8,4,2,54,128]{4,1,3,2,0:T(4,128)S(1)} %copy.497), channel_id=1, replica_groups=mesh['z_hi'=4,'z_lo'=4,'x_lo'=2,'core'=2,'y'=4,'x_hi'=2] {'x_lo','z_lo'}, dimensions={0} | all-to-all | bytes 3538944 | tf_op jit(solution)/shard_map/all_to_all | solution.py:145
  141.4 0.7 reshape.314
  142.1 35.6 %all_to_all.17 = f32[32,1,1728]{2,1,0:T(1,128)S(1)} all-to-all(f32[32,1,1728]{2,1,0:T(1,128)S(1)} %reshape.314), channel_id=1, replica_groups=mesh['z_hi'=4,'z_lo'=4,'x_lo'=2,'core'=2,'y'=4,'x_hi'=2] {'z_hi','y','x_..., dimensions={0} | all-to-all | bytes 442368 | tf_op jit(solution)/shard_map/all_to_all | solution.py:145
  178.2 1.2 reduce
  179.4 0.7 reshape.315
  180.3 0.6 fusion.41
  180.9 24.5 %all-gather = bf16[16,54,16]{1,2,0:T(8,128)(2,1)S(1)} all-gather(bf16[2,54,16]{1,2,0:T(8,128)(2,1)S(1)} %get-tuple-element.5), channel_id=2, replica_groups=mesh['z_hi'=4,'z_lo'=4,'x_lo'=2,'core'=2,'y'=4,'x_hi'=2] {'x_lo','z_lo'}, dimensions={0}, use_global_device_ids=true | all-gather | bytes 31104 | tf_op jit(solution)/shard_map/all_gather | solution.py:168
  205.4 31.8 %all-gather.1 = bf16[64,2,54,16]{2,3,1,0:T(8,128)(2,1)S(1)} all-gather(bf16[8,2,54,16]{2,3,1,0:T(8,128)(2,1)S(1)} %bitcast.215), channel_id=3, replica_groups=mesh['z_hi'=4,'z_lo'=4,'x_lo'=2,'core'=2,'y'=4,'x_hi'=2] {'z_hi','core'}, dimensions={0}, use_global_device_ids=true | all-gather | bytes 248832 | tf_op jit(solution)/shard_map/all_gather | solution.py:169
  237.2 0.5 copy.500
  237.8 1.4 reshape.307
  239.1 0.6 multiply_add_fusion
  (136 shorter events, 6.9 us)
Async XLA Ops:
  0.6 10.5 %copy-start.6 = (s32[1,8,12,4]{2,3,1,0:T(4,128)S(1)}, s32[1,8,12,4]{2,3,1,0:T(4,128)}, u32[]{:S(2)}) copy-start(s32[1,8,12,4]{2,3,1,0:T(4,128)} %param.9) | copy-start | bytes 4612
  1.6 10.0 %collective-permute-start = (bf16[8,12,1,128]{3,1,2,0:T(8,128)(2,1)S(1)}, bf16[8,12,1,128]{3,1,2,0:T(8,128)(2,1)S(1)}, u32[]{:S(2)}, u32[]{:S(2)}) collective-permute-start(bf16[8,12,1,128]{3,1,2,0:T(8,128)(2,1)S(1)} %get-tuple-element.63), channel_id=1, source_target_pairs={{0,1},{1,2},{2,3},{3,4},{4,5},{5,6},{6,7},{8,9},{9,10},{10,11},{11... | collective-permute-start | bytes 73736 | tf_op jit(solution)/shard_map/ppermute | solution.py:27
  7.1 6.2 %collective-permute-start.1 = (bf16[8,12,1,128]{3,1,2,0:T(8,128)(2,1)S(1)}, bf16[8,12,1,128]{3,1,2,0:T(8,128)(2,1)S(1)}, u32[]{:S(2)}, u32[]{:S(2)}) collective-permute-start(bf16[8,12,1,128]{3,1,2,0:T(8,128)(2,1)S(1)} %get-tuple-element.64), channel_id=1, source_target_pairs={{1,0},{2,1},{3,2},{4,3},{5,4},{6,5},{7,6},{9,8},{10,9},{11,10},{12... | collective-permute-start | bytes 73736 | tf_op jit(solution)/shard_map/ppermute | solution.py:29
  14.4 1.2 copy-start.2
  17.8 5.9 %copy-start.3 = (bf16[1,8,12,4,128]{4,3,2,1,0:T(4,128)(2,1)S(1)}, bf16[1,8,12,4,128]{4,3,2,1,0:T(4,128)(2,1)}, u32[]{:S(2)}) copy-start(bf16[1,8,12,4,128]{4,3,2,1,0:T(4,128)(2,1)} %param.8) | copy-start | bytes 294916
  18.0 11.8 %collective-permute-start.2 = (bf16[8,12,1,128]{3,0,2,1:T(8,128)(2,1)S(1)}, bf16[8,12,1,128]{3,0,2,1:T(8,128)(2,1)S(1)}, u32[]{:S(2)}, u32[]{:S(2)}) collective-permute-start(bf16[8,12,1,128]{3,0,2,1:T(8,128)(2,1)S(1)} %get-tuple-element.69), channel_id=1, source_target_pairs={{0,1},{1,2},{2,3},{3,4},{4,5},{5,6},{6,7},{8,9},{9,10},{10,11},{11... | collective-permute-start | bytes 73736 | tf_op jit(solution)/shard_map/ppermute | solution.py:27
  22.0 7.8 %collective-permute-start.3 = (bf16[8,12,1,128]{3,0,2,1:T(8,128)(2,1)S(1)}, bf16[8,12,1,128]{3,0,2,1:T(8,128)(2,1)S(1)}, u32[]{:S(2)}, u32[]{:S(2)}) collective-permute-start(bf16[8,12,1,128]{3,0,2,1:T(8,128)(2,1)S(1)} %get-tuple-element.70), channel_id=1, source_target_pairs={{1,0},{2,1},{3,2},{4,3},{5,4},{6,5},{7,6},{9,8},{10,9},{11,10},{12... | collective-permute-start | bytes 73736 | tf_op jit(solution)/shard_map/ppermute | solution.py:29
  30.0 1.2 copy-start.1
  30.6 3.0 %copy-start.4 = (bf16[1,8,12,4,128]{4,3,2,1,0:T(4,128)(2,1)S(1)}, bf16[1,8,12,4,128]{4,3,2,1,0:T(4,128)(2,1)}, u32[]{:S(2)}) copy-start(bf16[1,8,12,4,128]{4,3,2,1,0:T(4,128)(2,1)} %param.10) | copy-start | bytes 294916
  33.9 16.9 %collective-permute-start.4 = (bf16[8,12,1,128]{3,0,2,1:T(8,128)(2,1)S(1)}, bf16[8,12,1,128]{3,0,2,1:T(8,128)(2,1)S(1)}, u32[]{:S(2)}, u32[]{:S(2)}) collective-permute-start(bf16[8,12,1,128]{3,0,2,1:T(8,128)(2,1)S(1)} %get-tuple-element.65), channel_id=1, source_target_pairs={{0,1},{1,2},{2,3},{3,4},{4,5},{5,6},{6,7},{8,9},{9,10},{10,11},{11... | collective-permute-start | bytes 73736 | tf_op jit(solution)/shard_map/ppermute | solution.py:27
  39.4 11.4 %collective-permute-start.5 = (bf16[8,12,1,128]{3,0,2,1:T(8,128)(2,1)S(1)}, bf16[8,12,1,128]{3,0,2,1:T(8,128)(2,1)S(1)}, u32[]{:S(2)}, u32[]{:S(2)}) collective-permute-start(bf16[8,12,1,128]{3,0,2,1:T(8,128)(2,1)S(1)} %get-tuple-element.66), channel_id=1, source_target_pairs={{1,0},{2,1},{3,2},{4,3},{5,4},{6,5},{7,6},{9,8},{10,9},{11,10},{12... | collective-permute-start | bytes 73736 | tf_op jit(solution)/shard_map/ppermute | solution.py:29
  71.8 1.8 copy-start
  141.1 39.1 %copy-start.7 = (f32[2,54,16]{1,2,0:T(8,128)S(1)}, f32[2,54,16]{1,2,0:T(8,128)}, u32[]{:S(2)}) copy-start(f32[2,54,16]{1,2,0:T(8,128)} %param.12) | copy-start | bytes 20740
  141.1 39.1 %copy-start.8 = (f32[2,54,16]{1,2,0:T(8,128)S(1)}, f32[2,54,16]{1,2,0:T(8,128)}, u32[]{:S(2)}) copy-start(f32[2,54,16]{1,2,0:T(8,128)} %param.13) | copy-start | bytes 20740
  141.1 39.1 %copy-start.9 = (f32[2,54,16]{1,2,0:T(8,128)S(1)}, f32[2,54,16]{1,2,0:T(8,128)}, u32[]{:S(2)}) copy-start(f32[2,54,16]{1,2,0:T(8,128)} %param.14) | copy-start | bytes 20740
  141.4 97.7 %copy-start.10 = (f32[2,54,16]{1,2,0:T(8,128)S(1)}, f32[2,54,16]{1,2,0:T(8,128)}, u32[]{:S(2)}) copy-start(f32[2,54,16]{1,2,0:T(8,128)} %param.15) | copy-start | bytes 20740
  180.9 58.9 %copy-start.5 = (f32[2,54,16]{1,2,0:T(8,128)}, f32[2,54,16]{1,2,0:T(8,128)S(1)}, u32[]{:S(2)}) copy-start(f32[2,54,16]{1,2,0:T(8,128)S(1)} %get-tuple-element.6) | copy-start | bytes 20740
